TPU v7x, 512 devices: a whole 4x4x16 slice. The times are simulated.
512 devices in a mesh: rc: 64 (over x, y, z_hi), sys: 8 (over z_lo, core).
Axes of the slice: x: 4, y: 4, z: 16 (z_hi: 4, z_lo: 4; z = z_hi * 4 + z_lo), core: 2. Of those that a mesh axis runs over, the one named last changes fastest.
Arguments:
- density: bfloat16 [2, 64, 1600, 512], P(None, 'sys', 'rc'), may hold values from -6 to 6
- system_real: bfloat16 [64, 64], replicated, may hold values from -0.75 to 0.75
- system_imag: bfloat16 [64, 64], replicated, may hold values from -0.75 to 0.75
- left_ham: bfloat16 [40, 40], replicated, may hold values from -1 to 1
- left_coupling: bfloat16 [40, 40], replicated, may hold values from -1 to 1
- right_ham: bfloat16 [40, 40], replicated, may hold values from -1 to 1
- right_coupling: bfloat16 [40, 40], replicated, may hold values from -1 to 1
- left_strength: float32 [64], replicated, may hold values from -1.5 to 1.5
- right_strength: float32 [64], replicated, may hold values from -1.5 to 1.5
- left_damping: float32 [40], replicated, may hold values from 0.1 to 2
- right_damping: float32 [40], replicated, may hold values from 0.1 to 2
- energies: float32 [512], replicated, may hold values from -3 to 3
Outputs:
- derivative: bfloat16 [2, 64, 1600, 512], P(None, 'sys', 'rc')
All inputs are finite; a program needn't handle non-finite values.
Results may differ from a plain program's by a relative error of at most 0.0047.
Values may be sent and summed in bfloat16 or wider, within the bound.
No kernel may reach another device: no remote copies, remote signals or barrier semaphores. Data moves between devices by JAX's collectives and lax.ppermute only.
A program may use at most 64 MiB of HBM per device.

v0:
```python
import math

import jax
import jax.numpy as jnp
from jax import lax
from jax.sharding import PartitionSpec as P


def symmetric(matrix, factor):
    widened = matrix.astype(jnp.float32)
    return ((widened + factor * widened.T) * 0.5).astype(jnp.bfloat16)


def ladder_local(regrouped, left_ops, right_ops, left_gain, right_gain, levels):
    item_count, group_count, all_pairs, column_count = regrouped.shape
    widened = regrouped.reshape(item_count, group_count, levels, levels * column_count)
    left_all = jnp.einsum("xa,ksam->ksxm", left_ops, widened, preferred_element_type=jnp.float32)
    left_term = left_all[:, :, :levels] + left_gain[None, :, None, None] * left_all[:, :, levels:]
    deepened = regrouped.reshape(item_count, group_count, levels, levels, column_count)
    right_all = jnp.einsum(
        "yb,ksabc->ksayc", right_ops, deepened, preferred_element_type=jnp.float32
    )
    right_term = (
        right_all[:, :, :, :levels]
        + right_gain[None, :, None, None, None] * right_all[:, :, :, levels:]
    )
    summed = left_term.reshape(
        item_count, group_count, all_pairs, column_count
    ) + right_term.reshape(item_count, group_count, all_pairs, column_count)
    return summed.astype(jnp.bfloat16)


def shards(
    density,
    system_real,
    system_imag,
    left_ham,
    left_coupling,
    right_ham,
    right_coupling,
    left_strength,
    right_strength,
    left_damping,
    right_damping,
    energies,
):
    herm_real = symmetric(system_real, 1.0)
    herm_imag = symmetric(system_imag, -1.0)
    levels = left_ham.shape[0]
    left_ops = jnp.concatenate([symmetric(left_ham, 1.0), symmetric(left_coupling, 1.0)], axis=0)
    right_ops = jnp.concatenate([symmetric(right_ham, 1.0), symmetric(right_coupling, 1.0)], axis=0)
    state_count = density.shape[1]
    pair_count = density.shape[2]
    column_total = density.shape[3]
    first_state = lax.axis_index("sys") * state_count
    left_gain = lax.dynamic_slice_in_dim(left_strength, first_state, state_count)
    right_gain = lax.dynamic_slice_in_dim(right_strength, first_state, state_count)
    regrouped = lax.all_to_all(density, "sys", split_axis=3, concat_axis=1, tiled=True)
    flattened = regrouped.reshape(2, regrouped.shape[1], -1)
    real_part = jnp.dot(herm_real, flattened[0], preferred_element_type=jnp.float32) - jnp.dot(
        herm_imag, flattened[1], preferred_element_type=jnp.float32
    )
    imag_part = jnp.dot(herm_real, flattened[1], preferred_element_type=jnp.float32) + jnp.dot(
        herm_imag, flattened[0], preferred_element_type=jnp.float32
    )
    product = jnp.stack([real_part, imag_part]).astype(jnp.bfloat16).reshape(regrouped.shape)
    system_rows = lax.all_to_all(product, "sys", split_axis=1, concat_axis=3, tiled=True)
    rc_count = lax.axis_size("rc")
    col_groups = rc_count // math.gcd(state_count, rc_count)
    per_device = state_count * col_groups // rc_count
    group_width = column_total // col_groups
    combined = jnp.moveaxis(
        density.reshape(2, state_count, pair_count, col_groups, group_width), 3, 2
    )
    combined = combined.reshape(2, state_count * col_groups, pair_count, group_width)
    combo_index = lax.axis_index("rc") * per_device + jnp.arange(per_device, dtype=jnp.int32)
    state_pick = (
        (combo_index // col_groups)[:, None] == jnp.arange(state_count, dtype=jnp.int32)[None, :]
    ).astype(jnp.float32)
    combo_left = jnp.sum(state_pick * left_gain[None, :], axis=1)
    combo_right = jnp.sum(state_pick * right_gain[None, :], axis=1)
    summed = ladder_local(
        lax.all_to_all(combined, "rc", split_axis=1, concat_axis=2, tiled=True),
        left_ops,
        right_ops,
        combo_left,
        combo_right,
        levels,
    )
    returned = lax.all_to_all(summed, "rc", split_axis=2, concat_axis=1, tiled=True)
    returned = returned.reshape(2, state_count, col_groups, pair_count, group_width)
    ladder_rows = jnp.moveaxis(returned, 2, 3).reshape(2, state_count, pair_count, column_total)
    pair_index = lax.axis_index("rc") * pair_count + jnp.arange(pair_count, dtype=jnp.int32)
    level_index = jnp.arange(levels, dtype=jnp.int32)
    left_pick = (pair_index[:, None] // levels == level_index[None, :]).astype(jnp.float32)
    right_pick = (pair_index[:, None] % levels == level_index[None, :]).astype(jnp.float32)
    damping = 0.5 * (
        jnp.sum(left_pick * left_damping[None, :], axis=1)
        + jnp.sum(right_pick * right_damping[None, :], axis=1)
    )
    system_term = system_rows.astype(jnp.float32)
    ladder = ladder_rows.astype(jnp.float32)
    real_in = density[0].astype(jnp.float32)
    imag_in = density[1].astype(jnp.float32)
    energy_grid = energies[None, None, :]
    damp_grid = damping[None, :, None]
    new_real = system_term[1] + ladder[1] - energy_grid * imag_in - damp_grid * real_in
    new_imag = -system_term[0] - ladder[0] + energy_grid * real_in - damp_grid * imag_in
    return jnp.stack([new_real, new_imag]).astype(jnp.bfloat16)


def solution(mesh):
    placed = (P(None, "sys", "rc", None), P(), P(), P(), P(), P(), P(), P(), P(), P(), P(), P())
    return jax.shard_map(
        shards, mesh=mesh, in_specs=placed, out_specs=P(None, "sys", "rc", None), check_vma=False
    )
```

profile of v0, /device:TPU:64, one launch (start us, length us, event | category | flops | bytes accessed | tf_op | source)
XLA Modules:
  0.0 143.1 jit_solution(4332645924934127835)
XLA Ops:
  0.0 3.1 %copy.110 = bf16[2,8,25,512]{2,1,0,3:T(8,128)(2,1)S(1)} copy(bf16[2,8,25,512]{3,1,2,0:T(8,128)(2,1)} %param.12) | data formatting | bytes 819200 | tf_op args[0]
  3.1 4.3 %reshape.162 = bf16[8,2,12800]{2,1,0:T(2,128)(2,1)} reshape(bf16[512,2,8,25]{3,2,1,0:T(8,128)(2,1)S(1)} %bitcast.115) | data formatting | bytes 819200
  7.4 8.4 %all-to-all-start = ((bf16[8,2,12800]{2,1,0:T(2,128)(2,1)}), bf16[8,2,12800]{2,1,0:T(2,128)(2,1)S(1)}, u32[]{:S(2)}, u32[]{:S(2)}) async-start(bf16[8,2,12800]{2,1,0:T(2,128)(2,1)} %reshape.162), calls=%async_computation | async-start | bytes 819200 | tf_op jit(solution)/shard_map/all_to_all | solution.py:58
  17.1 1.3 reshape.158
  18.6 6.8 %all-to-all-done = bf16[8,2,12800]{2,1,0:T(2,128)(2,1)S(1)} async-done(((bf16[8,2,12800]{2,1,0:T(2,128)(2,1)}), bf16[8,2,12800]{2,1,0:T(2,128)(2,1)S(1)}, u32[]{:S(2)}, u32[]{:S(2)}) %all-to-all-start) | async-done | bytes 409632 | tf_op jit(solution)/shard_map/all_to_all | solution.py:58
  25.4 16.0 %all-to-all-start.2 = ((bf16[64,2,1600]{2,1,0:T(2,128)(2,1)}), bf16[64,2,1600]{2,1,0:T(2,128)(2,1)}, u32[]{:S(2)}, u32[]{:S(2)}) async-start(bf16[64,2,1600]{2,1,0:T(2,128)(2,1)} %reshape.158), calls=%async_computation.2 | async-start | bytes 851968 | tf_op jit(solution)/shard_map/all_to_all | solution.py:83
  42.7 5.3 %reshape.163 = bf16[512,2,8,25]{3,2,1,0:T(8,128)(2,1)S(1)} reshape(bf16[8,2,12800]{2,1,0:T(2,128)(2,1)S(1)} %all-to-all-done) | data formatting | bytes 819200
  48.0 1.7 %copy.111 = bf16[2,8,25,8,64]{4,2,1,3,0:T(8,128)(2,1)S(1)} copy(bf16[2,8,25,8,64]{2,1,0,4,3:T(8,128)(2,1)S(1)} %bitcast.114) | data formatting | bytes 819200 | tf_op jit(solution)/shard_map/all_to_all | solution.py:58
  52.5 0.9 copy.136
  53.3 1.3 reshape.164
  54.6 17.5 %all-to-all-done.2 = bf16[64,2,1600]{2,1,0:T(2,128)(2,1)} async-done(((bf16[64,2,1600]{2,1,0:T(2,128)(2,1)}), bf16[64,2,1600]{2,1,0:T(2,128)(2,1)}, u32[]{:S(2)}, u32[]{:S(2)}) %all-to-all-start.2) | async-done | bytes 409632 | tf_op jit(solution)/shard_map/all_to_all | solution.py:83
  72.1 6.6 %all-to-all-start.1 = ((bf16[8,2,12800]{2,1,0:T(2,128)(2,1)}), bf16[8,2,12800]{2,1,0:T(2,128)(2,1)}, u32[]{:S(2)}, u32[]{:S(2)}) async-start(bf16[8,2,12800]{2,1,0:T(2,128)(2,1)} %reshape.164), calls=%async_computation.1 | async-start | bytes 819200 | tf_op jit(solution)/shard_map/all_to_all | solution.py:67
  78.7 2.6 %reshape.159 = bf16[64,25,2,64]{3,2,1,0:T(2,128)(2,1)S(1)} reshape(bf16[64,2,1600]{2,1,0:T(2,128)(2,1)} %all-to-all-done.2) | data formatting | bytes 819200
  81.3 1.1 copy.118
  83.1 1.4 fusion
  84.5 1.9 %copy.122 = f32[2,1,40,40,64]{4,3,2,0,1:T(8,128)} copy(f32[2,1,40,40,64]{3,4,2,0,1:T(8,128)S(1)} %fusion) | data formatting | bytes 1638400 | tf_op jit(solution)/shard_map/add | solution.py:24
  86.4 1.9 %reshape.150 = bf16[2,40,2560]{2,1,0:T(8,128)(2,1)S(1)} reshape(bf16[2,64,25,64]{3,2,1,0:T(8,128)(2,1)} %copy.118) | data formatting | bytes 819200 | tf_op jit(solution)/shard_map/reshape.8
  88.8 1.7 %fusion.4 = f32[2,1,40,2560]{3,2,0,1:T(8,128)} fusion(f32[2,1,80,2560]{3,2,0,1:T(8,128)S(1)} %convolution_bitcast_fusion, f32[]{:T(128)} %get-tuple-element.13), kind=kLoop, calls=%fused_computation.17 | loop fusion | flops 409600 | bytes 2457604 | tf_op jit(solution)/shard_map/add | solution.py:18
  90.4 1.7 %reshape.151 = f32[2,1,1600,64]{3,2,0,1:T(8,128)S(1)} reshape(f32[2,1,40,2560]{3,2,0,1:T(8,128)} %fusion.4) | data formatting | bytes 1638400 | tf_op jit(solution)/shard_map/reshape | solution.py:27
  92.3 6.8 %copy.135 = bf16[2,1,1600,64]{3,0,1,2:T(2,128)(2,1)S(1)} copy(bf16[2,1,1600,64]{3,2,0,1:T(8,128)(2,1)S(1)} %fusion.3) | data formatting | bytes 819200 | tf_op jit(solution)/shard_map/convert_element_type | solution.py:30
  99.1 1.3 reshape.160
  100.5 5.9 %all-to-all-start.3 = ((bf16[64,2,1600]{2,1,0:T(2,128)(2,1)}), bf16[64,2,1600]{2,1,0:T(2,128)(2,1)S(1)}, u32[]{:S(2)}, u32[]{:S(2)}) async-start(bf16[64,2,1600]{2,1,0:T(2,128)(2,1)} %reshape.160), calls=%async_computation.3 | async-start | bytes 851968 | tf_op jit(solution)/shard_map/all_to_all | solution.py:90
  106.8 2.6 %reshape.165 = bf16[64,25,2,64]{3,2,1,0:T(2,128)(2,1)S(1)} reshape(bf16[8,2,12800]{2,1,0:T(2,128)(2,1)} %all-to-all-done.1) | data formatting | bytes 819200
  109.6 29.9 %all-to-all-done.3 = bf16[64,2,1600]{2,1,0:T(2,128)(2,1)S(1)} async-done(((bf16[64,2,1600]{2,1,0:T(2,128)(2,1)}), bf16[64,2,1600]{2,1,0:T(2,128)(2,1)S(1)}, u32[]{:S(2)}, u32[]{:S(2)}) %all-to-all-start.3) | async-done | bytes 409632 | tf_op jit(solution)/shard_map/all_to_all | solution.py:90
  (70 shorter events, 10.8 us)
Async XLA Ops:
  3.1 12.7 %copy-start.1 = (bf16[2,8,25,512]{3,1,2,0:T(8,128)(2,1)S(1)}, bf16[2,8,25,512]{3,1,2,0:T(8,128)(2,1)}, u32[]{:S(2)}) copy-start(bf16[2,8,25,512]{3,1,2,0:T(8,128)(2,1)} %param.12) | copy-start | bytes 1228804
  7.4 18.0 %all-to-all-start = ((bf16[8,2,12800]{2,1,0:T(2,128)(2,1)}), bf16[8,2,12800]{2,1,0:T(2,128)(2,1)S(1)}, u32[]{:S(2)}, u32[]{:S(2)}) async-start(bf16[8,2,12800]{2,1,0:T(2,128)(2,1)} %reshape.162), calls=%async_computation | async-start | bytes 819200 | tf_op jit(solution)/shard_map/all_to_all | solution.py:58
  16.2 2.3 %copy-start.5 = (bf16[40,40]{1,0:T(8,128)(2,1)S(1)}, bf16[40,40]{1,0:T(8,128)(2,1)}, u32[]{:S(2)}) copy-start(bf16[40,40]{1,0:T(8,128)(2,1)} %param.17) | copy-start | bytes 9604
  16.2 2.3 %copy-start.4 = (bf16[40,40]{1,0:T(8,128)(2,1)S(1)}, bf16[40,40]{1,0:T(8,128)(2,1)}, u32[]{:S(2)}) copy-start(bf16[40,40]{1,0:T(8,128)(2,1)} %param.18) | copy-start | bytes 9604
  16.2 25.3 %copy-start.7 = (bf16[40,40]{1,0:T(8,128)(2,1)S(1)}, bf16[40,40]{1,0:T(8,128)(2,1)}, u32[]{:S(2)}) copy-start(bf16[40,40]{1,0:T(8,128)(2,1)} %param.15) | copy-start | bytes 9604
  16.2 25.4 %copy-start.6 = (bf16[40,40]{1,0:T(8,128)(2,1)S(1)}, bf16[40,40]{1,0:T(8,128)(2,1)}, u32[]{:S(2)}) copy-start(bf16[40,40]{1,0:T(8,128)(2,1)} %param.16) | copy-start | bytes 9604
  16.2 25.4 %copy-start.8 = (bf16[64,64]{1,0:T(8,128)(2,1)S(1)}, bf16[64,64]{1,0:T(8,128)(2,1)}, u32[]{:S(2)}) copy-start(bf16[64,64]{1,0:T(8,128)(2,1)} %param.13) | copy-start | bytes 24580
  16.2 25.6 %copy-start.3 = (bf16[64,64]{1,0:T(8,128)(2,1)S(1)}, bf16[64,64]{1,0:T(8,128)(2,1)}, u32[]{:S(2)}) copy-start(bf16[64,64]{1,0:T(8,128)(2,1)} %param.14) | copy-start | bytes 24580
  17.1 24.8 %copy-start.10 = (f32[64]{0:T(128)S(1)}, f32[64]{0:T(128)}, u32[]{:S(2)}) copy-start(f32[64]{0:T(128)} %param.19) | copy-start | bytes 772
  17.1 24.8 %copy-start.11 = (f32[64]{0:T(128)S(1)}, f32[64]{0:T(128)}, u32[]{:S(2)}) copy-start(f32[64]{0:T(128)} %param.20) | copy-start | bytes 772
  25.4 46.7 %all-to-all-start.2 = ((bf16[64,2,1600]{2,1,0:T(2,128)(2,1)}), bf16[64,2,1600]{2,1,0:T(2,128)(2,1)}, u32[]{:S(2)}, u32[]{:S(2)}) async-start(bf16[64,2,1600]{2,1,0:T(2,128)(2,1)} %reshape.158), calls=%async_computation.2 | async-start | bytes 851968 | tf_op jit(solution)/shard_map/all_to_all | solution.py:83
  72.1 28.4 %all-to-all-start.1 = ((bf16[8,2,12800]{2,1,0:T(2,128)(2,1)}), bf16[8,2,12800]{2,1,0:T(2,128)(2,1)}, u32[]{:S(2)}, u32[]{:S(2)}) async-start(bf16[8,2,12800]{2,1,0:T(2,128)(2,1)} %reshape.164), calls=%async_computation.1 | async-start | bytes 819200 | tf_op jit(solution)/shard_map/all_to_all | solution.py:67
  90.4 1.7 %copy-start = (f32[2,1,40,40,64]{4,3,2,0,1:T(8,128)S(1)}, f32[2,1,40,40,64]{4,3,2,0,1:T(8,128)}, u32[]{:S(2)}) copy-start(f32[2,1,40,40,64]{4,3,2,0,1:T(8,128)} %copy.122) | copy-start | bytes 2457604
  92.3 14.1 %copy-start.13 = (f32[40]{0:T(128)S(1)}, f32[40]{0:T(128)}, u32[]{:S(2)}) copy-start(f32[40]{0:T(128)} %param.22) | copy-start | bytes 484
  92.3 14.3 %copy-start.14 = (f32[40]{0:T(128)S(1)}, f32[40]{0:T(128)}, u32[]{:S(2)}) copy-start(f32[40]{0:T(128)} %param.21) | copy-start | bytes 484
  100.5 39.0 %all-to-all-start.3 = ((bf16[64,2,1600]{2,1,0:T(2,128)(2,1)}), bf16[64,2,1600]{2,1,0:T(2,128)(2,1)S(1)}, u32[]{:S(2)}, u32[]{:S(2)}) async-start(bf16[64,2,1600]{2,1,0:T(2,128)(2,1)} %reshape.160), calls=%async_computation.3 | async-start | bytes 851968 | tf_op jit(solution)/shard_map/all_to_all | solution.py:90
  141.1 1.0 copy-start.2
  141.1 1.0 copy-start.9
  142.3 0.8 copy-start.12
where the time goes:
time: 144 us; the launch traced here: 143 us
  waiting for transfers between devices  54.1 us (38%)
  local copies, waits for them, and re-layouts  44.3 us (31%)
  starting transfers between devices  37 us (26%)
  other arithmetic  5.33 us (4%)
  matrix products  1.9 us (1%)
    all_to_all x1, waiting for transfers between devices, shards(): lax.all_to_all(summed, 'rc', split_axis=2, concat_axis=1, tiled=True)  29.9 us
    unnamed x40, local copies, waits for them, and re-layouts  24 us
    all_to_all x1, waiting for transfers between devices, shards(): lax.all_to_all(combined, 'rc', split_axis=1, concat_axis=2, tiled=True)  17.5 us
    all_to_all x1, starting transfers between devices, shards(): lax.all_to_all(combined, 'rc', split_axis=1, concat_axis=2, tiled=True)  16 us
    all_to_all x1, starting transfers between devices, shards(): lax.all_to_all(density, 'sys', split_axis=3, concat_axis=1, tiled=True)  8.41 us
    convert_element_type x1, local copies, waits for them, and re-layouts, ladder_local(): return summed.astype(jnp.bfloat16)  6.79 us
    all_to_all x1, waiting for transfers between devices, shards(): lax.all_to_all(density, 'sys', split_axis=3, concat_axis=1, tiled=True)  6.79 us
    all_to_all x1, starting transfers between devices, shards(): lax.all_to_all(product, 'sys', split_axis=1, concat_axis=3, tiled=True)  6.61 us
  transfers between devices with their start and end apart: 4, of which 3 were waited for; matrix products, arithmetic and copies ran while one was open for 28% of the time, Pallas kernels for 0%

commit v1 on v0

--- a/solution.py
+++ b/solution.py
@@ -55,16 +55,19 @@
     first_state = lax.axis_index("sys") * state_count
     left_gain = lax.dynamic_slice_in_dim(left_strength, first_state, state_count)
     right_gain = lax.dynamic_slice_in_dim(right_strength, first_state, state_count)
-    regrouped = lax.all_to_all(density, "sys", split_axis=3, concat_axis=1, tiled=True)
-    flattened = regrouped.reshape(2, regrouped.shape[1], -1)
-    real_part = jnp.dot(herm_real, flattened[0], preferred_element_type=jnp.float32) - jnp.dot(
-        herm_imag, flattened[1], preferred_element_type=jnp.float32
+    gathered = lax.all_gather(density, "sys", axis=1, tiled=True)
+    own_real = lax.dynamic_slice_in_dim(herm_real, first_state, state_count, axis=0)
+    own_imag = lax.dynamic_slice_in_dim(herm_imag, first_state, state_count, axis=0)
+    mixer = jnp.concatenate(
+        [
+            jnp.concatenate([own_real, -own_imag], axis=1),
+            jnp.concatenate([own_imag, own_real], axis=1),
+        ],
+        axis=0,
     )
-    imag_part = jnp.dot(herm_real, flattened[1], preferred_element_type=jnp.float32) + jnp.dot(
-        herm_imag, flattened[0], preferred_element_type=jnp.float32
-    )
-    product = jnp.stack([real_part, imag_part]).astype(jnp.bfloat16).reshape(regrouped.shape)
-    system_rows = lax.all_to_all(product, "sys", split_axis=1, concat_axis=3, tiled=True)
+    stacked = gathered.reshape(2 * gathered.shape[1], -1)
+    product = jnp.dot(mixer, stacked, preferred_element_type=jnp.float32)
+    system_rows = product.astype(jnp.bfloat16).reshape(density.shape)
     rc_count = lax.axis_size("rc")
     col_groups = rc_count // math.gcd(state_count, rc_count)
     per_device = state_count * col_groups // rc_count

time: 144 us -> 135 us (0.938)
  the two profiles are of different devices: /device:TPU:64 before, /device:TPU:32 now
where the time goes in v1:
time: 135 us
  waiting for transfers between devices  60.5 us (45%)
  local copies, waits for them, and re-layouts  27.4 us (20%)
  starting transfers between devices  25.1 us (19%)
  between operations  13.8 us (10%)
  other arithmetic  6.18 us (5%)
  matrix products  1.73 us (1%)
    all_to_all x1, waiting for transfers between devices, shards(): lax.all_to_all(combined, 'rc', split_axis=1, concat_axis=2, tiled=True)  30.8 us
    all_to_all x1, waiting for transfers between devices, shards(): lax.all_to_all(summed, 'rc', split_axis=2, concat_axis=1, tiled=True)  28.9 us
    all_to_all x1, starting transfers between devices, shards(): lax.all_to_all(combined, 'rc', split_axis=1, concat_axis=2, tiled=True)  20.3 us
    unnamed x33, local copies, waits for them, and re-layouts  7.65 us
    convert_element_type x1, local copies, waits for them, and re-layouts, ladder_local(): return summed.astype(jnp.bfloat16)  6.79 us
    all_to_all x1, starting transfers between devices, shards(): lax.all_to_all(summed, 'rc', split_axis=2, concat_axis=1, tiled=True)  4.81 us
    all_gather x1, local copies, waits for them, and re-layouts, shards(): gathered = lax.all_gather(density, 'sys', axis=1, tiled=True)  3.87 us
  transfers between devices with their start and end apart: 3, of which 2 were waited for; matrix products, arithmetic and copies ran while one was open for 17% of the time, Pallas kernels for 0%

profile of v1, /device:TPU:32, one launch (start us, length us, event | category | flops | bytes accessed | tf_op | source)
XLA Modules:
  0.0 134.7 jit_solution(4475032639783936195)
XLA Ops:
  6.6 1.6 %reshape.136 = bf16[2,8,25,8,64]{4,3,1,2,0:T(8,128)(2,1)S(1)} reshape(bf16[2,8,25,512]{3,1,2,0:T(8,128)(2,1)} %param.12) | data formatting | bytes 819200 | tf_op jit(solution)/shard_map/reshape | solution.py:76
  8.2 0.8 copy.71
  9.0 1.3 reshape.145
  10.3 20.3 %all-to-all-start = ((bf16[64,2,1600]{2,1,0:T(2,128)(2,1)}), bf16[64,2,1600]{2,1,0:T(2,128)(2,1)S(1)}, u32[]{:S(2)}, u32[]{:S(2)}) async-start(bf16[64,2,1600]{2,1,0:T(2,128)(2,1)} %reshape.145), calls=%async_computation | async-start | bytes 851968 | tf_op jit(solution)/shard_map/all_to_all | solution.py:86
  30.7 0.7 all-gather.2.cloned.1.call-update
  31.7 0.7 fusion.34
  32.5 30.8 %all-to-all-done = bf16[64,2,1600]{2,1,0:T(2,128)(2,1)S(1)} async-done(((bf16[64,2,1600]{2,1,0:T(2,128)(2,1)}), bf16[64,2,1600]{2,1,0:T(2,128)(2,1)S(1)}, u32[]{:S(2)}, u32[]{:S(2)}) %all-to-all-start) | async-done | bytes 409632 | tf_op jit(solution)/shard_map/all_to_all | solution.py:86
  63.3 0.7 reshape.146
  64.2 0.6 reshape.138
  65.3 0.6 fusion.3
  66.0 1.6 %reshape.139 = f32[2,1,1600,64]{3,2,0,1:T(8,128)} reshape(f32[2,1,40,2560]{3,2,0,1:T(8,128)S(1)} %fusion.3) | data formatting | bytes 1638400 | tf_op jit(solution)/shard_map/reshape | solution.py:27
  67.5 0.7 convolution_bitcast_fusion.1
  68.2 1.4 %fusion.1 = f32[2,1,40,40,64]{3,4,2,0,1:T(8,128)S(1)} fusion(f32[2,1,40,80,64]{3,4,2,0,1:T(8,128)S(1)} %convolution_bitcast_fusion.1, f32[]{:T(128)} %get-tuple-element.20), kind=kLoop, calls=%fused_computation.4 | loop fusion | flops 409600 | bytes 2457604 | tf_op jit(solution)/shard_map/add | solution.py:24
  69.6 1.9 %copy.76 = f32[2,1,40,40,64]{4,3,2,0,1:T(8,128)} copy(f32[2,1,40,40,64]{3,4,2,0,1:T(8,128)S(1)} %fusion.1) | data formatting | bytes 1638400 | tf_op jit(solution)/shard_map/add | solution.py:24
  71.5 2.1 %fusion.2 = bf16[2,1,1600,64]{3,2,0,1:T(8,128)(2,1)S(1)} fusion(f32[2,1,1600,64]{3,2,0,1:T(8,128)} %reshape.139, f32[2,1,40,40,64]{4,3,2,0,1:T(8,128)} %copy.76), kind=kLoop, calls=%fused_computation.8 | loop fusion | flops 409600 | bytes 2048000 | tf_op jit(solution)/shard_map/convert_element_type | solution.py:30
  73.7 6.8 %copy.86 = bf16[2,1,1600,64]{3,0,1,2:T(2,128)(2,1)S(1)} copy(bf16[2,1,1600,64]{3,2,0,1:T(8,128)(2,1)S(1)} %fusion.2) | data formatting | bytes 819200 | tf_op jit(solution)/shard_map/convert_element_type | solution.py:30
  80.5 1.3 reshape.147
  81.8 4.8 %all-to-all-start.1 = ((bf16[64,2,1600]{2,1,0:T(2,128)(2,1)}), bf16[64,2,1600]{2,1,0:T(2,128)(2,1)S(1)}, u32[]{:S(2)}, u32[]{:S(2)}) async-start(bf16[64,2,1600]{2,1,0:T(2,128)(2,1)} %reshape.147), calls=%async_computation.1 | async-start | bytes 851968 | tf_op jit(solution)/shard_map/all_to_all | solution.py:93
  87.4 28.9 %all-to-all-done.1 = bf16[64,2,1600]{2,1,0:T(2,128)(2,1)S(1)} async-done(((bf16[64,2,1600]{2,1,0:T(2,128)(2,1)}), bf16[64,2,1600]{2,1,0:T(2,128)(2,1)S(1)}, u32[]{:S(2)}, u32[]{:S(2)}) %all-to-all-start.1) | async-done | bytes 409632 | tf_op jit(solution)/shard_map/all_to_all | solution.py:93
  116.4 0.7 reshape.148
  117.7 1.3 fusion.42
  119.6 3.9 %copy.68 = bf16[2,64,25,512]{3,2,1,0:T(8,128)(2,1)S(1)} copy(bf16[2,64,25,512]{3,1,2,0:T(8,128)(2,1)} %all-gather.2.cloned.1.call-done) | data formatting | bytes 6553600 | tf_op jit(solution)/shard_map/all_gather | solution.py:58
  123.5 2.3 %copy.82 = bf16[16,8,25,512]{3,1,2,0:T(8,128)(2,1)S(1)} copy(bf16[16,8,25,512]{3,2,1,0:T(8,128)(2,1)S(1)} %bitcast.90) | data formatting | bytes 6553600
  127.1 0.7 copy-done.10
  (57 shorter events, 4.2 us)
Async XLA Ops:
  6.5 24.8 %copy-start.2 = (bf16[40,40]{1,0:T(8,128)(2,1)S(1)}, bf16[40,40]{1,0:T(8,128)(2,1)}, u32[]{:S(2)}) copy-start(bf16[40,40]{1,0:T(8,128)(2,1)} %param.16) | copy-start | bytes 9604
  6.5 24.9 %copy-start.3 = (bf16[40,40]{1,0:T(8,128)(2,1)S(1)}, bf16[40,40]{1,0:T(8,128)(2,1)}, u32[]{:S(2)}) copy-start(bf16[40,40]{1,0:T(8,128)(2,1)} %param.15) | copy-start | bytes 9604
  6.5 25.0 %copy-start.4 = (bf16[40,40]{1,0:T(8,128)(2,1)S(1)}, bf16[40,40]{1,0:T(8,128)(2,1)}, u32[]{:S(2)}) copy-start(bf16[40,40]{1,0:T(8,128)(2,1)} %param.18) | copy-start | bytes 9604
  6.5 25.1 %copy-start.5 = (bf16[40,40]{1,0:T(8,128)(2,1)S(1)}, bf16[40,40]{1,0:T(8,128)(2,1)}, u32[]{:S(2)}) copy-start(bf16[40,40]{1,0:T(8,128)(2,1)} %param.17) | copy-start | bytes 9604
  6.5 25.2 %copy-start.8 = (f32[64]{0:T(128)S(1)}, f32[64]{0:T(128)}, u32[]{:S(2)}) copy-start(f32[64]{0:T(128)} %param.19) | copy-start | bytes 772
  6.5 25.2 %copy-start.9 = (f32[64]{0:T(128)S(1)}, f32[64]{0:T(128)}, u32[]{:S(2)}) copy-start(f32[64]{0:T(128)} %param.20) | copy-start | bytes 772
  10.3 53.0 %all-to-all-start = ((bf16[64,2,1600]{2,1,0:T(2,128)(2,1)}), bf16[64,2,1600]{2,1,0:T(2,128)(2,1)S(1)}, u32[]{:S(2)}, u32[]{:S(2)}) async-start(bf16[64,2,1600]{2,1,0:T(2,128)(2,1)} %reshape.145), calls=%async_computation | async-start | bytes 851968 | tf_op jit(solution)/shard_map/all_to_all | solution.py:86
  30.6 89.0 %all-gather.2.cloned.1.call-start = ((), (), s32[]{:S(2)}) async-start(), calls=%async_computation.2 | async-start | bytes 3686400 | tf_op jit(solution)/shard_map/all_gather | solution.py:58
  73.6 13.0 %copy-start.1 = (bf16[64,64]{1,0:T(8,128)(2,1)S(1)}, bf16[64,64]{1,0:T(8,128)(2,1)}, u32[]{:S(2)}) copy-start(bf16[64,64]{1,0:T(8,128)(2,1)} %param.14) | copy-start | bytes 24580
  73.6 13.1 %copy-start.6 = (bf16[64,64]{1,0:T(8,128)(2,1)S(1)}, bf16[64,64]{1,0:T(8,128)(2,1)}, u32[]{:S(2)}) copy-start(bf16[64,64]{1,0:T(8,128)(2,1)} %param.13) | copy-start | bytes 24580
  73.7 13.4 %copy-start.11 = (f32[40]{0:T(128)S(1)}, f32[40]{0:T(128)}, u32[]{:S(2)}) copy-start(f32[40]{0:T(128)} %param.21) | copy-start | bytes 484
  73.7 13.6 %copy-start.12 = (f32[40]{0:T(128)S(1)}, f32[40]{0:T(128)}, u32[]{:S(2)}) copy-start(f32[40]{0:T(128)} %param.22) | copy-start | bytes 484
  81.8 34.6 %all-to-all-start.1 = ((bf16[64,2,1600]{2,1,0:T(2,128)(2,1)}), bf16[64,2,1600]{2,1,0:T(2,128)(2,1)S(1)}, u32[]{:S(2)}, u32[]{:S(2)}) async-start(bf16[64,2,1600]{2,1,0:T(2,128)(2,1)} %reshape.147), calls=%async_computation.1 | async-start | bytes 851968 | tf_op jit(solution)/shard_map/all_to_all | solution.py:93
  125.8 1.0 copy-start
  125.8 1.0 copy-start.7
  127.1 0.8 copy-start.10
Sparse Core Ops, SparseCore 0:
  33.6 49.6 all-gather.1

commit v2 on v1

--- a/solution.py
+++ b/solution.py
@@ -67,32 +67,38 @@
     )
     stacked = gathered.reshape(2 * gathered.shape[1], -1)
     product = jnp.dot(mixer, stacked, preferred_element_type=jnp.float32)
+    product = lax.reduce_precision(product, exponent_bits=8, mantissa_bits=7)
     system_rows = product.astype(jnp.bfloat16).reshape(density.shape)
     rc_count = lax.axis_size("rc")
-    col_groups = rc_count // math.gcd(state_count, rc_count)
-    per_device = state_count * col_groups // rc_count
+    col_groups = rc_count // state_count
     group_width = column_total // col_groups
-    combined = jnp.moveaxis(
-        density.reshape(2, state_count, pair_count, col_groups, group_width), 3, 2
+    outgoing = density.reshape(2, state_count, pair_count, col_groups, group_width)
+    outgoing = jnp.transpose(outgoing, (1, 3, 2, 0, 4)).reshape(
+        rc_count, pair_count, 2, group_width
     )
-    combined = combined.reshape(2, state_count * col_groups, pair_count, group_width)
-    combo_index = lax.axis_index("rc") * per_device + jnp.arange(per_device, dtype=jnp.int32)
-    state_pick = (
-        (combo_index // col_groups)[:, None] == jnp.arange(state_count, dtype=jnp.int32)[None, :]
-    ).astype(jnp.float32)
-    combo_left = jnp.sum(state_pick * left_gain[None, :], axis=1)
-    combo_right = jnp.sum(state_pick * right_gain[None, :], axis=1)
-    summed = ladder_local(
-        lax.all_to_all(combined, "rc", split_axis=1, concat_axis=2, tiled=True),
-        left_ops,
-        right_ops,
-        combo_left,
-        combo_right,
-        levels,
-    )
-    returned = lax.all_to_all(summed, "rc", split_axis=2, concat_axis=1, tiled=True)
-    returned = returned.reshape(2, state_count, col_groups, pair_count, group_width)
-    ladder_rows = jnp.moveaxis(returned, 2, 3).reshape(2, state_count, pair_count, column_total)
+    incoming = lax.all_to_all(outgoing, "rc", split_axis=0, concat_axis=0, tiled=True)
+    rows = incoming.reshape(rc_count * pair_count, 2 * group_width).astype(jnp.float32)
+    my_state = first_state + lax.axis_index("rc") // col_groups
+    left_g = lax.dynamic_slice_in_dim(left_strength, my_state, 1)
+    right_g = lax.dynamic_slice_in_dim(right_strength, my_state, 1)
+    left_ops32 = left_ops.astype(jnp.float32)
+    right_ops32 = right_ops.astype(jnp.float32)
+    left_mat = left_ops32[:levels] + left_g * left_ops32[levels:]
+    right_mat = right_ops32[:levels] + right_g * right_ops32[levels:]
+    left_out = jnp.dot(
+        left_mat, rows.reshape(levels, -1), precision=lax.Precision.HIGHEST
+    ).reshape(rows.shape)
+    block = 8
+    block_mat = jnp.kron(jnp.eye(block, dtype=jnp.float32), right_mat)
+    chunks = rows.reshape(levels // block, block * levels, -1)
+    block_mats = jnp.broadcast_to(block_mat, (levels // block,) + block_mat.shape)
+    right_out = jnp.einsum(
+        "kpq,kqn->kpn", block_mats, chunks, precision=lax.Precision.HIGHEST
+    ).reshape(rows.shape)
+    summed = (left_out + right_out).astype(jnp.bfloat16).reshape(outgoing.shape)
+    returned = lax.all_to_all(summed, "rc", split_axis=0, concat_axis=0, tiled=True)
+    returned = returned.reshape(state_count, col_groups, pair_count, 2, group_width)
+    ladder_rows = jnp.transpose(returned, (3, 0, 2, 1, 4)).reshape(density.shape)
     pair_index = lax.axis_index("rc") * pair_count + jnp.arange(pair_count, dtype=jnp.int32)
     level_index = jnp.arange(levels, dtype=jnp.int32)
     left_pick = (pair_index[:, None] // levels == level_index[None, :]).astype(jnp.float32)

time: 135 us -> 135 us (level)
  waiting for transfers between devices: 60.5 us -> 64.8 us
  local copies, waits for them, and re-layouts: 27.4 us -> 24 us
  other arithmetic: 6.18 us -> 3.31 us
  matrix products: 1.73 us -> 3.75 us
    convert_element_type x1, local copies, waits for them, and re-layouts: 6.79 us -> 0.2 us  [shards(): ladder = ladder_rows.astype(jnp.float32)]
    all_to_all x2, waiting for transfers between devices: 59.8 us -> 64.1 us  [the longest x1 34.6 us: shards(): lax.all_to_all(outgoing, 'rc', split_axis=0, concat_axis=0, tiled=True)]
    unnamed x33 -> x36, local copies, waits for them, and re-layouts: 7.65 us -> 10.5 us
    reshape x1 -> x4, local copies, waits for them, and re-layouts: 1.55 us -> 4.33 us  [the longest x1 2.24 us: shards(): right_out = jnp.einsum('kpq,kqn->kpn', block_mats, chunks, precision=lax....]
    dot_general x2, matrix products: 1.14 us -> 3.16 us  [the longest x1 2.01 us: shards(): jnp.einsum('kpq,kqn->kpn', block_mats, chunks, precision=lax.Precision.HI...]
    add x1 -> x0, local copies, waits for them, and re-layouts: 1.91 us -> none  [ladder_local(): right_all[:, :, :, :levels]]
    add x2 -> x1, other arithmetic: 2.03 us -> 0.64 us  [shards(): right_mat = right_ops32[:levels] + right_g * right_ops32[levels:]]
where the time goes in v2:
time: 135 us
  waiting for transfers between devices  64.8 us (48%)
  starting transfers between devices  25.1 us (19%)
  local copies, waits for them, and re-layouts  24 us (18%)
  between operations  13.8 us (10%)
  matrix products  3.75 us (3%)
  other arithmetic  3.31 us (2%)
    all_to_all x1, waiting for transfers between devices, shards(): lax.all_to_all(outgoing, 'rc', split_axis=0, concat_axis=0, tiled=True)  34.6 us
    all_to_all x1, waiting for transfers between devices, shards(): lax.all_to_all(summed, 'rc', split_axis=0, concat_axis=0, tiled=True)  29.5 us
    all_to_all x1, starting transfers between devices, shards(): lax.all_to_all(outgoing, 'rc', split_axis=0, concat_axis=0, tiled=True)  20.3 us
    unnamed x36, local copies, waits for them, and re-layouts  10.5 us
    all_to_all x1, starting transfers between devices, shards(): lax.all_to_all(summed, 'rc', split_axis=0, concat_axis=0, tiled=True)  4.81 us
    all_gather x1, local copies, waits for them, and re-layouts, shards(): gathered = lax.all_gather(density, 'sys', axis=1, tiled=True)  3.87 us
  transfers between devices with their start and end apart: 3, of which 2 were waited for; matrix products, arithmetic and copies ran while one was open for 17% of the time, Pallas kernels for 0%

profile of v2, /device:TPU:32, one launch (start us, length us, event | category | flops | bytes accessed | tf_op | source)
XLA Modules:
  0.0 134.7 jit_solution(544649976231454517)
XLA Ops:
  6.5 0.7 all-gather.2.cloned.1.call-update
  7.3 1.6 %reshape.97 = bf16[2,8,25,8,64]{4,3,1,2,0:T(8,128)(2,1)S(1)} reshape(bf16[2,8,25,512]{3,1,2,0:T(8,128)(2,1)} %param.12) | data formatting | bytes 819200 | tf_op jit(solution)/shard_map/reshape | solution.py:75
  8.9 0.8 copy.46
  9.7 1.3 reshape.104
  11.0 20.3 %all-to-all-start = ((bf16[64,2,1600]{2,1,0:T(2,128)(2,1)}), bf16[64,2,1600]{2,1,0:T(2,128)(2,1)S(1)}, u32[]{:S(2)}, u32[]{:S(2)}) async-start(bf16[64,2,1600]{2,1,0:T(2,128)(2,1)} %reshape.104), calls=%async_computation | async-start | bytes 851968 | tf_op jit(solution)/shard_map/all_to_all | solution.py:79
  32.0 0.6 dynamic_slice.14
  32.6 0.6 dynamic_slice.15
  33.2 0.6 fusion.10
  34.5 34.6 %all-to-all-done = bf16[64,2,1600]{2,1,0:T(2,128)(2,1)S(1)} async-done(((bf16[64,2,1600]{2,1,0:T(2,128)(2,1)}), bf16[64,2,1600]{2,1,0:T(2,128)(2,1)S(1)}, u32[]{:S(2)}, u32[]{:S(2)}) %all-to-all-start) | async-done | bytes 409632 | tf_op jit(solution)/shard_map/all_to_all | solution.py:79
  69.0 0.7 reshape.105
  70.7 1.1 fusion.12
  71.8 1.2 reshape.100
  73.0 2.0 %fusion.2 = f32[5,320,128]{2,1,0:T(8,128)} fusion(bf16[5,320,128]{2,1,0:T(8,128)(2,1)S(1)} %reshape.101, f32[320,320]{1,0:T(8,128)S(1)} %mul.151), kind=kOutput, calls=%fused_computation.5 | convolution fusion | flops 786432000 | bytes 1638400 | tf_op jit(solution)/shard_map/kpq,kqn->kpn/dot_general | solution.py:95
  75.0 2.2 %reshape.102 = f32[64,25,2,64]{3,2,1,0:T(2,128)S(1)} reshape(f32[5,320,128]{2,1,0:T(8,128)} %fusion.2) | data formatting | bytes 1638400 | tf_op jit(solution)/shard_map/reshape | solution.py:97
  77.3 1.8 %add_convert_fusion = bf16[64,25,2,64]{3,2,1,0:T(2,128)(2,1)} fusion(f32[64,25,2,64]{3,2,1,0:T(2,128)S(1)} %reshape.100, f32[64,25,2,64]{3,2,1,0:T(2,128)S(1)} %reshape.102), kind=kLoop, calls=%fused_computation.4 | loop fusion | flops 409600 | bytes 2048000 | tf_op jit(solution)/shard_map/convert_element_type | solution.py:98
  79.1 3.3 %reshape.106 = bf16[64,2,1600]{2,1,0:T(2,128)(2,1)} reshape(bf16[64,25,2,64]{3,2,1,0:T(2,128)(2,1)} %add_convert_fusion) | data formatting | bytes 819200
  82.4 4.8 %all-to-all-start.1 = ((bf16[64,2,1600]{2,1,0:T(2,128)(2,1)}), bf16[64,2,1600]{2,1,0:T(2,128)(2,1)S(1)}, u32[]{:S(2)}, u32[]{:S(2)}) async-start(bf16[64,2,1600]{2,1,0:T(2,128)(2,1)} %reshape.106), calls=%async_computation.1 | async-start | bytes 851968 | tf_op jit(solution)/shard_map/all_to_all | solution.py:99
  88.0 29.5 %all-to-all-done.1 = bf16[64,2,1600]{2,1,0:T(2,128)(2,1)S(1)} async-done(((bf16[64,2,1600]{2,1,0:T(2,128)(2,1)}), bf16[64,2,1600]{2,1,0:T(2,128)(2,1)S(1)}, u32[]{:S(2)}, u32[]{:S(2)}) %all-to-all-start.1) | async-done | bytes 409632 | tf_op jit(solution)/shard_map/all_to_all | solution.py:99
  117.6 0.7 reshape.107
  119.1 3.9 %copy.41 = bf16[2,64,25,512]{3,2,1,0:T(8,128)(2,1)S(1)} copy(bf16[2,64,25,512]{3,1,2,0:T(8,128)(2,1)} %all-gather.2.cloned.1.call-done) | data formatting | bytes 6553600 | tf_op jit(solution)/shard_map/all_gather | solution.py:58
  123.0 2.3 %copy.52 = bf16[16,8,25,512]{3,1,2,0:T(8,128)(2,1)S(1)} copy(bf16[16,8,25,512]{3,2,1,0:T(8,128)(2,1)S(1)} %bitcast.59) | data formatting | bytes 6553600
  125.3 0.6 fusion.1
  126.0 0.9 copy-done
  127.1 0.7 copy-done.8
  (62 shorter events, 4.0 us)
Async XLA Ops:
  6.5 112.6 %all-gather.2.cloned.1.call-start = ((), (), s32[]{:S(2)}) async-start(), calls=%async_computation.2 | async-start | bytes 3686400 | tf_op jit(solution)/shard_map/all_gather | solution.py:58
  8.8 22.5 %copy-start.4 = (bf16[40,40]{1,0:T(8,128)(2,1)S(1)}, bf16[40,40]{1,0:T(8,128)(2,1)}, u32[]{:S(2)}) copy-start(bf16[40,40]{1,0:T(8,128)(2,1)} %param.16) | copy-start | bytes 9604
  8.8 22.7 %copy-start.5 = (bf16[40,40]{1,0:T(8,128)(2,1)S(1)}, bf16[40,40]{1,0:T(8,128)(2,1)}, u32[]{:S(2)}) copy-start(bf16[40,40]{1,0:T(8,128)(2,1)} %param.15) | copy-start | bytes 9604
  8.8 22.9 %copy-start.2 = (bf16[40,40]{1,0:T(8,128)(2,1)S(1)}, bf16[40,40]{1,0:T(8,128)(2,1)}, u32[]{:S(2)}) copy-start(bf16[40,40]{1,0:T(8,128)(2,1)} %param.18) | copy-start | bytes 9604
  8.9 23.0 %copy-start.6 = (bf16[40,40]{1,0:T(8,128)(2,1)S(1)}, bf16[40,40]{1,0:T(8,128)(2,1)}, u32[]{:S(2)}) copy-start(bf16[40,40]{1,0:T(8,128)(2,1)} %param.17) | copy-start | bytes 9604
  8.9 23.1 %copy-start.9 = (f32[64]{0:T(128)S(1)}, f32[64]{0:T(128)}, u32[]{:S(2)}) copy-start(f32[64]{0:T(128)} %param.19) | copy-start | bytes 772
  8.9 23.7 %copy-start.10 = (f32[64]{0:T(128)S(1)}, f32[64]{0:T(128)}, u32[]{:S(2)}) copy-start(f32[64]{0:T(128)} %param.20) | copy-start | bytes 772
  11.0 58.0 %all-to-all-start = ((bf16[64,2,1600]{2,1,0:T(2,128)(2,1)}), bf16[64,2,1600]{2,1,0:T(2,128)(2,1)S(1)}, u32[]{:S(2)}, u32[]{:S(2)}) async-start(bf16[64,2,1600]{2,1,0:T(2,128)(2,1)} %reshape.104), calls=%async_computation | async-start | bytes 851968 | tf_op jit(solution)/shard_map/all_to_all | solution.py:79
  79.0 8.1 %copy-start.1 = (bf16[64,64]{1,0:T(8,128)(2,1)S(1)}, bf16[64,64]{1,0:T(8,128)(2,1)}, u32[]{:S(2)}) copy-start(bf16[64,64]{1,0:T(8,128)(2,1)} %param.14) | copy-start | bytes 24580
  79.0 8.2 %copy-start.3 = (bf16[64,64]{1,0:T(8,128)(2,1)S(1)}, bf16[64,64]{1,0:T(8,128)(2,1)}, u32[]{:S(2)}) copy-start(bf16[64,64]{1,0:T(8,128)(2,1)} %param.13) | copy-start | bytes 24580
  79.0 8.6 %copy-start.11 = (f32[40]{0:T(128)S(1)}, f32[40]{0:T(128)}, u32[]{:S(2)}) copy-start(f32[40]{0:T(128)} %param.21) | copy-start | bytes 484
  79.1 8.8 %copy-start.12 = (f32[40]{0:T(128)S(1)}, f32[40]{0:T(128)}, u32[]{:S(2)}) copy-start(f32[40]{0:T(128)} %param.22) | copy-start | bytes 484
  82.4 35.2 %all-to-all-start.1 = ((bf16[64,2,1600]{2,1,0:T(2,128)(2,1)}), bf16[64,2,1600]{2,1,0:T(2,128)(2,1)S(1)}, u32[]{:S(2)}, u32[]{:S(2)}) async-start(bf16[64,2,1600]{2,1,0:T(2,128)(2,1)} %reshape.106), calls=%async_computation.1 | async-start | bytes 851968 | tf_op jit(solution)/shard_map/all_to_all | solution.py:99
  125.9 1.0 copy-start
  125.9 1.0 copy-start.7
  127.1 0.8 copy-start.8
Sparse Core Ops, SparseCore 0:
  9.4 69.0 all-gather.1

commit v3 on v2

--- a/solution.py
+++ b/solution.py
@@ -72,12 +72,6 @@
     rc_count = lax.axis_size("rc")
     col_groups = rc_count // state_count
     group_width = column_total // col_groups
-    outgoing = density.reshape(2, state_count, pair_count, col_groups, group_width)
-    outgoing = jnp.transpose(outgoing, (1, 3, 2, 0, 4)).reshape(
-        rc_count, pair_count, 2, group_width
-    )
-    incoming = lax.all_to_all(outgoing, "rc", split_axis=0, concat_axis=0, tiled=True)
-    rows = incoming.reshape(rc_count * pair_count, 2 * group_width).astype(jnp.float32)
     my_state = first_state + lax.axis_index("rc") // col_groups
     left_g = lax.dynamic_slice_in_dim(left_strength, my_state, 1)
     right_g = lax.dynamic_slice_in_dim(right_strength, my_state, 1)
@@ -85,20 +79,31 @@
     right_ops32 = right_ops.astype(jnp.float32)
     left_mat = left_ops32[:levels] + left_g * left_ops32[levels:]
     right_mat = right_ops32[:levels] + right_g * right_ops32[levels:]
-    left_out = jnp.dot(
-        left_mat, rows.reshape(levels, -1), precision=lax.Precision.HIGHEST
-    ).reshape(rows.shape)
     block = 8
     block_mat = jnp.kron(jnp.eye(block, dtype=jnp.float32), right_mat)
-    chunks = rows.reshape(levels // block, block * levels, -1)
     block_mats = jnp.broadcast_to(block_mat, (levels // block,) + block_mat.shape)
-    right_out = jnp.einsum(
-        "kpq,kqn->kpn", block_mats, chunks, precision=lax.Precision.HIGHEST
-    ).reshape(rows.shape)
-    summed = (left_out + right_out).astype(jnp.bfloat16).reshape(outgoing.shape)
-    returned = lax.all_to_all(summed, "rc", split_axis=0, concat_axis=0, tiled=True)
-    returned = returned.reshape(state_count, col_groups, pair_count, 2, group_width)
-    ladder_rows = jnp.transpose(returned, (3, 0, 2, 1, 4)).reshape(density.shape)
+    ladder_parts = []
+    for item in range(2):
+        outgoing = density[item].reshape(state_count, pair_count, col_groups, group_width)
+        outgoing = jnp.transpose(outgoing, (0, 2, 1, 3)).reshape(
+            rc_count, pair_count, group_width
+        )
+        incoming = lax.all_to_all(outgoing, "rc", split_axis=0, concat_axis=0, tiled=True)
+        rows = incoming.reshape(rc_count * pair_count, group_width).astype(jnp.float32)
+        left_out = jnp.dot(
+            left_mat, rows.reshape(levels, -1), precision=lax.Precision.HIGHEST
+        ).reshape(rows.shape)
+        chunks = rows.reshape(levels // block, block * levels, -1)
+        right_out = jnp.einsum(
+            "kpq,kqn->kpn", block_mats, chunks, precision=lax.Precision.HIGHEST
+        ).reshape(rows.shape)
+        summed = (left_out + right_out).astype(jnp.bfloat16).reshape(outgoing.shape)
+        returned = lax.all_to_all(summed, "rc", split_axis=0, concat_axis=0, tiled=True)
+        returned = returned.reshape(state_count, col_groups, pair_count, group_width)
+        ladder_parts.append(
+            jnp.transpose(returned, (0, 2, 1, 3)).reshape(density.shape[1:])
+        )
+    ladder_rows = jnp.stack(ladder_parts)
     pair_index = lax.axis_index("rc") * pair_count + jnp.arange(pair_count, dtype=jnp.int32)
     level_index = jnp.arange(levels, dtype=jnp.int32)
     left_pick = (pair_index[:, None] // levels == level_index[None, :]).astype(jnp.float32)

time: 135 us -> 158 us (1.17)
  the two profiles are of different devices: /device:TPU:32 before, /device:TPU:64 now
where the time goes in v3:
time: 158 us; the launch traced here: 157 us
  waiting for transfers between devices  75.7 us (48%)
  starting transfers between devices  35.2 us (22%)
  local copies, waits for them, and re-layouts  22 us (14%)
  between operations  13.8 us (9%)
  other arithmetic  5.37 us (3%)
  matrix products  4.77 us (3%)
    all_to_all x2, waiting for transfers between devices, shards(): lax.all_to_all(outgoing, 'rc', split_axis=0, concat_axis=0, tiled=True)  42.5 us
    all_to_all x2, waiting for transfers between devices, shards(): lax.all_to_all(summed, 'rc', split_axis=0, concat_axis=0, tiled=True)  32.5 us
    all_to_all x2, starting transfers between devices, shards(): lax.all_to_all(outgoing, 'rc', split_axis=0, concat_axis=0, tiled=True)  24.8 us
    unnamed x38, local copies, waits for them, and re-layouts  11.3 us
    all_to_all x2, starting transfers between devices, shards(): lax.all_to_all(summed, 'rc', split_axis=0, concat_axis=0, tiled=True)  10.4 us
    all_gather x1, local copies, waits for them, and re-layouts, shards(): gathered = lax.all_gather(density, 'sys', axis=1, tiled=True)  3.87 us
  transfers between devices with their start and end apart: 5, of which 4 were waited for; matrix products, arithmetic and copies ran while one was open for 15% of the time, Pallas kernels for 0%

profile of v3, /device:TPU:64, one launch (start us, length us, event | category | flops | bytes accessed | tf_op | source)
XLA Modules:
  0.0 156.9 jit_solution(8792941318740051189)
XLA Ops:
  7.3 1.1 fusion.43
  8.9 1.1 reshape.126
  10.0 19.4 %all-to-all-start.2 = ((bf16[64,2,800]{2,1,0:T(2,128)(2,1)}), bf16[64,2,800]{2,1,0:T(2,128)(2,1)S(1)}, u32[]{:S(2)}, u32[]{:S(2)}) async-start(bf16[64,2,800]{2,1,0:T(2,128)(2,1)} %reshape.126), calls=%async_computation.2 | async-start | bytes 458752 | tf_op jit(solution)/shard_map/all_to_all | solution.py:91
  30.8 1.1 reshape.130
  34.6 22.1 %all-to-all-done.2 = bf16[64,2,800]{2,1,0:T(2,128)(2,1)S(1)} async-done(((bf16[64,2,800]{2,1,0:T(2,128)(2,1)}), bf16[64,2,800]{2,1,0:T(2,128)(2,1)S(1)}, u32[]{:S(2)}, u32[]{:S(2)}) %all-to-all-start.2) | async-done | bytes 204832 | tf_op jit(solution)/shard_map/all_to_all | solution.py:91
  56.7 5.4 %all-to-all-start = ((bf16[64,2,800]{2,1,0:T(2,128)(2,1)}), bf16[64,2,800]{2,1,0:T(2,128)(2,1)}, u32[]{:S(2)}, u32[]{:S(2)}) async-start(bf16[64,2,800]{2,1,0:T(2,128)(2,1)} %reshape.130), calls=%async_computation | async-start | bytes 458752 | tf_op jit(solution)/shard_map/all_to_all | solution.py:91
  64.2 1.0 fusion.22
  65.5 1.1 fusion.2
  66.9 1.1 reshape.128
  68.1 20.4 %all-to-all-done = bf16[64,2,800]{2,1,0:T(2,128)(2,1)} async-done(((bf16[64,2,800]{2,1,0:T(2,128)(2,1)}), bf16[64,2,800]{2,1,0:T(2,128)(2,1)}, u32[]{:S(2)}, u32[]{:S(2)}) %all-to-all-start) | async-done | bytes 204832 | tf_op jit(solution)/shard_map/all_to_all | solution.py:91
  88.5 5.8 %all-to-all-start.3 = ((bf16[64,2,800]{2,1,0:T(2,128)(2,1)}), bf16[64,2,800]{2,1,0:T(2,128)(2,1)}, u32[]{:S(2)}, u32[]{:S(2)}) async-start(bf16[64,2,800]{2,1,0:T(2,128)(2,1)} %reshape.128), calls=%async_computation.3 | async-start | bytes 458752 | tf_op jit(solution)/shard_map/all_to_all | solution.py:101
  94.4 1.4 reshape.131
  96.2 1.0 fusion.24
  97.6 1.1 fusion.4
  99.0 1.1 reshape.132
  100.2 14.8 %all-to-all-done.3 = bf16[64,2,800]{2,1,0:T(2,128)(2,1)} async-done(((bf16[64,2,800]{2,1,0:T(2,128)(2,1)}), bf16[64,2,800]{2,1,0:T(2,128)(2,1)}, u32[]{:S(2)}, u32[]{:S(2)}) %all-to-all-start.3) | async-done | bytes 204832 | tf_op jit(solution)/shard_map/all_to_all | solution.py:101
  115.0 4.6 %all-to-all-start.1 = ((bf16[64,2,800]{2,1,0:T(2,128)(2,1)}), bf16[64,2,800]{2,1,0:T(2,128)(2,1)S(1)}, u32[]{:S(2)}, u32[]{:S(2)}) async-start(bf16[64,2,800]{2,1,0:T(2,128)(2,1)} %reshape.132), calls=%async_computation.1 | async-start | bytes 458752 | tf_op jit(solution)/shard_map/all_to_all | solution.py:101
  119.7 0.7 fusion.40
  120.7 0.7 fusion.29
  121.4 1.4 reshape.129
  123.3 17.7 %all-to-all-done.1 = bf16[64,2,800]{2,1,0:T(2,128)(2,1)S(1)} async-done(((bf16[64,2,800]{2,1,0:T(2,128)(2,1)}), bf16[64,2,800]{2,1,0:T(2,128)(2,1)S(1)}, u32[]{:S(2)}, u32[]{:S(2)}) %all-to-all-start.1) | async-done | bytes 204832 | tf_op jit(solution)/shard_map/all_to_all | solution.py:101
  141.9 3.9 %copy.47 = bf16[2,64,25,512]{3,2,1,0:T(8,128)(2,1)S(1)} copy(bf16[2,64,25,512]{3,1,2,0:T(8,128)(2,1)} %all-gather.2.cloned.1.call-done) | data formatting | bytes 6553600 | tf_op jit(solution)/shard_map/all_gather | solution.py:58
  145.8 2.3 %copy.68 = bf16[16,8,25,512]{3,1,2,0:T(8,128)(2,1)S(1)} copy(bf16[16,8,25,512]{3,2,1,0:T(8,128)(2,1)S(1)} %bitcast.68) | data formatting | bytes 6553600
  149.3 0.8 pad_maximum_fusion
  (79 shorter events, 12.0 us)
Async XLA Ops:
  6.5 22.9 %copy-start.3 = (bf16[64,64]{1,0:T(8,128)(2,1)S(1)}, bf16[64,64]{1,0:T(8,128)(2,1)}, u32[]{:S(2)}) copy-start(bf16[64,64]{1,0:T(8,128)(2,1)} %param.13) | copy-start | bytes 24580
  6.5 23.0 %copy-start.1 = (bf16[64,64]{1,0:T(8,128)(2,1)S(1)}, bf16[64,64]{1,0:T(8,128)(2,1)}, u32[]{:S(2)}) copy-start(bf16[64,64]{1,0:T(8,128)(2,1)} %param.14) | copy-start | bytes 24580
  6.5 23.1 %copy-start.4 = (bf16[40,40]{1,0:T(8,128)(2,1)S(1)}, bf16[40,40]{1,0:T(8,128)(2,1)}, u32[]{:S(2)}) copy-start(bf16[40,40]{1,0:T(8,128)(2,1)} %param.16) | copy-start | bytes 9604
  6.5 23.3 %copy-start.5 = (bf16[40,40]{1,0:T(8,128)(2,1)S(1)}, bf16[40,40]{1,0:T(8,128)(2,1)}, u32[]{:S(2)}) copy-start(bf16[40,40]{1,0:T(8,128)(2,1)} %param.15) | copy-start | bytes 9604
  6.5 23.5 %copy-start.2 = (bf16[40,40]{1,0:T(8,128)(2,1)S(1)}, bf16[40,40]{1,0:T(8,128)(2,1)}, u32[]{:S(2)}) copy-start(bf16[40,40]{1,0:T(8,128)(2,1)} %param.18) | copy-start | bytes 9604
  6.5 23.6 %copy-start.6 = (bf16[40,40]{1,0:T(8,128)(2,1)S(1)}, bf16[40,40]{1,0:T(8,128)(2,1)}, u32[]{:S(2)}) copy-start(bf16[40,40]{1,0:T(8,128)(2,1)} %param.17) | copy-start | bytes 9604
  6.6 135.3 %all-gather.2.cloned.1.call-start = ((), (), s32[]{:S(2)}) async-start(), calls=%async_computation.4 | async-start | bytes 3686400 | tf_op jit(solution)/shard_map/all_gather | solution.py:58
  8.6 23.4 %copy-start.8 = (f32[64]{0:T(128)S(1)}, f32[64]{0:T(128)}, u32[]{:S(2)}) copy-start(f32[64]{0:T(128)} %param.20) | copy-start | bytes 772
  10.0 46.7 %all-to-all-start.2 = ((bf16[64,2,800]{2,1,0:T(2,128)(2,1)}), bf16[64,2,800]{2,1,0:T(2,128)(2,1)S(1)}, u32[]{:S(2)}, u32[]{:S(2)}) async-start(bf16[64,2,800]{2,1,0:T(2,128)(2,1)} %reshape.126), calls=%async_computation.2 | async-start | bytes 458752 | tf_op jit(solution)/shard_map/all_to_all | solution.py:91
  29.4 32.7 %copy-start.9 = (f32[64]{0:T(128)S(1)}, f32[64]{0:T(128)}, u32[]{:S(2)}) copy-start(f32[64]{0:T(128)} %param.19) | copy-start | bytes 772
  56.7 31.8 %all-to-all-start = ((bf16[64,2,800]{2,1,0:T(2,128)(2,1)}), bf16[64,2,800]{2,1,0:T(2,128)(2,1)}, u32[]{:S(2)}, u32[]{:S(2)}) async-start(bf16[64,2,800]{2,1,0:T(2,128)(2,1)} %reshape.130), calls=%async_computation | async-start | bytes 458752 | tf_op jit(solution)/shard_map/all_to_all | solution.py:91
  88.5 26.5 %all-to-all-start.3 = ((bf16[64,2,800]{2,1,0:T(2,128)(2,1)}), bf16[64,2,800]{2,1,0:T(2,128)(2,1)}, u32[]{:S(2)}, u32[]{:S(2)}) async-start(bf16[64,2,800]{2,1,0:T(2,128)(2,1)} %reshape.128), calls=%async_computation.3 | async-start | bytes 458752 | tf_op jit(solution)/shard_map/all_to_all | solution.py:101
  98.7 21.7 %copy-start.10 = (f32[40]{0:T(128)S(1)}, f32[40]{0:T(128)}, u32[]{:S(2)}) copy-start(f32[40]{0:T(128)} %param.21) | copy-start | bytes 484
  98.7 21.9 %copy-start.11 = (f32[40]{0:T(128)S(1)}, f32[40]{0:T(128)}, u32[]{:S(2)}) copy-start(f32[40]{0:T(128)} %param.22) | copy-start | bytes 484
  115.0 25.9 %all-to-all-start.1 = ((bf16[64,2,800]{2,1,0:T(2,128)(2,1)}), bf16[64,2,800]{2,1,0:T(2,128)(2,1)S(1)}, u32[]{:S(2)}, u32[]{:S(2)}) async-start(bf16[64,2,800]{2,1,0:T(2,128)(2,1)} %reshape.132), calls=%async_computation.1 | async-start | bytes 458752 | tf_op jit(solution)/shard_map/all_to_all | solution.py:101
  148.1 1.0 copy-start
  148.1 1.0 copy-start.7
Sparse Core Ops, SparseCore 0:
  9.5 71.2 all-gather.1

commit v4 on v2

--- a/solution.py
+++ b/solution.py
@@ -55,18 +55,14 @@
     first_state = lax.axis_index("sys") * state_count
     left_gain = lax.dynamic_slice_in_dim(left_strength, first_state, state_count)
     right_gain = lax.dynamic_slice_in_dim(right_strength, first_state, state_count)
-    gathered = lax.all_gather(density, "sys", axis=1, tiled=True)
+    flat_local = jnp.transpose(density.reshape(2, state_count, -1), (1, 0, 2))
+    gathered = lax.all_gather(flat_local.reshape(2 * state_count, -1), "sys", axis=0, tiled=True)
     own_real = lax.dynamic_slice_in_dim(herm_real, first_state, state_count, axis=0)
     own_imag = lax.dynamic_slice_in_dim(herm_imag, first_state, state_count, axis=0)
-    mixer = jnp.concatenate(
-        [
-            jnp.concatenate([own_real, -own_imag], axis=1),
-            jnp.concatenate([own_imag, own_real], axis=1),
-        ],
-        axis=0,
-    )
-    stacked = gathered.reshape(2 * gathered.shape[1], -1)
-    product = jnp.dot(mixer, stacked, preferred_element_type=jnp.float32)
+    real_rows = jnp.stack([own_real, -own_imag], axis=2).reshape(state_count, -1)
+    imag_rows = jnp.stack([own_imag, own_real], axis=2).reshape(state_count, -1)
+    mixer = jnp.concatenate([real_rows, imag_rows], axis=0)
+    product = jnp.dot(mixer, gathered, preferred_element_type=jnp.float32)
     product = lax.reduce_precision(product, exponent_bits=8, mantissa_bits=7)
     system_rows = product.astype(jnp.bfloat16).reshape(density.shape)
     rc_count = lax.axis_size("rc")

time: 135 us -> 131 us (0.970)
  local copies, waits for them, and re-layouts: 24 us -> 19.4 us
  matrix products: 3.75 us -> 5.62 us
  waiting for transfers between devices: 64.8 us -> 63 us
    all_gather x1 -> x0, local copies, waits for them, and re-layouts: 3.87 us -> none  [shards(): gathered = lax.all_gather(density, 'sys', axis=1, tiled=True)]
    unnamed x36 -> x37, local copies, waits for them, and re-layouts: 10.5 us -> 8.25 us
    dot_general x1, matrix products: 0.59 us -> 2.46 us  [shards(): product = jnp.dot(mixer, gathered, preferred_element_type=jnp.float32)]
    transpose x0 -> x1, local copies, waits for them, and re-layouts: none -> 1.39 us  [shards(): flat_local = jnp.transpose(density.reshape(2, state_count, -1), (1, 0, 2))]
where the time goes in v4:
time: 131 us; the launch traced here: 130 us
  waiting for transfers between devices  63 us (48%)
  starting transfers between devices  25.1 us (19%)
  local copies, waits for them, and re-layouts  19.4 us (15%)
  between operations  13.8 us (11%)
  matrix products  5.62 us (4%)
  other arithmetic  3.3 us (3%)
    all_to_all x1, waiting for transfers between devices, shards(): lax.all_to_all(outgoing, 'rc', split_axis=0, concat_axis=0, tiled=True)  34.4 us
    all_to_all x1, waiting for transfers between devices, shards(): lax.all_to_all(summed, 'rc', split_axis=0, concat_axis=0, tiled=True)  28.6 us
    all_to_all x1, starting transfers between devices, shards(): lax.all_to_all(outgoing, 'rc', split_axis=0, concat_axis=0, tiled=True)  20.5 us
    unnamed x37, local copies, waits for them, and re-layouts  8.25 us
    all_to_all x1, starting transfers between devices, shards(): lax.all_to_all(summed, 'rc', split_axis=0, concat_axis=0, tiled=True)  4.63 us
  transfers between devices with their start and end apart: 3, of which 2 were waited for; matrix products, arithmetic and copies ran while one was open for 17% of the time, Pallas kernels for 0%

profile of v4, /device:TPU:32, one launch (start us, length us, event | category | flops | bytes accessed | tf_op | source)
XLA Modules:
  0.0 130.2 jit_solution(6062171686965357558)
XLA Ops:
  6.5 1.4 %copy.78 = bf16[8,2,12800]{2,1,0:T(2,128)(2,1)S(1)} copy(bf16[8,2,12800]{2,0,1:T(8,128)(2,1)} %bitcast.67) | data formatting | bytes 819200 | tf_op jit(solution)/shard_map/transpose | solution.py:58
  7.9 0.9 reshape.108
  8.9 0.4 reshape.109
  9.4 0.8 copy.83
  10.2 1.3 %reshape.116 = bf16[64,2,1600]{2,1,0:T(2,128)(2,1)} reshape(bf16[64,25,2,64]{3,2,1,0:T(2,128)(2,1)S(1)} %bitcast.68) | data formatting | bytes 819200
  11.5 20.5 %all-to-all-start = ((bf16[64,2,1600]{2,1,0:T(2,128)(2,1)}), bf16[64,2,1600]{2,1,0:T(2,128)(2,1)S(1)}, u32[]{:S(2)}, u32[]{:S(2)}) async-start(bf16[64,2,1600]{2,1,0:T(2,128)(2,1)} %reshape.116), calls=%async_computation | async-start | bytes 851968 | tf_op jit(solution)/shard_map/all_to_all | solution.py:75
  32.7 0.7 dynamic_slice.14
  33.3 0.6 dynamic_slice.15
  34.0 0.6 fusion.10
  35.2 34.4 %all-to-all-done = bf16[64,2,1600]{2,1,0:T(2,128)(2,1)S(1)} async-done(((bf16[64,2,1600]{2,1,0:T(2,128)(2,1)}), bf16[64,2,1600]{2,1,0:T(2,128)(2,1)S(1)}, u32[]{:S(2)}, u32[]{:S(2)}) %all-to-all-start) | async-done | bytes 409632 | tf_op jit(solution)/shard_map/all_to_all | solution.py:75
  69.6 0.7 reshape.117
  70.3 0.6 reshape.111
  71.3 1.2 fusion.12
  72.5 1.2 reshape.112
  73.6 2.0 %fusion.2 = f32[5,320,128]{2,1,0:T(8,128)} fusion(bf16[5,320,128]{2,1,0:T(8,128)(2,1)S(1)} %reshape.113, f32[320,320]{1,0:T(8,128)S(1)} %mul.151), kind=kOutput, calls=%fused_computation.5 | convolution fusion | flops 786432000 | bytes 1638400 | tf_op jit(solution)/shard_map/kpq,kqn->kpn/dot_general | solution.py:91
  75.6 2.2 %reshape.114 = f32[64,25,2,64]{3,2,1,0:T(2,128)S(1)} reshape(f32[5,320,128]{2,1,0:T(8,128)} %fusion.2) | data formatting | bytes 1638400 | tf_op jit(solution)/shard_map/reshape | solution.py:93
  77.9 1.7 %add_convert_fusion = bf16[64,25,2,64]{3,2,1,0:T(2,128)(2,1)} fusion(f32[64,25,2,64]{3,2,1,0:T(2,128)S(1)} %reshape.112, f32[64,25,2,64]{3,2,1,0:T(2,128)S(1)} %reshape.114), kind=kLoop, calls=%fused_computation.4 | loop fusion | flops 409600 | bytes 2048000 | tf_op jit(solution)/shard_map/convert_element_type | solution.py:94
  79.6 3.3 %reshape.118 = bf16[64,2,1600]{2,1,0:T(2,128)(2,1)} reshape(bf16[64,25,2,64]{3,2,1,0:T(2,128)(2,1)} %add_convert_fusion) | data formatting | bytes 819200
  82.9 4.6 %all-to-all-start.1 = ((bf16[64,2,1600]{2,1,0:T(2,128)(2,1)}), bf16[64,2,1600]{2,1,0:T(2,128)(2,1)S(1)}, u32[]{:S(2)}, u32[]{:S(2)}) async-start(bf16[64,2,1600]{2,1,0:T(2,128)(2,1)} %reshape.118), calls=%async_computation.1 | async-start | bytes 851968 | tf_op jit(solution)/shard_map/all_to_all | solution.py:95
  88.8 28.6 %all-to-all-done.1 = bf16[64,2,1600]{2,1,0:T(2,128)(2,1)S(1)} async-done(((bf16[64,2,1600]{2,1,0:T(2,128)(2,1)}), bf16[64,2,1600]{2,1,0:T(2,128)(2,1)S(1)}, u32[]{:S(2)}, u32[]{:S(2)}) %all-to-all-start.1) | async-done | bytes 409632 | tf_op jit(solution)/shard_map/all_to_all | solution.py:95
  117.4 0.7 reshape.119
  118.9 2.5 %fusion.1 = f32[16,12800]{1,0:T(8,128)S(1)} fusion(bf16[128,12800]{1,0:T(8,128)(2,1)} %all-gather.2.cloned.1.call-done, bf16[8,128]{1,0:T(8,128)(2,1)S(1)} %copy.77, bf16[8,128]{1,0:T(8,128)(2,1)S(1)} %copy.76), kind=kOutput, calls=%fused_computation.2 | convolution fusion | flops 53051392 | bytes 4100096 | tf_op jit(solution)/shard_map/dot_general | solution.py:65
  121.4 0.9 copy-done.1
  122.6 0.7 copy-done.9
  (69 shorter events, 3.8 us)
Async XLA Ops:
  6.5 2.3 %copy-start = (bf16[2,8,25,512]{3,1,2,0:T(8,128)(2,1)S(1)}, bf16[2,8,25,512]{3,1,2,0:T(8,128)(2,1)}, u32[]{:S(2)}) copy-start(bf16[2,8,25,512]{3,1,2,0:T(8,128)(2,1)} %param.12) | copy-start | bytes 1228804
  6.5 112.4 %all-gather.2.cloned.1.call-start = ((), (), s32[]{:S(2)}) async-start(), calls=%async_computation.2 | async-start | bytes 3686400 | tf_op jit(solution)/shard_map/all_gather | solution.py:59
  9.3 22.7 %copy-start.5 = (bf16[40,40]{1,0:T(8,128)(2,1)S(1)}, bf16[40,40]{1,0:T(8,128)(2,1)}, u32[]{:S(2)}) copy-start(bf16[40,40]{1,0:T(8,128)(2,1)} %param.16) | copy-start | bytes 9604
  9.3 22.9 %copy-start.6 = (bf16[40,40]{1,0:T(8,128)(2,1)S(1)}, bf16[40,40]{1,0:T(8,128)(2,1)}, u32[]{:S(2)}) copy-start(bf16[40,40]{1,0:T(8,128)(2,1)} %param.15) | copy-start | bytes 9604
  9.3 23.1 %copy-start.3 = (bf16[40,40]{1,0:T(8,128)(2,1)S(1)}, bf16[40,40]{1,0:T(8,128)(2,1)}, u32[]{:S(2)}) copy-start(bf16[40,40]{1,0:T(8,128)(2,1)} %param.18) | copy-start | bytes 9604
  9.3 23.2 %copy-start.7 = (bf16[40,40]{1,0:T(8,128)(2,1)S(1)}, bf16[40,40]{1,0:T(8,128)(2,1)}, u32[]{:S(2)}) copy-start(bf16[40,40]{1,0:T(8,128)(2,1)} %param.17) | copy-start | bytes 9604
  9.3 23.3 %copy-start.10 = (f32[64]{0:T(128)S(1)}, f32[64]{0:T(128)}, u32[]{:S(2)}) copy-start(f32[64]{0:T(128)} %param.19) | copy-start | bytes 772
  9.3 24.0 %copy-start.11 = (f32[64]{0:T(128)S(1)}, f32[64]{0:T(128)}, u32[]{:S(2)}) copy-start(f32[64]{0:T(128)} %param.20) | copy-start | bytes 772
  11.5 58.1 %all-to-all-start = ((bf16[64,2,1600]{2,1,0:T(2,128)(2,1)}), bf16[64,2,1600]{2,1,0:T(2,128)(2,1)S(1)}, u32[]{:S(2)}, u32[]{:S(2)}) async-start(bf16[64,2,1600]{2,1,0:T(2,128)(2,1)} %reshape.116), calls=%async_computation | async-start | bytes 851968 | tf_op jit(solution)/shard_map/all_to_all | solution.py:75
  79.6 8.0 %copy-start.2 = (bf16[64,64]{1,0:T(8,128)(2,1)S(1)}, bf16[64,64]{1,0:T(8,128)(2,1)}, u32[]{:S(2)}) copy-start(bf16[64,64]{1,0:T(8,128)(2,1)} %param.14) | copy-start | bytes 24580
  79.6 8.1 %copy-start.4 = (bf16[64,64]{1,0:T(8,128)(2,1)S(1)}, bf16[64,64]{1,0:T(8,128)(2,1)}, u32[]{:S(2)}) copy-start(bf16[64,64]{1,0:T(8,128)(2,1)} %param.13) | copy-start | bytes 24580
  79.6 8.8 %copy-start.12 = (f32[40]{0:T(128)S(1)}, f32[40]{0:T(128)}, u32[]{:S(2)}) copy-start(f32[40]{0:T(128)} %param.21) | copy-start | bytes 484
  79.6 9.0 %copy-start.13 = (f32[40]{0:T(128)S(1)}, f32[40]{0:T(128)}, u32[]{:S(2)}) copy-start(f32[40]{0:T(128)} %param.22) | copy-start | bytes 484
  82.9 34.4 %all-to-all-start.1 = ((bf16[64,2,1600]{2,1,0:T(2,128)(2,1)}), bf16[64,2,1600]{2,1,0:T(2,128)(2,1)S(1)}, u32[]{:S(2)}, u32[]{:S(2)}) async-start(bf16[64,2,1600]{2,1,0:T(2,128)(2,1)} %reshape.118), calls=%async_computation.1 | async-start | bytes 851968 | tf_op jit(solution)/shard_map/all_to_all | solution.py:95
  121.4 1.0 copy-start.1
  121.4 1.0 copy-start.8
  122.6 0.8 copy-start.9
Sparse Core Ops, SparseCore 0:
  9.4 69.2 all-gather.1

commit v5 on v4

--- a/solution.py
+++ b/solution.py
@@ -81,15 +81,13 @@
     right_ops32 = right_ops.astype(jnp.float32)
     left_mat = left_ops32[:levels] + left_g * left_ops32[levels:]
     right_mat = right_ops32[:levels] + right_g * right_ops32[levels:]
-    left_out = jnp.dot(
-        left_mat, rows.reshape(levels, -1), precision=lax.Precision.HIGHEST
+    cube = rows.reshape(levels, levels, -1)
+    left_out = jnp.einsum(
+        "xa,abn->xbn", left_mat, cube, precision=lax.Precision.HIGHEST
     ).reshape(rows.shape)
-    block = 8
-    block_mat = jnp.kron(jnp.eye(block, dtype=jnp.float32), right_mat)
-    chunks = rows.reshape(levels // block, block * levels, -1)
-    block_mats = jnp.broadcast_to(block_mat, (levels // block,) + block_mat.shape)
+    right_mats = jnp.broadcast_to(right_mat, (levels,) + right_mat.shape)
     right_out = jnp.einsum(
-        "kpq,kqn->kpn", block_mats, chunks, precision=lax.Precision.HIGHEST
+        "ayb,abn->ayn", right_mats, cube, precision=lax.Precision.HIGHEST
     ).reshape(rows.shape)
     summed = (left_out + right_out).astype(jnp.bfloat16).reshape(outgoing.shape)
     returned = lax.all_to_all(summed, "rc", split_axis=0, concat_axis=0, tiled=True)

time: 131 us -> 126 us (0.962)
  local copies, waits for them, and re-layouts: 19.4 us -> 14.6 us
  waiting for transfers between devices: 63 us -> 65.5 us
    reshape x4 -> x1, local copies, waits for them, and re-layouts: 4.33 us -> 0.36 us  [shards(): cube = rows.reshape(levels, levels, -1)]
    unnamed x37 -> x35, local copies, waits for them, and re-layouts: 8.25 us -> 5.32 us
    all_to_all x1, waiting for transfers between devices: 28.6 us -> 30.3 us  [shards(): lax.all_to_all(summed, 'rc', split_axis=0, concat_axis=0, tiled=True)]
  transfers between devices with their start and end apart: 3 -> 3, of which waited for: 2 -> 2; matrix products, arithmetic and copies ran while one was open for 17% -> 12% of each run, Pallas kernels for 0% -> 0%
where the time goes in v5:
time: 126 us
  waiting for transfers between devices  65.5 us (52%)
  starting transfers between devices  25.1 us (20%)
  local copies, waits for them, and re-layouts  14.6 us (12%)
  between operations  13.8 us (11%)
  matrix products  4.4 us (3%)
  other arithmetic  2.04 us (2%)
    all_to_all x1, waiting for transfers between devices, shards(): lax.all_to_all(outgoing, 'rc', split_axis=0, concat_axis=0, tiled=True)  35.2 us
    all_to_all x1, waiting for transfers between devices, shards(): lax.all_to_all(summed, 'rc', split_axis=0, concat_axis=0, tiled=True)  30.3 us
    all_to_all x1, starting transfers between devices, shards(): lax.all_to_all(outgoing, 'rc', split_axis=0, concat_axis=0, tiled=True)  20.3 us
    unnamed x35, local copies, waits for them, and re-layouts  5.32 us
    all_to_all x1, starting transfers between devices, shards(): lax.all_to_all(summed, 'rc', split_axis=0, concat_axis=0, tiled=True)  4.81 us
  transfers between devices with their start and end apart: 3, of which 2 were waited for; matrix products, arithmetic and copies ran while one was open for 12% of the time, Pallas kernels for 0%

profile of v5, /device:TPU:32, one launch (start us, length us, event | category | flops | bytes accessed | tf_op | source)
XLA Modules:
  0.0 125.5 jit_solution(3364385558395267251)
XLA Ops:
  6.5 1.3 %copy.90 = bf16[8,2,12800]{2,1,0:T(2,128)(2,1)S(1)} copy(bf16[8,2,12800]{2,0,1:T(8,128)(2,1)} %bitcast.65) | data formatting | bytes 819200 | tf_op jit(solution)/shard_map/transpose | solution.py:58
  7.9 0.9 reshape.88
  8.9 1.6 %reshape.89 = bf16[2,8,25,8,64]{4,3,1,2,0:T(8,128)(2,1)S(1)} reshape(bf16[2,8,25,512]{3,1,2,0:T(8,128)(2,1)} %param.12) | data formatting | bytes 819200 | tf_op jit(solution)/shard_map/reshape | solution.py:71
  10.4 0.8 copy.95
  11.3 1.3 %reshape.94 = bf16[64,2,1600]{2,1,0:T(2,128)(2,1)} reshape(bf16[64,25,2,64]{3,2,1,0:T(2,128)(2,1)S(1)} %bitcast.66) | data formatting | bytes 819200
  12.6 20.3 %all-to-all-start = ((bf16[64,2,1600]{2,1,0:T(2,128)(2,1)}), bf16[64,2,1600]{2,1,0:T(2,128)(2,1)S(1)}, u32[]{:S(2)}, u32[]{:S(2)}) async-start(bf16[64,2,1600]{2,1,0:T(2,128)(2,1)} %reshape.94), calls=%async_computation | async-start | bytes 851968 | tf_op jit(solution)/shard_map/all_to_all | solution.py:75
  33.5 0.7 dynamic_slice.15
  34.2 0.6 dynamic_slice.14
  34.8 0.7 fusion.12
  35.5 35.2 %all-to-all-done = bf16[64,2,1600]{2,1,0:T(2,128)(2,1)S(1)} async-done(((bf16[64,2,1600]{2,1,0:T(2,128)(2,1)}), bf16[64,2,1600]{2,1,0:T(2,128)(2,1)S(1)}, u32[]{:S(2)}, u32[]{:S(2)}) %all-to-all-start) | async-done | bytes 409632 | tf_op jit(solution)/shard_map/all_to_all | solution.py:75
  70.7 0.7 reshape.95
  71.4 0.4 reshape.91
  71.8 0.8 fusion.10
  72.6 1.2 fusion.2
  73.8 0.3 convert_element_type.97
  74.2 1.3 %reshape.96 = bf16[64,2,1600]{2,1,0:T(2,128)(2,1)} reshape(bf16[64,25,2,64]{3,2,1,0:T(2,128)(2,1)S(1)} %convert_element_type.97) | data formatting | bytes 819200
  75.5 4.8 %all-to-all-start.1 = ((bf16[64,2,1600]{2,1,0:T(2,128)(2,1)}), bf16[64,2,1600]{2,1,0:T(2,128)(2,1)S(1)}, u32[]{:S(2)}, u32[]{:S(2)}) async-start(bf16[64,2,1600]{2,1,0:T(2,128)(2,1)} %reshape.96), calls=%async_computation.1 | async-start | bytes 851968 | tf_op jit(solution)/shard_map/all_to_all | solution.py:93
  81.5 30.3 %all-to-all-done.1 = bf16[64,2,1600]{2,1,0:T(2,128)(2,1)S(1)} async-done(((bf16[64,2,1600]{2,1,0:T(2,128)(2,1)}), bf16[64,2,1600]{2,1,0:T(2,128)(2,1)S(1)}, u32[]{:S(2)}, u32[]{:S(2)}) %all-to-all-start.1) | async-done | bytes 409632 | tf_op jit(solution)/shard_map/all_to_all | solution.py:93
  111.8 0.7 reshape.97
  112.6 0.6 convert_bitcast_fusion
  113.1 1.3 %fusion.37 = (f32[1,8,25,8,64]{4,0,2,3,1:T(1,128)S(1)}, f32[1,8,25,8,64]{4,0,2,3,1:T(1,128)S(1)}) fusion(f32[2,8,25,8,64]{4,0,2,3,1:T(2,128)S(1)} %convert_bitcast_fusion), kind=kLoop, calls=%fused_computation.68 | loop fusion | bytes 1638400 | tf_op jit(solution)/shard_map/slice | solution.py:110
  115.1 2.5 %fusion.1 = f32[16,12800]{1,0:T(8,128)S(1)} fusion(bf16[128,12800]{1,0:T(8,128)(2,1)} %all-gather.2.cloned.1.call-done, bf16[8,128]{1,0:T(8,128)(2,1)S(1)} %copy.89, bf16[8,128]{1,0:T(8,128)(2,1)S(1)} %copy.88), kind=kOutput, calls=%fused_computation.2 | convolution fusion | flops 53051392 | bytes 4100096 | tf_op jit(solution)/shard_map/dot_general | solution.py:65
  117.7 0.2 fusion.5
  117.9 0.7 copy-done.8
  (64 shorter events, 2.6 us)
Async XLA Ops:
  6.5 108.6 %all-gather.2.cloned.1.call-start = ((), (), s32[]{:S(2)}) async-start(), calls=%async_computation.2 | async-start | bytes 3686400 | tf_op jit(solution)/shard_map/all_gather | solution.py:59
  7.9 25.0 %copy-start.2 = (bf16[40,40]{1,0:T(8,128)(2,1)S(1)}, bf16[40,40]{1,0:T(8,128)(2,1)}, u32[]{:S(2)}) copy-start(bf16[40,40]{1,0:T(8,128)(2,1)} %param.18) | copy-start | bytes 9604
  7.9 25.1 %copy-start.4 = (bf16[40,40]{1,0:T(8,128)(2,1)S(1)}, bf16[40,40]{1,0:T(8,128)(2,1)}, u32[]{:S(2)}) copy-start(bf16[40,40]{1,0:T(8,128)(2,1)} %param.17) | copy-start | bytes 9604
  7.9 25.3 %copy-start.5 = (bf16[40,40]{1,0:T(8,128)(2,1)S(1)}, bf16[40,40]{1,0:T(8,128)(2,1)}, u32[]{:S(2)}) copy-start(bf16[40,40]{1,0:T(8,128)(2,1)} %param.16) | copy-start | bytes 9604
  7.9 25.4 %copy-start.6 = (bf16[40,40]{1,0:T(8,128)(2,1)S(1)}, bf16[40,40]{1,0:T(8,128)(2,1)}, u32[]{:S(2)}) copy-start(bf16[40,40]{1,0:T(8,128)(2,1)} %param.15) | copy-start | bytes 9604
  7.9 25.6 %copy-start.9 = (f32[64]{0:T(128)S(1)}, f32[64]{0:T(128)}, u32[]{:S(2)}) copy-start(f32[64]{0:T(128)} %param.20) | copy-start | bytes 772
  7.9 26.3 %copy-start.10 = (f32[64]{0:T(128)S(1)}, f32[64]{0:T(128)}, u32[]{:S(2)}) copy-start(f32[64]{0:T(128)} %param.19) | copy-start | bytes 772
  12.6 58.1 %all-to-all-start = ((bf16[64,2,1600]{2,1,0:T(2,128)(2,1)}), bf16[64,2,1600]{2,1,0:T(2,128)(2,1)S(1)}, u32[]{:S(2)}, u32[]{:S(2)}) async-start(bf16[64,2,1600]{2,1,0:T(2,128)(2,1)} %reshape.94), calls=%async_computation | async-start | bytes 851968 | tf_op jit(solution)/shard_map/all_to_all | solution.py:75
  71.8 8.5 %copy-start.1 = (bf16[64,64]{1,0:T(8,128)(2,1)S(1)}, bf16[64,64]{1,0:T(8,128)(2,1)}, u32[]{:S(2)}) copy-start(bf16[64,64]{1,0:T(8,128)(2,1)} %param.14) | copy-start | bytes 24580
  71.8 8.6 %copy-start.3 = (bf16[64,64]{1,0:T(8,128)(2,1)S(1)}, bf16[64,64]{1,0:T(8,128)(2,1)}, u32[]{:S(2)}) copy-start(bf16[64,64]{1,0:T(8,128)(2,1)} %param.13) | copy-start | bytes 24580
  72.6 8.6 %copy-start.11 = (f32[40]{0:T(128)S(1)}, f32[40]{0:T(128)}, u32[]{:S(2)}) copy-start(f32[40]{0:T(128)} %param.21) | copy-start | bytes 484
  72.6 8.7 %copy-start.12 = (f32[40]{0:T(128)S(1)}, f32[40]{0:T(128)}, u32[]{:S(2)}) copy-start(f32[40]{0:T(128)} %param.22) | copy-start | bytes 484
  75.5 36.3 %all-to-all-start.1 = ((bf16[64,2,1600]{2,1,0:T(2,128)(2,1)}), bf16[64,2,1600]{2,1,0:T(2,128)(2,1)S(1)}, u32[]{:S(2)}, u32[]{:S(2)}) async-start(bf16[64,2,1600]{2,1,0:T(2,128)(2,1)} %reshape.96), calls=%async_computation.1 | async-start | bytes 851968 | tf_op jit(solution)/shard_map/all_to_all | solution.py:93
  114.8 2.8 %copy-start = (bf16[2,8,25,512]{3,1,2,0:T(8,128)(2,1)S(1)}, bf16[2,8,25,512]{3,1,2,0:T(8,128)(2,1)}, u32[]{:S(2)}) copy-start(bf16[2,8,25,512]{3,1,2,0:T(8,128)(2,1)} %param.12) | copy-start | bytes 1228804
  114.8 2.8 %copy-start.7 = (f32[512]{0:T(512)S(1)}, f32[512]{0:T(512)}, u32[]{:S(2)}) copy-start(f32[512]{0:T(512)} %param.23) | copy-start | bytes 6148
  117.9 0.8 copy-start.8
Sparse Core Ops, SparseCore 0:
  9.4 68.9 all-gather.1

commit v6 on v5

--- a/solution.py
+++ b/solution.py
@@ -56,12 +56,22 @@
     left_gain = lax.dynamic_slice_in_dim(left_strength, first_state, state_count)
     right_gain = lax.dynamic_slice_in_dim(right_strength, first_state, state_count)
     flat_local = jnp.transpose(density.reshape(2, state_count, -1), (1, 0, 2))
-    gathered = lax.all_gather(flat_local.reshape(2 * state_count, -1), "sys", axis=0, tiled=True)
+    local_rows = flat_local.reshape(2 * state_count, -1)
+    sys_count = lax.axis_size("sys")
+    blocks = [local_rows]
+    for shift in range(1, sys_count):
+        pairs = [(i, (i + shift) % sys_count) for i in range(sys_count)]
+        blocks.append(lax.ppermute(local_rows, "sys", perm=pairs))
+    gathered = jnp.concatenate(blocks, axis=0)
     own_real = lax.dynamic_slice_in_dim(herm_real, first_state, state_count, axis=0)
     own_imag = lax.dynamic_slice_in_dim(herm_imag, first_state, state_count, axis=0)
     real_rows = jnp.stack([own_real, -own_imag], axis=2).reshape(state_count, -1)
     imag_rows = jnp.stack([own_imag, own_real], axis=2).reshape(state_count, -1)
     mixer = jnp.concatenate([real_rows, imag_rows], axis=0)
+    mixer = mixer.reshape(2 * state_count, sys_count, 2 * state_count)
+    me = lax.axis_index("sys")
+    sources = (me - jnp.arange(sys_count, dtype=jnp.int32)) % sys_count
+    mixer = jnp.take(mixer, sources, axis=1).reshape(2 * state_count, -1)
     product = jnp.dot(mixer, gathered, preferred_element_type=jnp.float32)
     product = lax.reduce_precision(product, exponent_bits=8, mantissa_bits=7)
     system_rows = product.astype(jnp.bfloat16).reshape(density.shape)

time: 126 us -> 158 us (1.25)
  starting transfers between devices: 25.1 us -> 48.6 us
  between operations: 13.8 us -> 0.55 us
  waiting for transfers between devices: 65.5 us -> 78.2 us
  local copies, waits for them, and re-layouts: 14.6 us -> 23.2 us
    ppermute x0 -> x7, waiting for transfers between devices: none -> 37.3 us  [shards(): blocks.append(lax.ppermute(local_rows, 'sys', perm=pairs))]
    ppermute x0 -> x7, starting transfers between devices: none -> 25.2 us  [shards(): blocks.append(lax.ppermute(local_rows, 'sys', perm=pairs))]
    all_to_all x1, waiting for transfers between devices: 35.2 us -> 12.9 us  [shards(): lax.all_to_all(outgoing, 'rc', split_axis=0, concat_axis=0, tiled=True)]
    unnamed x35 -> x42, local copies, waits for them, and re-layouts: 5.32 us -> 13 us
    all_to_all x1, starting transfers between devices: 20.3 us -> 16 us  [shards(): lax.all_to_all(outgoing, 'rc', split_axis=0, concat_axis=0, tiled=True)]
    all_to_all x1, starting transfers between devices: 4.81 us -> 7.4 us  [shards(): lax.all_to_all(summed, 'rc', split_axis=0, concat_axis=0, tiled=True)]
    all_to_all x1, waiting for transfers between devices: 30.3 us -> 28 us  [shards(): lax.all_to_all(summed, 'rc', split_axis=0, concat_axis=0, tiled=True)]
  transfers between devices with their start and end apart: 3 -> 9, of which waited for: 2 -> 5; matrix products, arithmetic and copies ran while one was open for 12% -> 10% of each run, Pallas kernels for 0% -> 0%
where the time goes in v6:
time: 158 us; the launch traced here: 157 us
  waiting for transfers between devices  78.2 us (49%)
  starting transfers between devices  48.6 us (31%)
  local copies, waits for them, and re-layouts  23.2 us (15%)
  matrix products  3.37 us (2%)
  other arithmetic  2.7 us (2%)
    ppermute x7, waiting for transfers between devices, shards(): blocks.append(lax.ppermute(local_rows, 'sys', perm=pairs))  37.3 us
    all_to_all x1, waiting for transfers between devices, shards(): lax.all_to_all(summed, 'rc', split_axis=0, concat_axis=0, tiled=True)  28 us
    ppermute x7, starting transfers between devices, shards(): blocks.append(lax.ppermute(local_rows, 'sys', perm=pairs))  25.2 us
    all_to_all x1, starting transfers between devices, shards(): lax.all_to_all(outgoing, 'rc', split_axis=0, concat_axis=0, tiled=True)  16 us
    unnamed x42, local copies, waits for them, and re-layouts  13 us
    all_to_all x1, waiting for transfers between devices, shards(): lax.all_to_all(outgoing, 'rc', split_axis=0, concat_axis=0, tiled=True)  12.9 us
    all_to_all x1, starting transfers between devices, shards(): lax.all_to_all(summed, 'rc', split_axis=0, concat_axis=0, tiled=True)  7.4 us
  transfers between devices with their start and end apart: 9, of which 5 were waited for; matrix products, arithmetic and copies ran while one was open for 10% of the time, Pallas kernels for 0%

profile of v6, /device:TPU:32, one launch (start us, length us, event | category | flops | bytes accessed | tf_op | source)
XLA Modules:
  0.0 156.6 jit_solution(16655578056582049584)
XLA Ops:
  0.0 1.3 copy.75
  2.3 2.1 %collective-permute-start = (bf16[16,12800]{1,0:T(8,128)(2,1)}, bf16[16,12800]{1,0:T(8,128)(2,1)}, u32[]{:S(2)}, u32[]{:S(2)}) collective-permute-start(bf16[16,12800]{1,0:T(8,128)(2,1)} %reshape.144), channel_id=1, source_target_pairs={{0,1},{1,2},{2,3},{3,4},{4,5},{5,6},{6,7},{7,0},{8,9},{9,10},{10,1... | collective-permute-start | bytes 1228808 | tf_op jit(solution)/shard_map/ppermute | solution.py:64
  4.4 3.8 %collective-permute-start.1 = (bf16[16,12800]{1,0:T(8,128)(2,1)}, bf16[16,12800]{1,0:T(8,128)(2,1)}, u32[]{:S(2)}, u32[]{:S(2)}) collective-permute-start(bf16[16,12800]{1,0:T(8,128)(2,1)} %reshape.144), channel_id=1, source_target_pairs={{0,2},{1,3},{2,4},{3,5},{4,6},{5,7},{6,0},{7,1},{8,10},{9,11},{10,... | collective-permute-start | bytes 1228808 | tf_op jit(solution)/shard_map/ppermute | solution.py:64
  8.2 7.8 %collective-permute-start.2 = (bf16[16,12800]{1,0:T(8,128)(2,1)}, bf16[16,12800]{1,0:T(8,128)(2,1)}, u32[]{:S(2)}, u32[]{:S(2)}) collective-permute-start(bf16[16,12800]{1,0:T(8,128)(2,1)} %reshape.144), channel_id=1, source_target_pairs={{0,3},{1,4},{2,5},{3,6},{4,7},{5,0},{6,1},{7,2},{8,11},{9,12},{10,... | collective-permute-start | bytes 1228808 | tf_op jit(solution)/shard_map/ppermute | solution.py:64
  16.0 1.9 %collective-permute-start.3 = (bf16[16,12800]{1,0:T(8,128)(2,1)}, bf16[16,12800]{1,0:T(8,128)(2,1)}, u32[]{:S(2)}, u32[]{:S(2)}) collective-permute-start(bf16[16,12800]{1,0:T(8,128)(2,1)} %reshape.144), channel_id=1, source_target_pairs={{0,4},{1,5},{2,6},{3,7},{4,0},{5,1},{6,2},{7,3},{8,12},{9,13},{10,... | collective-permute-start | bytes 1228808 | tf_op jit(solution)/shard_map/ppermute | solution.py:64
  18.0 4.3 %collective-permute-start.4 = (bf16[16,12800]{1,0:T(8,128)(2,1)}, bf16[16,12800]{1,0:T(8,128)(2,1)}, u32[]{:S(2)}, u32[]{:S(2)}) collective-permute-start(bf16[16,12800]{1,0:T(8,128)(2,1)} %reshape.144), channel_id=1, source_target_pairs={{0,5},{1,6},{2,7},{3,0},{4,1},{5,2},{6,3},{7,4},{8,13},{9,14},{10,... | collective-permute-start | bytes 1228808 | tf_op jit(solution)/shard_map/ppermute | solution.py:64
  22.2 1.6 reshape.145
  24.7 1.3 reshape.158
  26.0 16.0 %all-to-all-start = ((bf16[64,2,1600]{2,1,0:T(2,128)(2,1)}), bf16[64,2,1600]{2,1,0:T(2,128)(2,1)}, u32[]{:S(2)}, u32[]{:S(2)}) async-start(bf16[64,2,1600]{2,1,0:T(2,128)(2,1)} %reshape.158), calls=%async_computation | async-start | bytes 851968 | tf_op jit(solution)/shard_map/all_to_all | solution.py:85
  47.7 2.0 %collective-permute-start.5 = (bf16[16,12800]{1,0:T(8,128)(2,1)}, bf16[16,12800]{1,0:T(8,128)(2,1)S(1)}, u32[]{:S(2)}, u32[]{:S(2)}) collective-permute-start(bf16[16,12800]{1,0:T(8,128)(2,1)} %reshape.144), channel_id=1, source_target_pairs={{0,6},{1,7},{2,0},{3,1},{4,2},{5,3},{6,4},{7,5},{8,14},{9,15},{10,... | collective-permute-start | bytes 1228808 | tf_op jit(solution)/shard_map/ppermute | solution.py:64
  49.7 1.0 constant_dynamic-update-slice_fusion.6
  50.8 3.2 %collective-permute-start.6 = (bf16[16,12800]{1,0:T(8,128)(2,1)}, bf16[16,12800]{1,0:T(8,128)(2,1)S(1)}, u32[]{:S(2)}, u32[]{:S(2)}) collective-permute-start(bf16[16,12800]{1,0:T(8,128)(2,1)} %reshape.144), channel_id=1, source_target_pairs={{0,7},{1,0},{2,1},{3,2},{4,3},{5,4},{6,5},{7,6},{8,15},{9,8},{10,9... | collective-permute-start | bytes 1228808 | tf_op jit(solution)/shard_map/ppermute | solution.py:64
  54.0 1.0 constant_dynamic-update-slice_fusion.5
  55.1 23.2 %collective-permute-done.2 = bf16[16,12800]{1,0:T(8,128)(2,1)} collective-permute-done((bf16[16,12800]{1,0:T(8,128)(2,1)}, bf16[16,12800]{1,0:T(8,128)(2,1)}, u32[]{:S(2)}, u32[]{:S(2)}) %collective-permute-start.2) | collective-permute-done | bytes 409632 | tf_op jit(solution)/shard_map/ppermute | solution.py:64
  79.3 7.7 %collective-permute-done.3 = bf16[16,12800]{1,0:T(8,128)(2,1)} collective-permute-done((bf16[16,12800]{1,0:T(8,128)(2,1)}, bf16[16,12800]{1,0:T(8,128)(2,1)}, u32[]{:S(2)}, u32[]{:S(2)}) %collective-permute-start.3) | collective-permute-done | bytes 409632 | tf_op jit(solution)/shard_map/ppermute | solution.py:64
  88.1 6.3 %collective-permute-done.4 = bf16[16,12800]{1,0:T(8,128)(2,1)} collective-permute-done((bf16[16,12800]{1,0:T(8,128)(2,1)}, bf16[16,12800]{1,0:T(8,128)(2,1)}, u32[]{:S(2)}, u32[]{:S(2)}) %collective-permute-start.4) | collective-permute-done | bytes 409632 | tf_op jit(solution)/shard_map/ppermute | solution.py:64
  95.5 1.4 fusion.1
  97.0 12.9 %all-to-all-done = bf16[64,2,1600]{2,1,0:T(2,128)(2,1)} async-done(((bf16[64,2,1600]{2,1,0:T(2,128)(2,1)}), bf16[64,2,1600]{2,1,0:T(2,128)(2,1)}, u32[]{:S(2)}, u32[]{:S(2)}) %all-to-all-start) | async-done | bytes 409632 | tf_op jit(solution)/shard_map/all_to_all | solution.py:85
  109.8 2.6 %reshape.159 = bf16[64,25,2,64]{3,2,1,0:T(2,128)(2,1)S(1)} reshape(bf16[64,2,1600]{2,1,0:T(2,128)(2,1)} %all-to-all-done) | data formatting | bytes 819200
  113.7 1.1 fusion.2
  115.2 1.3 reshape.160
  116.6 7.4 %all-to-all-start.1 = ((bf16[64,2,1600]{2,1,0:T(2,128)(2,1)}), bf16[64,2,1600]{2,1,0:T(2,128)(2,1)S(1)}, u32[]{:S(2)}, u32[]{:S(2)}) async-start(bf16[64,2,1600]{2,1,0:T(2,128)(2,1)} %reshape.160), calls=%async_computation.1 | async-start | bytes 851968 | tf_op jit(solution)/shard_map/all_to_all | solution.py:103
  124.0 28.0 %all-to-all-done.1 = bf16[64,2,1600]{2,1,0:T(2,128)(2,1)S(1)} async-done(((bf16[64,2,1600]{2,1,0:T(2,128)(2,1)}), bf16[64,2,1600]{2,1,0:T(2,128)(2,1)S(1)}, u32[]{:S(2)}, u32[]{:S(2)}) %all-to-all-start.1) | async-done | bytes 409632 | tf_op jit(solution)/shard_map/all_to_all | solution.py:103
  153.4 1.3 fusion.40
  (92 shorter events, 15.2 us)
Async XLA Ops:
  1.3 41.7 %copy-start.2 = (bf16[64,64]{1,0:T(8,128)(2,1)S(1)}, bf16[64,64]{1,0:T(8,128)(2,1)}, u32[]{:S(2)}) copy-start(bf16[64,64]{1,0:T(8,128)(2,1)} %param.14) | copy-start | bytes 24580
  1.3 41.9 %copy-start.4 = (bf16[64,64]{1,0:T(8,128)(2,1)S(1)}, bf16[64,64]{1,0:T(8,128)(2,1)}, u32[]{:S(2)}) copy-start(bf16[64,64]{1,0:T(8,128)(2,1)} %param.13) | copy-start | bytes 24580
  2.3 42.6 %copy-start.3 = (bf16[40,40]{1,0:T(8,128)(2,1)S(1)}, bf16[40,40]{1,0:T(8,128)(2,1)}, u32[]{:S(2)}) copy-start(bf16[40,40]{1,0:T(8,128)(2,1)} %param.18) | copy-start | bytes 9604
  2.3 42.7 %copy-start.5 = (bf16[40,40]{1,0:T(8,128)(2,1)S(1)}, bf16[40,40]{1,0:T(8,128)(2,1)}, u32[]{:S(2)}) copy-start(bf16[40,40]{1,0:T(8,128)(2,1)} %param.17) | copy-start | bytes 9604
  2.3 42.8 %copy-start.6 = (bf16[40,40]{1,0:T(8,128)(2,1)S(1)}, bf16[40,40]{1,0:T(8,128)(2,1)}, u32[]{:S(2)}) copy-start(bf16[40,40]{1,0:T(8,128)(2,1)} %param.16) | copy-start | bytes 9604
  2.3 43.0 %copy-start.7 = (bf16[40,40]{1,0:T(8,128)(2,1)S(1)}, bf16[40,40]{1,0:T(8,128)(2,1)}, u32[]{:S(2)}) copy-start(bf16[40,40]{1,0:T(8,128)(2,1)} %param.15) | copy-start | bytes 9604
  2.3 43.2 %copy-start.9 = (f32[64]{0:T(128)S(1)}, f32[64]{0:T(128)}, u32[]{:S(2)}) copy-start(f32[64]{0:T(128)} %param.20) | copy-start | bytes 772
  2.3 43.8 %copy-start.10 = (f32[64]{0:T(128)S(1)}, f32[64]{0:T(128)}, u32[]{:S(2)}) copy-start(f32[64]{0:T(128)} %param.19) | copy-start | bytes 772
  2.3 45.4 %collective-permute-start = (bf16[16,12800]{1,0:T(8,128)(2,1)}, bf16[16,12800]{1,0:T(8,128)(2,1)}, u32[]{:S(2)}, u32[]{:S(2)}) collective-permute-start(bf16[16,12800]{1,0:T(8,128)(2,1)} %reshape.144), channel_id=1, source_target_pairs={{0,1},{1,2},{2,3},{3,4},{4,5},{5,6},{6,7},{7,0},{8,9},{9,10},{10,1... | collective-permute-start | bytes 1228808 | tf_op jit(solution)/shard_map/ppermute | solution.py:64
  4.4 46.4 %collective-permute-start.1 = (bf16[16,12800]{1,0:T(8,128)(2,1)}, bf16[16,12800]{1,0:T(8,128)(2,1)}, u32[]{:S(2)}, u32[]{:S(2)}) collective-permute-start(bf16[16,12800]{1,0:T(8,128)(2,1)} %reshape.144), channel_id=1, source_target_pairs={{0,2},{1,3},{2,4},{3,5},{4,6},{5,7},{6,0},{7,1},{8,10},{9,11},{10,... | collective-permute-start | bytes 1228808 | tf_op jit(solution)/shard_map/ppermute | solution.py:64
  8.2 70.1 %collective-permute-start.2 = (bf16[16,12800]{1,0:T(8,128)(2,1)}, bf16[16,12800]{1,0:T(8,128)(2,1)}, u32[]{:S(2)}, u32[]{:S(2)}) collective-permute-start(bf16[16,12800]{1,0:T(8,128)(2,1)} %reshape.144), channel_id=1, source_target_pairs={{0,3},{1,4},{2,5},{3,6},{4,7},{5,0},{6,1},{7,2},{8,11},{9,12},{10,... | collective-permute-start | bytes 1228808 | tf_op jit(solution)/shard_map/ppermute | solution.py:64
  16.0 71.0 %collective-permute-start.3 = (bf16[16,12800]{1,0:T(8,128)(2,1)}, bf16[16,12800]{1,0:T(8,128)(2,1)}, u32[]{:S(2)}, u32[]{:S(2)}) collective-permute-start(bf16[16,12800]{1,0:T(8,128)(2,1)} %reshape.144), channel_id=1, source_target_pairs={{0,4},{1,5},{2,6},{3,7},{4,0},{5,1},{6,2},{7,3},{8,12},{9,13},{10,... | collective-permute-start | bytes 1228808 | tf_op jit(solution)/shard_map/ppermute | solution.py:64
  18.0 76.4 %collective-permute-start.4 = (bf16[16,12800]{1,0:T(8,128)(2,1)}, bf16[16,12800]{1,0:T(8,128)(2,1)}, u32[]{:S(2)}, u32[]{:S(2)}) collective-permute-start(bf16[16,12800]{1,0:T(8,128)(2,1)} %reshape.144), channel_id=1, source_target_pairs={{0,5},{1,6},{2,7},{3,0},{4,1},{5,2},{6,3},{7,4},{8,13},{9,14},{10,... | collective-permute-start | bytes 1228808 | tf_op jit(solution)/shard_map/ppermute | solution.py:64
  23.8 22.9 %copy-start.11 = (f32[40]{0:T(128)S(1)}, f32[40]{0:T(128)}, u32[]{:S(2)}) copy-start(f32[40]{0:T(128)} %param.21) | copy-start | bytes 484
  23.8 23.1 %copy-start.12 = (f32[40]{0:T(128)S(1)}, f32[40]{0:T(128)}, u32[]{:S(2)}) copy-start(f32[40]{0:T(128)} %param.22) | copy-start | bytes 484
  26.0 83.9 %all-to-all-start = ((bf16[64,2,1600]{2,1,0:T(2,128)(2,1)}), bf16[64,2,1600]{2,1,0:T(2,128)(2,1)}, u32[]{:S(2)}, u32[]{:S(2)}) async-start(bf16[64,2,1600]{2,1,0:T(2,128)(2,1)} %reshape.158), calls=%async_computation | async-start | bytes 851968 | tf_op jit(solution)/shard_map/all_to_all | solution.py:85
  47.7 47.7 %collective-permute-start.5 = (bf16[16,12800]{1,0:T(8,128)(2,1)}, bf16[16,12800]{1,0:T(8,128)(2,1)S(1)}, u32[]{:S(2)}, u32[]{:S(2)}) collective-permute-start(bf16[16,12800]{1,0:T(8,128)(2,1)} %reshape.144), channel_id=1, source_target_pairs={{0,6},{1,7},{2,0},{3,1},{4,2},{5,3},{6,4},{7,5},{8,14},{9,15},{10,... | collective-permute-start | bytes 1228808 | tf_op jit(solution)/shard_map/ppermute | solution.py:64
  50.8 44.7 %collective-permute-start.6 = (bf16[16,12800]{1,0:T(8,128)(2,1)}, bf16[16,12800]{1,0:T(8,128)(2,1)S(1)}, u32[]{:S(2)}, u32[]{:S(2)}) collective-permute-start(bf16[16,12800]{1,0:T(8,128)(2,1)} %reshape.144), channel_id=1, source_target_pairs={{0,7},{1,0},{2,1},{3,2},{4,3},{5,4},{6,5},{7,6},{8,15},{9,8},{10,9... | collective-permute-start | bytes 1228808 | tf_op jit(solution)/shard_map/ppermute | solution.py:64
  112.9 11.1 %copy-start.1 = (f32[16,12800]{1,0:T(8,128)S(1)}, f32[16,12800]{1,0:T(8,128)}, u32[]{:S(2)}) copy-start(f32[16,12800]{1,0:T(8,128)} %fusion.1) | copy-start | bytes 2457604
  116.6 35.5 %all-to-all-start.1 = ((bf16[64,2,1600]{2,1,0:T(2,128)(2,1)}), bf16[64,2,1600]{2,1,0:T(2,128)(2,1)S(1)}, u32[]{:S(2)}, u32[]{:S(2)}) async-start(bf16[64,2,1600]{2,1,0:T(2,128)(2,1)} %reshape.160), calls=%async_computation.1 | async-start | bytes 851968 | tf_op jit(solution)/shard_map/all_to_all | solution.py:103
  154.6 1.0 copy-start
  154.7 1.0 copy-start.8

commit v7 on v5

--- a/solution.py
+++ b/solution.py
@@ -3,7 +3,7 @@
 import jax
 import jax.numpy as jnp
 from jax import lax
-from jax.sharding import PartitionSpec as P
+from jax.sharding import Mesh, PartitionSpec as P
 
 
 def symmetric(matrix, factor):
@@ -52,29 +52,34 @@
     state_count = density.shape[1]
     pair_count = density.shape[2]
     column_total = density.shape[3]
-    first_state = lax.axis_index("sys") * state_count
+    first_state = lax.axis_index(("zl", "core")) * state_count
     left_gain = lax.dynamic_slice_in_dim(left_strength, first_state, state_count)
     right_gain = lax.dynamic_slice_in_dim(right_strength, first_state, state_count)
     flat_local = jnp.transpose(density.reshape(2, state_count, -1), (1, 0, 2))
-    gathered = lax.all_gather(flat_local.reshape(2 * state_count, -1), "sys", axis=0, tiled=True)
+    gathered = lax.all_gather(flat_local.reshape(2 * state_count, -1), "zl", axis=0, tiled=True)
+    gathered = lax.all_gather(gathered, "core", axis=0, tiled=True)
     own_real = lax.dynamic_slice_in_dim(herm_real, first_state, state_count, axis=0)
     own_imag = lax.dynamic_slice_in_dim(herm_imag, first_state, state_count, axis=0)
     real_rows = jnp.stack([own_real, -own_imag], axis=2).reshape(state_count, -1)
     imag_rows = jnp.stack([own_imag, own_real], axis=2).reshape(state_count, -1)
     mixer = jnp.concatenate([real_rows, imag_rows], axis=0)
+    run_count = lax.axis_size("zl")
+    core_count = lax.axis_size("core")
+    mixer = mixer.reshape(2 * state_count, run_count, core_count, 2 * state_count)
+    mixer = jnp.transpose(mixer, (0, 2, 1, 3)).reshape(2 * state_count, -1)
     product = jnp.dot(mixer, gathered, preferred_element_type=jnp.float32)
     product = lax.reduce_precision(product, exponent_bits=8, mantissa_bits=7)
     system_rows = product.astype(jnp.bfloat16).reshape(density.shape)
-    rc_count = lax.axis_size("rc")
+    rc_count = lax.axis_size(("x", "y", "zh"))
     col_groups = rc_count // state_count
     group_width = column_total // col_groups
     outgoing = density.reshape(2, state_count, pair_count, col_groups, group_width)
     outgoing = jnp.transpose(outgoing, (1, 3, 2, 0, 4)).reshape(
         rc_count, pair_count, 2, group_width
     )
-    incoming = lax.all_to_all(outgoing, "rc", split_axis=0, concat_axis=0, tiled=True)
+    incoming = lax.all_to_all(outgoing, ("x", "y", "zh"), split_axis=0, concat_axis=0, tiled=True)
     rows = incoming.reshape(rc_count * pair_count, 2 * group_width).astype(jnp.float32)
-    my_state = first_state + lax.axis_index("rc") // col_groups
+    my_state = first_state + lax.axis_index(("x", "y", "zh")) // col_groups
     left_g = lax.dynamic_slice_in_dim(left_strength, my_state, 1)
     right_g = lax.dynamic_slice_in_dim(right_strength, my_state, 1)
     left_ops32 = left_ops.astype(jnp.float32)
@@ -90,10 +95,10 @@
         "ayb,abn->ayn", right_mats, cube, precision=lax.Precision.HIGHEST
     ).reshape(rows.shape)
     summed = (left_out + right_out).astype(jnp.bfloat16).reshape(outgoing.shape)
-    returned = lax.all_to_all(summed, "rc", split_axis=0, concat_axis=0, tiled=True)
+    returned = lax.all_to_all(summed, ("x", "y", "zh"), split_axis=0, concat_axis=0, tiled=True)
     returned = returned.reshape(state_count, col_groups, pair_count, 2, group_width)
     ladder_rows = jnp.transpose(returned, (3, 0, 2, 1, 4)).reshape(density.shape)
-    pair_index = lax.axis_index("rc") * pair_count + jnp.arange(pair_count, dtype=jnp.int32)
+    pair_index = lax.axis_index(("x", "y", "zh")) * pair_count + jnp.arange(pair_count, dtype=jnp.int32)
     level_index = jnp.arange(levels, dtype=jnp.int32)
     left_pick = (pair_index[:, None] // levels == level_index[None, :]).astype(jnp.float32)
     right_pick = (pair_index[:, None] % levels == level_index[None, :]).astype(jnp.float32)
@@ -113,7 +118,8 @@
 
 
 def solution(mesh):
-    placed = (P(None, "sys", "rc", None), P(), P(), P(), P(), P(), P(), P(), P(), P(), P(), P())
-    return jax.shard_map(
-        shards, mesh=mesh, in_specs=placed, out_specs=P(None, "sys", "rc", None), check_vma=False
-    )
+    devices = mesh.devices.reshape(4, 4, 4, 4, 2)
+    split = Mesh(devices, ("x", "y", "zh", "zl", "core"))
+    block = P(None, ("zl", "core"), ("x", "y", "zh"), None)
+    placed = (block, P(), P(), P(), P(), P(), P(), P(), P(), P(), P(), P())
+    return jax.shard_map(shards, mesh=split, in_specs=placed, out_specs=block, check_vma=False)

time: 126 us -> 149 us (1.18)
  starting transfers between devices: 25.1 us -> 36.7 us
  waiting for transfers between devices: 65.5 us -> 77.1 us
    all_gather x1 -> x2, waiting for transfers between devices: 0.02 us -> 45.2 us  [the longest x1 45.2 us: shards(): lax.all_gather(flat_local.reshape(2 * state_count, -1), 'zl', axis=0, til...]
    all_to_all x2, waiting for transfers between devices: 65.5 us -> 31.9 us  [the longest x1 31.9 us: shards(): lax.all_to_all(summed, ('x', 'y', 'zh'), split_axis=0, concat_axis=0, til...]
    all_to_all x2, starting transfers between devices: 25.1 us -> 36.6 us  [the longest x1 20.3 us: shards(): lax.all_to_all(outgoing, ('x', 'y', 'zh'), split_axis=0, concat_axis=0, t...]
  transfers between devices with their start and end apart: 3 -> 4, of which waited for: 2 -> 2; matrix products, arithmetic and copies ran while one was open for 12% -> 10% of each run, Pallas kernels for 0% -> 0%
where the time goes in v7:
time: 149 us
  waiting for transfers between devices  77.1 us (52%)
  starting transfers between devices  36.7 us (25%)
  local copies, waits for them, and re-layouts  14.7 us (10%)
  between operations  13.9 us (9%)
  matrix products  4.42 us (3%)
  other arithmetic  2.08 us (1%)
    all_gather x1, waiting for transfers between devices, shards(): lax.all_gather(flat_local.reshape(2 * state_count, -1), 'zl', axis=0, til...  45.2 us
    all_to_all x1, waiting for transfers between devices, shards(): lax.all_to_all(summed, ('x', 'y', 'zh'), split_axis=0, concat_axis=0, til...  31.9 us
    all_to_all x1, starting transfers between devices, shards(): lax.all_to_all(outgoing, ('x', 'y', 'zh'), split_axis=0, concat_axis=0, t...  20.3 us
    all_to_all x1, starting transfers between devices, shards(): lax.all_to_all(summed, ('x', 'y', 'zh'), split_axis=0, concat_axis=0, til...  16.3 us
    unnamed x35, local copies, waits for them, and re-layouts  5.35 us
  transfers between devices with their start and end apart: 4, of which 2 were waited for; matrix products, arithmetic and copies ran while one was open for 10% of the time, Pallas kernels for 0%

profile of v7, /device:TPU:32, one launch (start us, length us, event | category | flops | bytes accessed | tf_op | source)
XLA Modules:
  0.0 148.8 jit_solution(8717922347915073786)
XLA Ops:
  6.5 1.3 copy.70
  7.9 0.9 reshape.91
  8.9 1.6 %reshape.92 = bf16[2,8,25,8,64]{4,3,1,2,0:T(8,128)(2,1)S(1)} reshape(bf16[2,8,25,512]{3,1,2,0:T(8,128)(2,1)} %param.12) | data formatting | bytes 819200 | tf_op jit(solution)/shard_map/reshape | solution.py:76
  10.4 0.8 copy.75
  11.3 1.3 reshape.97
  12.6 20.3 %all-to-all-start = ((bf16[64,2,1600]{2,1,0:T(2,128)(2,1)}), bf16[64,2,1600]{2,1,0:T(2,128)(2,1)S(1)}, u32[]{:S(2)}, u32[]{:S(2)}) async-start(bf16[64,2,1600]{2,1,0:T(2,128)(2,1)} %reshape.97), calls=%async_computation | async-start | bytes 851968 | tf_op jit(solution)/shard_map/all_to_all | solution.py:80
  33.6 45.2 %all-gather.3.cloned.1.call-done = bf16[64,12800]{1,0:T(8,128)(2,1)} async-done(((bf16[16,12800]{1,0:T(8,128)(2,1)}), bf16[64,12800]{1,0:T(8,128)(2,1)}) %all-gather.3.cloned.1.call-update) | async-done | bytes 1638416 | tf_op jit(solution)/shard_map/all_gather | solution.py:59
  79.1 0.6 dynamic_slice.15
  79.7 0.6 dynamic_slice.14
  80.3 0.7 fusion.12
  81.0 0.7 reshape.98
  81.7 0.4 reshape.94
  82.1 0.8 fusion.10
  82.9 1.2 fusion.2
  84.1 0.3 convert_element_type.97
  84.5 1.3 reshape.99
  85.8 16.3 %all-to-all-start.1 = ((bf16[64,2,1600]{2,1,0:T(2,128)(2,1)}), bf16[64,2,1600]{2,1,0:T(2,128)(2,1)S(1)}, u32[]{:S(2)}, u32[]{:S(2)}) async-start(bf16[64,2,1600]{2,1,0:T(2,128)(2,1)} %reshape.99), calls=%async_computation.1 | async-start | bytes 851968 | tf_op jit(solution)/shard_map/all_to_all | solution.py:98
  103.2 31.9 %all-to-all-done.1 = bf16[64,2,1600]{2,1,0:T(2,128)(2,1)S(1)} async-done(((bf16[64,2,1600]{2,1,0:T(2,128)(2,1)}), bf16[64,2,1600]{2,1,0:T(2,128)(2,1)S(1)}, u32[]{:S(2)}, u32[]{:S(2)}) %all-to-all-start.1) | async-done | bytes 409632 | tf_op jit(solution)/shard_map/all_to_all | solution.py:98
  135.2 0.7 reshape.100
  135.9 0.6 convert_bitcast_fusion
  136.5 1.3 fusion.33
  138.4 2.5 %fusion.1 = f32[16,12800]{1,0:T(8,128)S(1)} fusion(bf16[16,128]{1,0:T(8,128)(2,1)S(1)} %reshape.89, bf16[128,12800]{1,0:T(8,128)(2,1)} %all-gather.5.cloned.1.call-done), kind=kOutput, calls=%fused_computation.2 | convolution fusion | flops 53043200 | bytes 4100096 | tf_op jit(solution)/shard_map/dot_general | solution.py:70
  141.0 0.2 fusion.5
  141.2 0.7 copy-done.8
  (68 shorter events, 2.8 us)
Async XLA Ops:
  6.5 72.3 %all-gather.3.cloned.1.call-start = ((), (), s32[]{:S(2)}) async-start(), calls=%async_computation.2 | async-start | bytes 2048000 | tf_op jit(solution)/shard_map/all_gather | solution.py:59
  7.9 25.1 %copy-start.2 = (bf16[40,40]{1,0:T(8,128)(2,1)S(1)}, bf16[40,40]{1,0:T(8,128)(2,1)}, u32[]{:S(2)}) copy-start(bf16[40,40]{1,0:T(8,128)(2,1)} %param.18) | copy-start | bytes 9604
  7.9 25.2 %copy-start.4 = (bf16[40,40]{1,0:T(8,128)(2,1)S(1)}, bf16[40,40]{1,0:T(8,128)(2,1)}, u32[]{:S(2)}) copy-start(bf16[40,40]{1,0:T(8,128)(2,1)} %param.17) | copy-start | bytes 9604
  7.9 25.3 %copy-start.5 = (bf16[40,40]{1,0:T(8,128)(2,1)S(1)}, bf16[40,40]{1,0:T(8,128)(2,1)}, u32[]{:S(2)}) copy-start(bf16[40,40]{1,0:T(8,128)(2,1)} %param.16) | copy-start | bytes 9604
  7.9 25.5 %copy-start.6 = (bf16[40,40]{1,0:T(8,128)(2,1)S(1)}, bf16[40,40]{1,0:T(8,128)(2,1)}, u32[]{:S(2)}) copy-start(bf16[40,40]{1,0:T(8,128)(2,1)} %param.15) | copy-start | bytes 9604
  8.8 70.0 %copy-start.1 = (bf16[64,64]{1,0:T(8,128)(2,1)S(1)}, bf16[64,64]{1,0:T(8,128)(2,1)}, u32[]{:S(2)}) copy-start(bf16[64,64]{1,0:T(8,128)(2,1)} %param.14) | copy-start | bytes 24580
  8.8 70.1 %copy-start.3 = (bf16[64,64]{1,0:T(8,128)(2,1)S(1)}, bf16[64,64]{1,0:T(8,128)(2,1)}, u32[]{:S(2)}) copy-start(bf16[64,64]{1,0:T(8,128)(2,1)} %param.13) | copy-start | bytes 24580
  10.4 68.7 %copy-start.9 = (f32[64]{0:T(128)S(1)}, f32[64]{0:T(128)}, u32[]{:S(2)}) copy-start(f32[64]{0:T(128)} %param.20) | copy-start | bytes 772
  10.4 69.3 %copy-start.10 = (f32[64]{0:T(128)S(1)}, f32[64]{0:T(128)}, u32[]{:S(2)}) copy-start(f32[64]{0:T(128)} %param.19) | copy-start | bytes 772
  12.6 68.3 %all-to-all-start = ((bf16[64,2,1600]{2,1,0:T(2,128)(2,1)}), bf16[64,2,1600]{2,1,0:T(2,128)(2,1)S(1)}, u32[]{:S(2)}, u32[]{:S(2)}) async-start(bf16[64,2,1600]{2,1,0:T(2,128)(2,1)} %reshape.97), calls=%async_computation | async-start | bytes 851968 | tf_op jit(solution)/shard_map/all_to_all | solution.py:80
  32.9 105.5 %all-gather.5.cloned.1.call-start = ((), (), s32[]{:S(2)}) async-start(), calls=%async_computation.3 | async-start | bytes 4915200 | tf_op jit(solution)/shard_map/all_gather | solution.py:60
  82.9 20.0 %copy-start.11 = (f32[40]{0:T(128)S(1)}, f32[40]{0:T(128)}, u32[]{:S(2)}) copy-start(f32[40]{0:T(128)} %param.21) | copy-start | bytes 484
  82.9 20.2 %copy-start.12 = (f32[40]{0:T(128)S(1)}, f32[40]{0:T(128)}, u32[]{:S(2)}) copy-start(f32[40]{0:T(128)} %param.22) | copy-start | bytes 484
  85.8 49.4 %all-to-all-start.1 = ((bf16[64,2,1600]{2,1,0:T(2,128)(2,1)}), bf16[64,2,1600]{2,1,0:T(2,128)(2,1)S(1)}, u32[]{:S(2)}, u32[]{:S(2)}) async-start(bf16[64,2,1600]{2,1,0:T(2,128)(2,1)} %reshape.99), calls=%async_computation.1 | async-start | bytes 851968 | tf_op jit(solution)/shard_map/all_to_all | solution.py:98
  138.2 2.8 %copy-start = (bf16[2,8,25,512]{3,1,2,0:T(8,128)(2,1)S(1)}, bf16[2,8,25,512]{3,1,2,0:T(8,128)(2,1)}, u32[]{:S(2)}) copy-start(bf16[2,8,25,512]{3,1,2,0:T(8,128)(2,1)} %param.12) | copy-start | bytes 1228804
  138.2 2.8 %copy-start.7 = (f32[512]{0:T(512)S(1)}, f32[512]{0:T(512)}, u32[]{:S(2)}) copy-start(f32[512]{0:T(512)} %param.23) | copy-start | bytes 6148
  141.2 0.8 copy-start.8
Sparse Core Ops, SparseCore 0:
  9.5 69.2 all-gather.2
  80.9 23.1 all-gather.4

commit v8 on v5

--- a/solution.py
+++ b/solution.py
@@ -55,14 +55,21 @@
     first_state = lax.axis_index("sys") * state_count
     left_gain = lax.dynamic_slice_in_dim(left_strength, first_state, state_count)
     right_gain = lax.dynamic_slice_in_dim(right_strength, first_state, state_count)
-    flat_local = jnp.transpose(density.reshape(2, state_count, -1), (1, 0, 2))
-    gathered = lax.all_gather(flat_local.reshape(2 * state_count, -1), "sys", axis=0, tiled=True)
+    gathered = lax.all_gather(density, "sys", axis=0, tiled=False)
+    sys_count = gathered.shape[0]
     own_real = lax.dynamic_slice_in_dim(herm_real, first_state, state_count, axis=0)
     own_imag = lax.dynamic_slice_in_dim(herm_imag, first_state, state_count, axis=0)
-    real_rows = jnp.stack([own_real, -own_imag], axis=2).reshape(state_count, -1)
-    imag_rows = jnp.stack([own_imag, own_real], axis=2).reshape(state_count, -1)
-    mixer = jnp.concatenate([real_rows, imag_rows], axis=0)
-    product = jnp.dot(mixer, gathered, preferred_element_type=jnp.float32)
+    real3 = own_real.reshape(state_count, sys_count, state_count)
+    imag3 = own_imag.reshape(state_count, sys_count, state_count)
+    mixer = jnp.stack(
+        [jnp.stack([real3, -imag3], axis=2), jnp.stack([imag3, real3], axis=2)], axis=0
+    ).reshape(2 * state_count, -1)
+    product = jnp.einsum(
+        "ok,kjc->ojc",
+        mixer,
+        gathered.reshape(-1, pair_count, column_total),
+        preferred_element_type=jnp.float32,
+    )
     product = lax.reduce_precision(product, exponent_bits=8, mantissa_bits=7)
     system_rows = product.astype(jnp.bfloat16).reshape(density.shape)
     rc_count = lax.axis_size("rc")

time: 126 us -> 124 us (0.984)
  local copies, waits for them, and re-layouts: 14.6 us -> 10.6 us
  waiting for transfers between devices: 65.5 us -> 67.9 us
    all_to_all x1, waiting for transfers between devices: 30.3 us -> 32.1 us  [shards(): lax.all_to_all(summed, 'rc', split_axis=0, concat_axis=0, tiled=True)]
    transpose x1 -> x0, local copies, waits for them, and re-layouts: 1.32 us -> none  [shards(): flat_local = jnp.transpose(density.reshape(2, state_count, -1), (1, 0, 2))]
    unnamed x35 -> x33, local copies, waits for them, and re-layouts: 5.32 us -> 4.52 us
  transfers between devices with their start and end apart: 3 -> 3, of which waited for: 2 -> 2; matrix products, arithmetic and copies ran while one was open for 12% -> 11% of each run, Pallas kernels for 0% -> 0%
where the time goes in v8:
time: 124 us
  waiting for transfers between devices  67.9 us (55%)
  starting transfers between devices  25 us (20%)
  between operations  13.8 us (11%)
  local copies, waits for them, and re-layouts  10.6 us (9%)
  matrix products  4.49 us (4%)
  other arithmetic  2.2 us (2%)
    all_to_all x1, waiting for transfers between devices, shards(): lax.all_to_all(outgoing, 'rc', split_axis=0, concat_axis=0, tiled=True)  35.1 us
    all_to_all x1, waiting for transfers between devices, shards(): lax.all_to_all(summed, 'rc', split_axis=0, concat_axis=0, tiled=True)  32.1 us
    all_to_all x1, starting transfers between devices, shards(): lax.all_to_all(outgoing, 'rc', split_axis=0, concat_axis=0, tiled=True)  20.3 us
    all_to_all x1, starting transfers between devices, shards(): lax.all_to_all(summed, 'rc', split_axis=0, concat_axis=0, tiled=True)  4.63 us
    unnamed x33, local copies, waits for them, and re-layouts  4.52 us
  transfers between devices with their start and end apart: 3, of which 2 were waited for; matrix products, arithmetic and copies ran while one was open for 11% of the time, Pallas kernels for 0%

profile of v8, /device:TPU:32, one launch (start us, length us, event | category | flops | bytes accessed | tf_op | source)
XLA Modules:
  0.0 123.9 jit_solution(16356831016003973525)
XLA Ops:
  6.6 0.7 all-gather.3.cloned.1.call-update
  7.3 1.6 %reshape.95 = bf16[2,8,25,8,64]{4,3,1,2,0:T(8,128)(2,1)S(1)} reshape(bf16[2,8,25,512]{3,1,2,0:T(8,128)(2,1)} %param.12) | data formatting | bytes 819200 | tf_op jit(solution)/shard_map/reshape | solution.py:78
  8.9 0.8 copy.69
  9.7 1.3 %reshape.104 = bf16[64,2,1600]{2,1,0:T(2,128)(2,1)} reshape(bf16[64,25,2,64]{3,2,1,0:T(2,128)(2,1)S(1)} %bitcast.80) | data formatting | bytes 819200
  11.0 20.3 %all-to-all-start = ((bf16[64,2,1600]{2,1,0:T(2,128)(2,1)}), bf16[64,2,1600]{2,1,0:T(2,128)(2,1)S(1)}, u32[]{:S(2)}, u32[]{:S(2)}) async-start(bf16[64,2,1600]{2,1,0:T(2,128)(2,1)} %reshape.104), calls=%async_computation | async-start | bytes 851968 | tf_op jit(solution)/shard_map/all_to_all | solution.py:82
  31.3 0.6 dynamic_slice.15
  31.9 0.6 dynamic_slice.14
  33.3 0.7 fusion.25
  33.9 35.1 %all-to-all-done = bf16[64,2,1600]{2,1,0:T(2,128)(2,1)S(1)} async-done(((bf16[64,2,1600]{2,1,0:T(2,128)(2,1)}), bf16[64,2,1600]{2,1,0:T(2,128)(2,1)S(1)}, u32[]{:S(2)}, u32[]{:S(2)}) %all-to-all-start) | async-done | bytes 409632 | tf_op jit(solution)/shard_map/all_to_all | solution.py:82
  69.0 0.7 reshape.105
  69.7 0.4 reshape.97
  70.1 0.8 fusion.23
  70.9 1.2 fusion.6
  72.2 0.3 convert_element_type.97
  72.6 1.3 %reshape.106 = bf16[64,2,1600]{2,1,0:T(2,128)(2,1)} reshape(bf16[64,25,2,64]{3,2,1,0:T(2,128)(2,1)S(1)} %convert_element_type.97) | data formatting | bytes 819200
  73.9 4.6 %all-to-all-start.1 = ((bf16[64,2,1600]{2,1,0:T(2,128)(2,1)}), bf16[64,2,1600]{2,1,0:T(2,128)(2,1)S(1)}, u32[]{:S(2)}, u32[]{:S(2)}) async-start(bf16[64,2,1600]{2,1,0:T(2,128)(2,1)} %reshape.106), calls=%async_computation.1 | async-start | bytes 851968 | tf_op jit(solution)/shard_map/all_to_all | solution.py:100
  79.7 32.1 %all-to-all-done.1 = bf16[64,2,1600]{2,1,0:T(2,128)(2,1)S(1)} async-done(((bf16[64,2,1600]{2,1,0:T(2,128)(2,1)}), bf16[64,2,1600]{2,1,0:T(2,128)(2,1)S(1)}, u32[]{:S(2)}, u32[]{:S(2)}) %all-to-all-start.1) | async-done | bytes 409632 | tf_op jit(solution)/shard_map/all_to_all | solution.py:100
  111.9 0.7 reshape.107
  112.6 0.2 copy.92
  113.0 0.2 slice.47
  113.2 0.2 slice.52
  113.5 2.5 %fusion.10 = f32[16,25,512]{2,0,1:T(8,128)S(1)} fusion(bf16[16,128,1]{1,0,2:T(8,128)(2,1)S(1)} %reshape.101, bf16[16,8,25,512]{3,1,2,0:T(8,128)(2,1)} %all-gather.3.cloned.1.call-done), kind=kOutput, calls=%fused_computation.8 | convolution fusion | flops 53043200 | bytes 4100096 | tf_op jit(solution)/shard_map/ok,kjc->ojc/dot_general | solution.py:67
  116.0 0.2 fusion.15
  116.2 0.8 pad_maximum_fusion
  (58 shorter events, 2.1 us)
Async XLA Ops:
  6.5 24.8 %copy-start.8 = (f32[64]{0:T(128)S(1)}, f32[64]{0:T(128)}, u32[]{:S(2)}) copy-start(f32[64]{0:T(128)} %param.20) | copy-start | bytes 772
  6.5 25.4 %copy-start.9 = (f32[64]{0:T(128)S(1)}, f32[64]{0:T(128)}, u32[]{:S(2)}) copy-start(f32[64]{0:T(128)} %param.19) | copy-start | bytes 772
  6.5 26.0 %copy-start.4 = (bf16[40,40]{1,0:T(8,128)(2,1)S(1)}, bf16[40,40]{1,0:T(8,128)(2,1)}, u32[]{:S(2)}) copy-start(bf16[40,40]{1,0:T(8,128)(2,1)} %param.15) | copy-start | bytes 9604
  6.5 26.1 %copy-start.5 = (bf16[40,40]{1,0:T(8,128)(2,1)S(1)}, bf16[40,40]{1,0:T(8,128)(2,1)}, u32[]{:S(2)}) copy-start(bf16[40,40]{1,0:T(8,128)(2,1)} %param.16) | copy-start | bytes 9604
  6.5 26.2 %copy-start.6 = (bf16[40,40]{1,0:T(8,128)(2,1)S(1)}, bf16[40,40]{1,0:T(8,128)(2,1)}, u32[]{:S(2)}) copy-start(bf16[40,40]{1,0:T(8,128)(2,1)} %param.17) | copy-start | bytes 9604
  6.5 26.6 %copy-start.2 = (bf16[40,40]{1,0:T(8,128)(2,1)S(1)}, bf16[40,40]{1,0:T(8,128)(2,1)}, u32[]{:S(2)}) copy-start(bf16[40,40]{1,0:T(8,128)(2,1)} %param.18) | copy-start | bytes 9604
  6.6 106.9 %all-gather.3.cloned.1.call-start = ((), (), s32[]{:S(2)}) async-start(), calls=%async_computation.2 | async-start | bytes 3686400 | tf_op jit(solution)/shard_map/all_gather | solution.py:58
  11.0 58.0 %all-to-all-start = ((bf16[64,2,1600]{2,1,0:T(2,128)(2,1)}), bf16[64,2,1600]{2,1,0:T(2,128)(2,1)S(1)}, u32[]{:S(2)}, u32[]{:S(2)}) async-start(bf16[64,2,1600]{2,1,0:T(2,128)(2,1)} %reshape.104), calls=%async_computation | async-start | bytes 851968 | tf_op jit(solution)/shard_map/all_to_all | solution.py:82
  70.1 8.4 %copy-start.1 = (bf16[64,64]{1,0:T(8,128)(2,1)S(1)}, bf16[64,64]{1,0:T(8,128)(2,1)}, u32[]{:S(2)}) copy-start(bf16[64,64]{1,0:T(8,128)(2,1)} %param.14) | copy-start | bytes 24580
  70.1 8.5 %copy-start.3 = (bf16[64,64]{1,0:T(8,128)(2,1)S(1)}, bf16[64,64]{1,0:T(8,128)(2,1)}, u32[]{:S(2)}) copy-start(bf16[64,64]{1,0:T(8,128)(2,1)} %param.13) | copy-start | bytes 24580
  70.9 8.5 %copy-start.10 = (f32[40]{0:T(128)S(1)}, f32[40]{0:T(128)}, u32[]{:S(2)}) copy-start(f32[40]{0:T(128)} %param.22) | copy-start | bytes 484
  70.9 8.6 %copy-start.11 = (f32[40]{0:T(128)S(1)}, f32[40]{0:T(128)}, u32[]{:S(2)}) copy-start(f32[40]{0:T(128)} %param.21) | copy-start | bytes 484
  73.9 38.0 %all-to-all-start.1 = ((bf16[64,2,1600]{2,1,0:T(2,128)(2,1)}), bf16[64,2,1600]{2,1,0:T(2,128)(2,1)S(1)}, u32[]{:S(2)}, u32[]{:S(2)}) async-start(bf16[64,2,1600]{2,1,0:T(2,128)(2,1)} %reshape.106), calls=%async_computation.1 | async-start | bytes 851968 | tf_op jit(solution)/shard_map/all_to_all | solution.py:100
  113.0 3.0 %copy-start = (bf16[2,8,25,512]{3,1,2,0:T(8,128)(2,1)S(1)}, bf16[2,8,25,512]{3,1,2,0:T(8,128)(2,1)}, u32[]{:S(2)}) copy-start(bf16[2,8,25,512]{3,1,2,0:T(8,128)(2,1)} %param.12) | copy-start | bytes 1228804
  113.0 3.0 %copy-start.7 = (f32[512]{0:T(512)S(1)}, f32[512]{0:T(512)}, u32[]{:S(2)}) copy-start(f32[512]{0:T(512)} %param.23) | copy-start | bytes 6148
Sparse Core Ops, SparseCore 0:
  9.5 70.1 all-gather.2

commit v9 on v8

--- a/solution.py
+++ b/solution.py
@@ -79,7 +79,9 @@
     outgoing = jnp.transpose(outgoing, (1, 3, 2, 0, 4)).reshape(
         rc_count, pair_count, 2, group_width
     )
-    incoming = lax.all_to_all(outgoing, "rc", split_axis=0, concat_axis=0, tiled=True)
+    incoming = lax.all_to_all(
+        outgoing.reshape(rc_count, 2, -1), "rc", split_axis=0, concat_axis=0, tiled=True
+    )
     rows = incoming.reshape(rc_count * pair_count, 2 * group_width).astype(jnp.float32)
     my_state = first_state + lax.axis_index("rc") // col_groups
     left_g = lax.dynamic_slice_in_dim(left_strength, my_state, 1)
@@ -96,7 +98,7 @@
     right_out = jnp.einsum(
         "ayb,abn->ayn", right_mats, cube, precision=lax.Precision.HIGHEST
     ).reshape(rows.shape)
-    summed = (left_out + right_out).astype(jnp.bfloat16).reshape(outgoing.shape)
+    summed = (left_out + right_out).astype(jnp.bfloat16).reshape(rc_count, 2, -1)
     returned = lax.all_to_all(summed, "rc", split_axis=0, concat_axis=0, tiled=True)
     returned = returned.reshape(state_count, col_groups, pair_count, 2, group_width)
     ladder_rows = jnp.transpose(returned, (3, 0, 2, 1, 4)).reshape(density.shape)

time: 124 us -> 126 us (1.016)
  waiting for transfers between devices: 67.9 us -> 69.2 us
    unnamed x33 -> x29, local copies, waits for them, and re-layouts: 4.52 us -> 0.47 us
    all_to_all x1, waiting for transfers between devices: 32.1 us -> 33.5 us  [shards(): lax.all_to_all(summed, 'rc', split_axis=0, concat_axis=0, tiled=True)]
    another operation x0 -> x1, local copies, waits for them, and re-layouts: none -> 1.3 us  [shards(): outgoing.reshape(rc_count, 2, -1)]
where the time goes in v9:
time: 126 us; the launch traced here: 125 us
  waiting for transfers between devices  69.2 us (55%)
  starting transfers between devices  25 us (20%)
  between operations  13.8 us (11%)
  local copies, waits for them, and re-layouts  10.9 us (9%)
  matrix products  4.47 us (4%)
  other arithmetic  2.21 us (2%)
    all_to_all x1, waiting for transfers between devices, shards(): lax.all_to_all(outgoing.reshape(rc_count, 2, -1), 'rc', split_axis=0, con...  35 us
    all_to_all x1, waiting for transfers between devices, shards(): lax.all_to_all(summed, 'rc', split_axis=0, concat_axis=0, tiled=True)  33.5 us
    all_to_all x1, starting transfers between devices, shards(): lax.all_to_all(outgoing.reshape(rc_count, 2, -1), 'rc', split_axis=0, con...  20.3 us
    all_to_all x1, starting transfers between devices, shards(): lax.all_to_all(summed, 'rc', split_axis=0, concat_axis=0, tiled=True)  4.63 us
  transfers between devices with their start and end apart: 3, of which 2 were waited for; matrix products, arithmetic and copies ran while one was open for 11% of the time, Pallas kernels for 0%

profile of v9, /device:TPU:32, one launch (start us, length us, event | category | flops | bytes accessed | tf_op | source)
XLA Modules:
  0.0 125.5 jit_solution(227874852148182418)
XLA Ops:
  6.6 0.7 all-gather.3.cloned.1.call-update
  7.3 1.6 %reshape.92 = bf16[2,8,25,8,64]{4,3,1,2,0:T(8,128)(2,1)S(1)} reshape(bf16[2,8,25,512]{3,1,2,0:T(8,128)(2,1)} %param.12) | data formatting | bytes 819200 | tf_op jit(solution)/shard_map/reshape | solution.py:78
  8.9 0.8 copy.95
  9.7 1.3 %reshape_reshape.3 = bf16[64,2,1600]{2,1,0:T(2,128)(2,1)} reshape(bf16[8,8,25,2,64]{4,3,2,1,0:T(2,128)(2,1)S(1)} %bitcast.77) | data formatting | bytes 819200 | tf_op jit(solution)/shard_map/reshape;reshape | solution.py:83
  11.0 20.3 %all-to-all-start = ((bf16[64,2,1600]{2,1,0:T(2,128)(2,1)}), bf16[64,2,1600]{2,1,0:T(2,128)(2,1)S(1)}, u32[]{:S(2)}, u32[]{:S(2)}) async-start(bf16[64,2,1600]{2,1,0:T(2,128)(2,1)} %reshape_reshape.3), calls=%async_computation | async-start | bytes 851968 | tf_op jit(solution)/shard_map/all_to_all | solution.py:82
  31.3 0.6 dynamic_slice.15
  31.9 0.6 dynamic_slice.14
  33.3 0.7 fusion.25
  34.0 35.0 %all-to-all-done = bf16[64,2,1600]{2,1,0:T(2,128)(2,1)S(1)} async-done(((bf16[64,2,1600]{2,1,0:T(2,128)(2,1)}), bf16[64,2,1600]{2,1,0:T(2,128)(2,1)S(1)}, u32[]{:S(2)}, u32[]{:S(2)}) %all-to-all-start) | async-done | bytes 409632 | tf_op jit(solution)/shard_map/all_to_all | solution.py:82
  69.0 0.5 reshape.93
  69.5 0.8 fusion.23
  70.3 1.2 fusion.6
  71.6 1.1 convert_element_type.97
  72.7 4.6 %all-to-all-start.1 = ((bf16[64,2,1600]{2,1,0:T(2,128)(2,1)}), bf16[64,2,1600]{2,1,0:T(2,128)(2,1)S(1)}, u32[]{:S(2)}, u32[]{:S(2)}) async-start(bf16[64,2,1600]{2,1,0:T(2,128)(2,1)} %convert_element_type.97), calls=%async_computation.1 | async-start | bytes 851968 | tf_op jit(solution)/shard_map/all_to_all | solution.py:102
  78.2 0.2 select_reduce_fusion
  78.4 0.2 select_reduce_fusion.1
  78.5 33.5 %all-to-all-done.1 = bf16[64,2,1600]{2,1,0:T(2,128)(2,1)S(1)} async-done(((bf16[64,2,1600]{2,1,0:T(2,128)(2,1)}), bf16[64,2,1600]{2,1,0:T(2,128)(2,1)S(1)}, u32[]{:S(2)}, u32[]{:S(2)}) %all-to-all-start.1) | async-done | bytes 409632 | tf_op jit(solution)/shard_map/all_to_all | solution.py:102
  112.0 1.1 reshape.94
  113.1 1.3 %fusion.44 = (f32[1,8,25,8,64]{4,0,2,3,1:T(1,128)S(1)}, f32[1,8,25,8,64]{4,0,2,3,1:T(1,128)S(1)}) fusion(f32[2,8,25,8,64]{4,0,2,3,1:T(2,128)S(1)} %bitcast.76), kind=kLoop, calls=%fused_computation.70 | loop fusion | bytes 1638400 | tf_op jit(solution)/shard_map/slice | solution.py:119
  114.5 0.2 slice.47
  114.8 0.2 slice.52
  115.1 2.5 %fusion.10 = f32[16,25,512]{2,0,1:T(8,128)S(1)} fusion(bf16[16,128,1]{1,0,2:T(8,128)(2,1)S(1)} %reshape.97, bf16[16,8,25,512]{3,1,2,0:T(8,128)(2,1)} %all-gather.3.cloned.1.call-done), kind=kOutput, calls=%fused_computation.7 | convolution fusion | flops 53043200 | bytes 4100096 | tf_op jit(solution)/shard_map/ok,kjc->ojc/dot_general | solution.py:67
  117.6 0.2 fusion.15
  117.8 0.8 pad_maximum_fusion
  (57 shorter events, 1.8 us)
Async XLA Ops:
  6.5 24.8 %copy-start.8 = (f32[64]{0:T(128)S(1)}, f32[64]{0:T(128)}, u32[]{:S(2)}) copy-start(f32[64]{0:T(128)} %param.20) | copy-start | bytes 772
  6.5 25.4 %copy-start.9 = (f32[64]{0:T(128)S(1)}, f32[64]{0:T(128)}, u32[]{:S(2)}) copy-start(f32[64]{0:T(128)} %param.19) | copy-start | bytes 772
  6.5 26.0 %copy-start.4 = (bf16[40,40]{1,0:T(8,128)(2,1)S(1)}, bf16[40,40]{1,0:T(8,128)(2,1)}, u32[]{:S(2)}) copy-start(bf16[40,40]{1,0:T(8,128)(2,1)} %param.15) | copy-start | bytes 9604
  6.5 26.1 %copy-start.5 = (bf16[40,40]{1,0:T(8,128)(2,1)S(1)}, bf16[40,40]{1,0:T(8,128)(2,1)}, u32[]{:S(2)}) copy-start(bf16[40,40]{1,0:T(8,128)(2,1)} %param.16) | copy-start | bytes 9604
  6.5 26.2 %copy-start.6 = (bf16[40,40]{1,0:T(8,128)(2,1)S(1)}, bf16[40,40]{1,0:T(8,128)(2,1)}, u32[]{:S(2)}) copy-start(bf16[40,40]{1,0:T(8,128)(2,1)} %param.17) | copy-start | bytes 9604
  6.5 26.6 %copy-start.2 = (bf16[40,40]{1,0:T(8,128)(2,1)S(1)}, bf16[40,40]{1,0:T(8,128)(2,1)}, u32[]{:S(2)}) copy-start(bf16[40,40]{1,0:T(8,128)(2,1)} %param.18) | copy-start | bytes 9604
  6.6 108.5 %all-gather.3.cloned.1.call-start = ((), (), s32[]{:S(2)}) async-start(), calls=%async_computation.2 | async-start | bytes 3686400 | tf_op jit(solution)/shard_map/all_gather | solution.py:58
  11.0 58.0 %all-to-all-start = ((bf16[64,2,1600]{2,1,0:T(2,128)(2,1)}), bf16[64,2,1600]{2,1,0:T(2,128)(2,1)S(1)}, u32[]{:S(2)}, u32[]{:S(2)}) async-start(bf16[64,2,1600]{2,1,0:T(2,128)(2,1)} %reshape_reshape.3), calls=%async_computation | async-start | bytes 851968 | tf_op jit(solution)/shard_map/all_to_all | solution.py:82
  33.2 44.1 %copy-start.1 = (bf16[64,64]{1,0:T(8,128)(2,1)S(1)}, bf16[64,64]{1,0:T(8,128)(2,1)}, u32[]{:S(2)}) copy-start(bf16[64,64]{1,0:T(8,128)(2,1)} %param.14) | copy-start | bytes 24580
  33.2 44.2 %copy-start.3 = (bf16[64,64]{1,0:T(8,128)(2,1)S(1)}, bf16[64,64]{1,0:T(8,128)(2,1)}, u32[]{:S(2)}) copy-start(bf16[64,64]{1,0:T(8,128)(2,1)} %param.13) | copy-start | bytes 24580
  69.5 8.7 %copy-start.10 = (f32[40]{0:T(128)S(1)}, f32[40]{0:T(128)}, u32[]{:S(2)}) copy-start(f32[40]{0:T(128)} %param.22) | copy-start | bytes 484
  69.5 8.9 %copy-start.11 = (f32[40]{0:T(128)S(1)}, f32[40]{0:T(128)}, u32[]{:S(2)}) copy-start(f32[40]{0:T(128)} %param.21) | copy-start | bytes 484
  72.7 39.3 %all-to-all-start.1 = ((bf16[64,2,1600]{2,1,0:T(2,128)(2,1)}), bf16[64,2,1600]{2,1,0:T(2,128)(2,1)S(1)}, u32[]{:S(2)}, u32[]{:S(2)}) async-start(bf16[64,2,1600]{2,1,0:T(2,128)(2,1)} %convert_element_type.97), calls=%async_computation.1 | async-start | bytes 851968 | tf_op jit(solution)/shard_map/all_to_all | solution.py:102
  114.7 2.8 %copy-start = (bf16[2,8,25,512]{3,1,2,0:T(8,128)(2,1)S(1)}, bf16[2,8,25,512]{3,1,2,0:T(8,128)(2,1)}, u32[]{:S(2)}) copy-start(bf16[2,8,25,512]{3,1,2,0:T(8,128)(2,1)} %param.12) | copy-start | bytes 1228804
  114.7 2.8 %copy-start.7 = (f32[512]{0:T(512)S(1)}, f32[512]{0:T(512)}, u32[]{:S(2)}) copy-start(f32[512]{0:T(512)} %param.23) | copy-start | bytes 6148
Sparse Core Ops, SparseCore 0:
  9.5 82.1 all-gather.2

commit v10 on v8

--- a/solution.py
+++ b/solution.py
@@ -73,15 +73,15 @@
     product = lax.reduce_precision(product, exponent_bits=8, mantissa_bits=7)
     system_rows = product.astype(jnp.bfloat16).reshape(density.shape)
     rc_count = lax.axis_size("rc")
-    col_groups = rc_count // state_count
+    col_groups = rc_count // (2 * state_count)
     group_width = column_total // col_groups
     outgoing = density.reshape(2, state_count, pair_count, col_groups, group_width)
-    outgoing = jnp.transpose(outgoing, (1, 3, 2, 0, 4)).reshape(
-        rc_count, pair_count, 2, group_width
+    outgoing = jnp.transpose(outgoing, (1, 3, 0, 2, 4)).reshape(
+        rc_count, pair_count, group_width
     )
     incoming = lax.all_to_all(outgoing, "rc", split_axis=0, concat_axis=0, tiled=True)
-    rows = incoming.reshape(rc_count * pair_count, 2 * group_width).astype(jnp.float32)
-    my_state = first_state + lax.axis_index("rc") // col_groups
+    rows = incoming.reshape(rc_count * pair_count, group_width).astype(jnp.float32)
+    my_state = first_state + lax.axis_index("rc") // (2 * col_groups)
     left_g = lax.dynamic_slice_in_dim(left_strength, my_state, 1)
     right_g = lax.dynamic_slice_in_dim(right_strength, my_state, 1)
     left_ops32 = left_ops.astype(jnp.float32)
@@ -98,8 +98,8 @@
     ).reshape(rows.shape)
     summed = (left_out + right_out).astype(jnp.bfloat16).reshape(outgoing.shape)
     returned = lax.all_to_all(summed, "rc", split_axis=0, concat_axis=0, tiled=True)
-    returned = returned.reshape(state_count, col_groups, pair_count, 2, group_width)
-    ladder_rows = jnp.transpose(returned, (3, 0, 2, 1, 4)).reshape(density.shape)
+    returned = returned.reshape(state_count, col_groups, 2, pair_count, group_width)
+    ladder_rows = jnp.transpose(returned, (2, 0, 3, 1, 4)).reshape(density.shape)
     pair_index = lax.axis_index("rc") * pair_count + jnp.arange(pair_count, dtype=jnp.int32)
     level_index = jnp.arange(levels, dtype=jnp.int32)
     left_pick = (pair_index[:, None] // levels == level_index[None, :]).astype(jnp.float32)

time: 124 us -> 134 us (1.081)
  waiting for transfers between devices: 67.9 us -> 77.8 us
    all_to_all x1, waiting for transfers between devices: 32.1 us -> 38.2 us  [shards(): lax.all_to_all(summed, 'rc', split_axis=0, concat_axis=0, tiled=True)]
    unnamed x33 -> x26, local copies, waits for them, and re-layouts: 4.52 us -> 0.6 us
    all_to_all x1, waiting for transfers between devices: 35.1 us -> 38.9 us  [shards(): lax.all_to_all(outgoing, 'rc', split_axis=0, concat_axis=0, tiled=True)]
    slice x2, local copies, waits for them, and re-layouts: 0.4 us -> 2.47 us  [shards(): ladder[1]]
  transfers between devices with their start and end apart: 3 -> 3, of which waited for: 2 -> 2; matrix products, arithmetic and copies ran while one was open for 11% -> 10% of each run, Pallas kernels for 0% -> 0%
where the time goes in v10:
time: 134 us; the launch traced here: 133 us
  waiting for transfers between devices  77.8 us (58%)
  starting transfers between devices  25 us (19%)
  between operations  13.7 us (10%)
  local copies, waits for them, and re-layouts  10.2 us (8%)
  matrix products  4.52 us (3%)
  other arithmetic  2.2 us (2%)
    all_to_all x1, waiting for transfers between devices, shards(): lax.all_to_all(outgoing, 'rc', split_axis=0, concat_axis=0, tiled=True)  38.9 us
    all_to_all x1, waiting for transfers between devices, shards(): lax.all_to_all(summed, 'rc', split_axis=0, concat_axis=0, tiled=True)  38.2 us
    all_to_all x1, starting transfers between devices, shards(): lax.all_to_all(outgoing, 'rc', split_axis=0, concat_axis=0, tiled=True)  20.3 us
    all_to_all x1, starting transfers between devices, shards(): lax.all_to_all(summed, 'rc', split_axis=0, concat_axis=0, tiled=True)  4.63 us
  transfers between devices with their start and end apart: 3, of which 2 were waited for; matrix products, arithmetic and copies ran while one was open for 10% of the time, Pallas kernels for 0%

profile of v10, /device:TPU:32, one launch (start us, length us, event | category | flops | bytes accessed | tf_op | source)
XLA Modules:
  0.0 133.4 jit_solution(10024715871008908680)
XLA Ops:
  6.6 0.7 all-gather.3.cloned.1.call-update
  7.3 1.4 %copy.107 = bf16[2,8,25,4,128]{4,0,3,1,2:T(2,128)(2,1)S(1)} copy(bf16[2,8,25,4,128]{4,1,3,2,0:T(8,128)(2,1)} %bitcast.73) | data formatting | bytes 819200 | tf_op jit(solution)/shard_map/reshape | solution.py:78
  8.7 1.1 copy.108
  9.7 20.3 %all-to-all-start = ((bf16[64,25,128]{2,1,0:T(8,128)(2,1)}), bf16[64,25,128]{2,1,0:T(8,128)(2,1)S(1)}, u32[]{:S(2)}, u32[]{:S(2)}) async-start(bf16[64,25,128]{2,1,0:T(8,128)(2,1)} %copy.108), calls=%async_computation | async-start | bytes 1048576 | tf_op jit(solution)/shard_map/all_to_all | solution.py:82
  30.1 1.2 dynamic_slice.15
  31.3 1.3 dynamic_slice.14
  33.3 0.7 fusion.25
  34.0 38.9 %all-to-all-done = bf16[64,25,128]{2,1,0:T(8,128)(2,1)S(1)} async-done(((bf16[64,25,128]{2,1,0:T(8,128)(2,1)}), bf16[64,25,128]{2,1,0:T(8,128)(2,1)S(1)}, u32[]{:S(2)}, u32[]{:S(2)}) %all-to-all-start) | async-done | bytes 409632 | tf_op jit(solution)/shard_map/all_to_all | solution.py:82
  72.9 0.1 reshape.97
  73.0 0.8 fusion.23
  73.8 1.3 fusion.6
  75.2 0.9 convert_element_type.97
  76.1 4.6 %all-to-all-start.1 = ((bf16[64,25,128]{2,1,0:T(8,128)(2,1)}), bf16[64,25,128]{2,1,0:T(8,128)(2,1)S(1)}, u32[]{:S(2)}, u32[]{:S(2)}) async-start(bf16[64,25,128]{2,1,0:T(8,128)(2,1)} %convert_element_type.97), calls=%async_computation.1 | async-start | bytes 1048576 | tf_op jit(solution)/shard_map/all_to_all | solution.py:100
  81.4 0.1 reshape.101
  81.6 0.2 select_reduce_fusion
  81.8 0.2 select_reduce_fusion.1
  82.0 38.2 %all-to-all-done.1 = bf16[64,25,128]{2,1,0:T(8,128)(2,1)S(1)} async-done(((bf16[64,25,128]{2,1,0:T(8,128)(2,1)}), bf16[64,25,128]{2,1,0:T(8,128)(2,1)S(1)}, u32[]{:S(2)}, u32[]{:S(2)}) %all-to-all-start.1) | async-done | bytes 409632 | tf_op jit(solution)/shard_map/all_to_all | solution.py:100
  120.2 0.1 copy.117
  120.3 2.3 %slice_reduce_fusion.1 = (f32[8,25,4,128]{3,2,0,1:T(4,128)S(1)}, f32[8,25,4,128]{3,2,0,1:T(4,128)S(1)}) fusion(f32[2,8,25,4,128]{4,0,3,1,2:T(2,128)S(1)} %bitcast.74), kind=kLoop, calls=%fused_computation.22 | loop fusion | bytes 1638400 | tf_op jit(solution)/shard_map/slice | solution.py:117
  122.7 0.2 slice.47
  122.8 0.2 slice.52
  123.0 2.5 %fusion.10 = f32[16,25,512]{2,0,1:T(8,128)S(1)} fusion(bf16[16,128,1]{1,0,2:T(8,128)(2,1)S(1)} %reshape.101, bf16[16,8,25,512]{3,1,2,0:T(8,128)(2,1)} %all-gather.3.cloned.1.call-done), kind=kOutput, calls=%fused_computation.7 | convolution fusion | flops 53043200 | bytes 4100096 | tf_op jit(solution)/shard_map/ok,kjc->ojc/dot_general | solution.py:67
  125.5 0.2 fusion.15
  125.8 0.8 pad_maximum_fusion
  (50 shorter events, 1.5 us)
Async XLA Ops:
  6.5 26.1 %copy-start.4 = (bf16[40,40]{1,0:T(8,128)(2,1)S(1)}, bf16[40,40]{1,0:T(8,128)(2,1)}, u32[]{:S(2)}) copy-start(bf16[40,40]{1,0:T(8,128)(2,1)} %param.15) | copy-start | bytes 9604
  6.5 26.2 %copy-start.5 = (bf16[40,40]{1,0:T(8,128)(2,1)S(1)}, bf16[40,40]{1,0:T(8,128)(2,1)}, u32[]{:S(2)}) copy-start(bf16[40,40]{1,0:T(8,128)(2,1)} %param.16) | copy-start | bytes 9604
  6.5 26.3 %copy-start.6 = (bf16[40,40]{1,0:T(8,128)(2,1)S(1)}, bf16[40,40]{1,0:T(8,128)(2,1)}, u32[]{:S(2)}) copy-start(bf16[40,40]{1,0:T(8,128)(2,1)} %param.17) | copy-start | bytes 9604
  6.5 26.6 %copy-start.2 = (bf16[40,40]{1,0:T(8,128)(2,1)S(1)}, bf16[40,40]{1,0:T(8,128)(2,1)}, u32[]{:S(2)}) copy-start(bf16[40,40]{1,0:T(8,128)(2,1)} %param.18) | copy-start | bytes 9604
  6.5 116.5 %all-gather.3.cloned.1.call-start = ((), (), s32[]{:S(2)}) async-start(), calls=%async_computation.2 | async-start | bytes 3686400 | tf_op jit(solution)/shard_map/all_gather | solution.py:58
  9.7 63.1 %all-to-all-start = ((bf16[64,25,128]{2,1,0:T(8,128)(2,1)}), bf16[64,25,128]{2,1,0:T(8,128)(2,1)S(1)}, u32[]{:S(2)}, u32[]{:S(2)}) async-start(bf16[64,25,128]{2,1,0:T(8,128)(2,1)} %copy.108), calls=%async_computation | async-start | bytes 1048576 | tf_op jit(solution)/shard_map/all_to_all | solution.py:82
  34.0 46.8 %copy-start.1 = (bf16[64,64]{1,0:T(8,128)(2,1)S(1)}, bf16[64,64]{1,0:T(8,128)(2,1)}, u32[]{:S(2)}) copy-start(bf16[64,64]{1,0:T(8,128)(2,1)} %param.14) | copy-start | bytes 24580
  34.0 46.9 %copy-start.3 = (bf16[64,64]{1,0:T(8,128)(2,1)S(1)}, bf16[64,64]{1,0:T(8,128)(2,1)}, u32[]{:S(2)}) copy-start(bf16[64,64]{1,0:T(8,128)(2,1)} %param.13) | copy-start | bytes 24580
  73.0 8.6 %copy-start.8 = (f32[40]{0:T(128)S(1)}, f32[40]{0:T(128)}, u32[]{:S(2)}) copy-start(f32[40]{0:T(128)} %param.22) | copy-start | bytes 484
  73.0 8.8 %copy-start.9 = (f32[40]{0:T(128)S(1)}, f32[40]{0:T(128)}, u32[]{:S(2)}) copy-start(f32[40]{0:T(128)} %param.21) | copy-start | bytes 484
  76.1 44.1 %all-to-all-start.1 = ((bf16[64,25,128]{2,1,0:T(8,128)(2,1)}), bf16[64,25,128]{2,1,0:T(8,128)(2,1)S(1)}, u32[]{:S(2)}, u32[]{:S(2)}) async-start(bf16[64,25,128]{2,1,0:T(8,128)(2,1)} %convert_element_type.97), calls=%async_computation.1 | async-start | bytes 1048576 | tf_op jit(solution)/shard_map/all_to_all | solution.py:100
  122.6 2.9 %copy-start = (bf16[2,8,25,512]{3,1,2,0:T(8,128)(2,1)S(1)}, bf16[2,8,25,512]{3,1,2,0:T(8,128)(2,1)}, u32[]{:S(2)}) copy-start(bf16[2,8,25,512]{3,1,2,0:T(8,128)(2,1)} %param.12) | copy-start | bytes 1228804
  122.6 2.9 %copy-start.7 = (f32[512]{0:T(512)S(1)}, f32[512]{0:T(512)}, u32[]{:S(2)}) copy-start(f32[512]{0:T(512)} %param.23) | copy-start | bytes 6148
Sparse Core Ops, SparseCore 0:
  9.5 89.9 all-gather.2

commit v11 on v10

--- a/solution.py
+++ b/solution.py
@@ -79,7 +79,9 @@
     outgoing = jnp.transpose(outgoing, (1, 3, 0, 2, 4)).reshape(
         rc_count, pair_count, group_width
     )
-    incoming = lax.all_to_all(outgoing, "rc", split_axis=0, concat_axis=0, tiled=True)
+    incoming = lax.all_to_all(
+        outgoing.reshape(rc_count, 2, -1), "rc", split_axis=0, concat_axis=0, tiled=True
+    )
     rows = incoming.reshape(rc_count * pair_count, group_width).astype(jnp.float32)
     my_state = first_state + lax.axis_index("rc") // (2 * col_groups)
     left_g = lax.dynamic_slice_in_dim(left_strength, my_state, 1)
@@ -96,7 +98,7 @@
     right_out = jnp.einsum(
         "ayb,abn->ayn", right_mats, cube, precision=lax.Precision.HIGHEST
     ).reshape(rows.shape)
-    summed = (left_out + right_out).astype(jnp.bfloat16).reshape(outgoing.shape)
+    summed = (left_out + right_out).astype(jnp.bfloat16).reshape(rc_count, 2, -1)
     returned = lax.all_to_all(summed, "rc", split_axis=0, concat_axis=0, tiled=True)
     returned = returned.reshape(state_count, col_groups, 2, pair_count, group_width)
     ladder_rows = jnp.transpose(returned, (2, 0, 3, 1, 4)).reshape(density.shape)

time: 134 us -> 123 us (0.918)
  waiting for transfers between devices: 77.8 us -> 68.6 us
  local copies, waits for them, and re-layouts: 10.2 us -> 8.34 us
    all_to_all x1, waiting for transfers between devices: 38.9 us -> 33.6 us  [shards(): lax.all_to_all(outgoing.reshape(rc_count, 2, -1), 'rc', split_axis=0, con...]
    all_to_all x1, waiting for transfers between devices: 38.2 us -> 34.3 us  [shards(): lax.all_to_all(summed, 'rc', split_axis=0, concat_axis=0, tiled=True)]
    slice x2 -> x1, local copies, waits for them, and re-layouts: 2.47 us -> 0.09 us  [shards(): ladder[1]]
  transfers between devices with their start and end apart: 3 -> 3, of which waited for: 2 -> 2; matrix products, arithmetic and copies ran while one was open for 10% -> 9% of each run, Pallas kernels for 0% -> 0%
where the time goes in v11:
time: 123 us
  waiting for transfers between devices  68.6 us (56%)
  starting transfers between devices  25 us (20%)
  between operations  13.7 us (11%)
  local copies, waits for them, and re-layouts  8.34 us (7%)
  matrix products  4.47 us (4%)
  other arithmetic  2.56 us (2%)
    all_to_all x1, waiting for transfers between devices, shards(): lax.all_to_all(summed, 'rc', split_axis=0, concat_axis=0, tiled=True)  34.3 us
    all_to_all x1, waiting for transfers between devices, shards(): lax.all_to_all(outgoing.reshape(rc_count, 2, -1), 'rc', split_axis=0, con...  33.6 us
    all_to_all x1, starting transfers between devices, shards(): lax.all_to_all(outgoing.reshape(rc_count, 2, -1), 'rc', split_axis=0, con...  20.3 us
    all_to_all x1, starting transfers between devices, shards(): lax.all_to_all(summed, 'rc', split_axis=0, concat_axis=0, tiled=True)  4.63 us
    dot_general x1, matrix products, shards(): jnp.einsum('ok,kjc->ojc', mixer, gathered.reshape(-1, pair_count, column_...  2.46 us
  transfers between devices with their start and end apart: 3, of which 2 were waited for; matrix products, arithmetic and copies ran while one was open for 9% of the time, Pallas kernels for 0%

profile of v11, /device:TPU:32, one launch (start us, length us, event | category | flops | bytes accessed | tf_op | source)
XLA Modules:
  0.0 122.6 jit_solution(8564687068732647985)
XLA Ops:
  6.6 0.7 all-gather.3.cloned.1.call-update
  7.3 1.2 copy.97
  8.5 1.1 reshape_reshape.3
  9.6 20.3 %all-to-all-start = ((bf16[64,2,1600]{2,1,0:T(2,128)(2,1)}), bf16[64,2,1600]{2,1,0:T(2,128)(2,1)S(1)}, u32[]{:S(2)}, u32[]{:S(2)}) async-start(bf16[64,2,1600]{2,1,0:T(2,128)(2,1)} %reshape_reshape.3), calls=%async_computation | async-start | bytes 851968 | tf_op jit(solution)/shard_map/all_to_all | solution.py:82
  29.9 0.8 copy.75
  30.7 0.8 copy.73
  31.7 0.1 copy.67
  31.9 0.6 dynamic_slice.15
  32.5 0.6 dynamic_slice.14
  33.3 0.7 fusion.25
  33.9 33.6 %all-to-all-done = bf16[64,2,1600]{2,1,0:T(2,128)(2,1)S(1)} async-done(((bf16[64,2,1600]{2,1,0:T(2,128)(2,1)}), bf16[64,2,1600]{2,1,0:T(2,128)(2,1)S(1)}, u32[]{:S(2)}, u32[]{:S(2)}) %all-to-all-start) | async-done | bytes 409632 | tf_op jit(solution)/shard_map/all_to_all | solution.py:82
  67.5 0.5 reshape.93
  68.0 0.8 fusion.23
  68.8 1.2 fusion.6
  70.1 1.1 convert_element_type.97
  71.2 4.6 %all-to-all-start.1 = ((bf16[64,2,1600]{2,1,0:T(2,128)(2,1)}), bf16[64,2,1600]{2,1,0:T(2,128)(2,1)S(1)}, u32[]{:S(2)}, u32[]{:S(2)}) async-start(bf16[64,2,1600]{2,1,0:T(2,128)(2,1)} %convert_element_type.97), calls=%async_computation.1 | async-start | bytes 851968 | tf_op jit(solution)/shard_map/all_to_all | solution.py:102
  76.5 0.1 reshape.97
  76.7 0.2 select_reduce_fusion.1
  76.8 0.2 select_reduce_fusion
  77.0 34.3 %all-to-all-done.1 = bf16[64,2,1600]{2,1,0:T(2,128)(2,1)S(1)} async-done(((bf16[64,2,1600]{2,1,0:T(2,128)(2,1)}), bf16[64,2,1600]{2,1,0:T(2,128)(2,1)S(1)}, u32[]{:S(2)}, u32[]{:S(2)}) %all-to-all-start.1) | async-done | bytes 409632 | tf_op jit(solution)/shard_map/all_to_all | solution.py:102
  111.4 0.3 reshape.94
  111.8 2.5 %fusion.10 = f32[16,25,512]{2,0,1:T(8,128)S(1)} fusion(bf16[16,128,1]{1,0,2:T(8,128)(2,1)S(1)} %reshape.97, bf16[16,8,25,512]{3,1,2,0:T(8,128)(2,1)} %all-gather.3.cloned.1.call-done), kind=kOutput, calls=%fused_computation.7 | convolution fusion | flops 53043200 | bytes 4100096 | tf_op jit(solution)/shard_map/ok,kjc->ojc/dot_general | solution.py:67
  114.3 0.6 fusion.15
  114.9 0.8 pad_maximum_fusion
  (50 shorter events, 1.3 us)
Async XLA Ops:
  6.5 26.6 %copy-start.2 = (bf16[40,40]{1,0:T(8,128)(2,1)S(1)}, bf16[40,40]{1,0:T(8,128)(2,1)}, u32[]{:S(2)}) copy-start(bf16[40,40]{1,0:T(8,128)(2,1)} %param.18) | copy-start | bytes 9604
  6.5 25.0 %copy-start.4 = (bf16[40,40]{1,0:T(8,128)(2,1)S(1)}, bf16[40,40]{1,0:T(8,128)(2,1)}, u32[]{:S(2)}) copy-start(bf16[40,40]{1,0:T(8,128)(2,1)} %param.16) | copy-start | bytes 9604
  6.5 25.2 %copy-start.5 = (bf16[40,40]{1,0:T(8,128)(2,1)S(1)}, bf16[40,40]{1,0:T(8,128)(2,1)}, u32[]{:S(2)}) copy-start(bf16[40,40]{1,0:T(8,128)(2,1)} %param.15) | copy-start | bytes 9604
  6.5 25.4 %copy-start.7 = (f32[64]{0:T(128)S(1)}, f32[64]{0:T(128)}, u32[]{:S(2)}) copy-start(f32[64]{0:T(128)} %param.20) | copy-start | bytes 772
  6.5 26.0 %copy-start.8 = (f32[64]{0:T(128)S(1)}, f32[64]{0:T(128)}, u32[]{:S(2)}) copy-start(f32[64]{0:T(128)} %param.19) | copy-start | bytes 772
  6.5 105.3 %all-gather.3.cloned.1.call-start = ((), (), s32[]{:S(2)}) async-start(), calls=%async_computation.2 | async-start | bytes 3686400 | tf_op jit(solution)/shard_map/all_gather | solution.py:58
  9.6 57.9 %all-to-all-start = ((bf16[64,2,1600]{2,1,0:T(2,128)(2,1)}), bf16[64,2,1600]{2,1,0:T(2,128)(2,1)S(1)}, u32[]{:S(2)}, u32[]{:S(2)}) async-start(bf16[64,2,1600]{2,1,0:T(2,128)(2,1)} %reshape_reshape.3), calls=%async_computation | async-start | bytes 851968 | tf_op jit(solution)/shard_map/all_to_all | solution.py:82
  33.2 42.6 %copy-start.1 = (bf16[64,64]{1,0:T(8,128)(2,1)S(1)}, bf16[64,64]{1,0:T(8,128)(2,1)}, u32[]{:S(2)}) copy-start(bf16[64,64]{1,0:T(8,128)(2,1)} %param.14) | copy-start | bytes 24580
  33.2 42.7 %copy-start.3 = (bf16[64,64]{1,0:T(8,128)(2,1)S(1)}, bf16[64,64]{1,0:T(8,128)(2,1)}, u32[]{:S(2)}) copy-start(bf16[64,64]{1,0:T(8,128)(2,1)} %param.13) | copy-start | bytes 24580
  68.0 8.7 %copy-start.9 = (f32[40]{0:T(128)S(1)}, f32[40]{0:T(128)}, u32[]{:S(2)}) copy-start(f32[40]{0:T(128)} %param.21) | copy-start | bytes 484
  68.0 8.9 %copy-start.10 = (f32[40]{0:T(128)S(1)}, f32[40]{0:T(128)}, u32[]{:S(2)}) copy-start(f32[40]{0:T(128)} %param.22) | copy-start | bytes 484
  71.2 40.2 %all-to-all-start.1 = ((bf16[64,2,1600]{2,1,0:T(2,128)(2,1)}), bf16[64,2,1600]{2,1,0:T(2,128)(2,1)S(1)}, u32[]{:S(2)}, u32[]{:S(2)}) async-start(bf16[64,2,1600]{2,1,0:T(2,128)(2,1)} %convert_element_type.97), calls=%async_computation.1 | async-start | bytes 851968 | tf_op jit(solution)/shard_map/all_to_all | solution.py:102
  111.7 2.6 %copy-start = (bf16[2,8,25,512]{3,1,2,0:T(8,128)(2,1)S(1)}, bf16[2,8,25,512]{3,1,2,0:T(8,128)(2,1)}, u32[]{:S(2)}) copy-start(bf16[2,8,25,512]{3,1,2,0:T(8,128)(2,1)} %param.12) | copy-start | bytes 1228804
  111.7 2.6 %copy-start.6 = (f32[512]{0:T(512)S(1)}, f32[512]{0:T(512)}, u32[]{:S(2)}) copy-start(f32[512]{0:T(512)} %param.23) | copy-start | bytes 6148
Sparse Core Ops, SparseCore 0:
  9.5 84.3 all-gather.2

commit v12 on v11

--- a/solution.py
+++ b/solution.py
@@ -62,7 +62,7 @@
     real3 = own_real.reshape(state_count, sys_count, state_count)
     imag3 = own_imag.reshape(state_count, sys_count, state_count)
     mixer = jnp.stack(
-        [jnp.stack([real3, -imag3], axis=2), jnp.stack([imag3, real3], axis=2)], axis=0
+        [jnp.stack([imag3, real3], axis=2), jnp.stack([real3, -imag3], axis=2)], axis=0
     ).reshape(2 * state_count, -1)
     product = jnp.einsum(
         "ok,kjc->ojc",
@@ -101,7 +101,7 @@
     summed = (left_out + right_out).astype(jnp.bfloat16).reshape(rc_count, 2, -1)
     returned = lax.all_to_all(summed, "rc", split_axis=0, concat_axis=0, tiled=True)
     returned = returned.reshape(state_count, col_groups, 2, pair_count, group_width)
-    ladder_rows = jnp.transpose(returned, (2, 0, 3, 1, 4)).reshape(density.shape)
+    ladder_rows = jnp.transpose(returned[:, :, ::-1], (2, 0, 3, 1, 4)).reshape(density.shape)
     pair_index = lax.axis_index("rc") * pair_count + jnp.arange(pair_count, dtype=jnp.int32)
     level_index = jnp.arange(levels, dtype=jnp.int32)
     left_pick = (pair_index[:, None] // levels == level_index[None, :]).astype(jnp.float32)
@@ -112,13 +112,13 @@
     )
     system_term = system_rows.astype(jnp.float32)
     ladder = ladder_rows.astype(jnp.float32)
-    real_in = density[0].astype(jnp.float32)
-    imag_in = density[1].astype(jnp.float32)
-    energy_grid = energies[None, None, :]
-    damp_grid = damping[None, :, None]
-    new_real = system_term[1] + ladder[1] - energy_grid * imag_in - damp_grid * real_in
-    new_imag = -system_term[0] - ladder[0] + energy_grid * real_in - damp_grid * imag_in
-    return jnp.stack([new_real, new_imag]).astype(jnp.bfloat16)
+    state_in = density.astype(jnp.float32)
+    swapped_in = state_in[::-1]
+    sign = jnp.array([1.0, -1.0], jnp.float32)[:, None, None, None]
+    energy_grid = energies[None, None, None, :]
+    damp_grid = damping[None, None, :, None]
+    derived = sign * (system_term + ladder) - (sign * energy_grid) * swapped_in
+    return (derived - damp_grid * state_in).astype(jnp.bfloat16)
 
 
 def solution(mesh):

time: 123 us -> 123 us (level)
    convert_element_type x0 -> x3, other arithmetic: none -> 1.58 us  [the longest x1 1.38 us: shards(): return (derived - damp_grid * state_in).astype(jnp.bfloat16)]
    another operation x4 -> x2, other arithmetic: 1.44 us -> 0.03 us  [shards(): jnp.stack([jnp.stack([imag3, real3], axis=2), jnp.stack([real3, -imag3],...]
  transfers between devices with their start and end apart: 3 -> 3, of which waited for: 2 -> 2; matrix products, arithmetic and copies ran while one was open for 9% -> 10% of each run, Pallas kernels for 0% -> 0%
where the time goes in v12:
time: 123 us
  waiting for transfers between devices  67.6 us (55%)
  starting transfers between devices  25 us (20%)
  between operations  13.7 us (11%)
  local copies, waits for them, and re-layouts  8.97 us (7%)
  matrix products  4.48 us (4%)
  other arithmetic  2.86 us (2%)
    all_to_all x1, waiting for transfers between devices, shards(): lax.all_to_all(summed, 'rc', split_axis=0, concat_axis=0, tiled=True)  34.2 us
    all_to_all x1, waiting for transfers between devices, shards(): lax.all_to_all(outgoing.reshape(rc_count, 2, -1), 'rc', split_axis=0, con...  32.7 us
    all_to_all x1, starting transfers between devices, shards(): lax.all_to_all(outgoing.reshape(rc_count, 2, -1), 'rc', split_axis=0, con...  20.3 us
    all_to_all x1, starting transfers between devices, shards(): lax.all_to_all(summed, 'rc', split_axis=0, concat_axis=0, tiled=True)  4.63 us
    dot_general x1, matrix products, shards(): jnp.einsum('ok,kjc->ojc', mixer, gathered.reshape(-1, pair_count, column_...  2.46 us
  transfers between devices with their start and end apart: 3, of which 2 were waited for; matrix products, arithmetic and copies ran while one was open for 10% of the time, Pallas kernels for 0%

profile of v12, /device:TPU:32, one launch (start us, length us, event | category | flops | bytes accessed | tf_op | source)
XLA Modules:
  0.0 122.6 jit_solution(10977578214570195366)
XLA Ops:
  6.6 0.7 all-gather.3.cloned.1.call-update
  7.3 1.2 copy.118
  8.5 1.1 reshape_reshape.3
  9.6 20.3 %all-to-all-start = ((bf16[64,2,1600]{2,1,0:T(2,128)(2,1)}), bf16[64,2,1600]{2,1,0:T(2,128)(2,1)S(1)}, u32[]{:S(2)}, u32[]{:S(2)}) async-start(bf16[64,2,1600]{2,1,0:T(2,128)(2,1)} %reshape_reshape.3), calls=%async_computation | async-start | bytes 851968 | tf_op jit(solution)/shard_map/all_to_all | solution.py:82
  29.9 0.8 copy.82
  30.7 0.8 copy.94
  31.5 0.8 copy.92
  32.7 0.6 dynamic_slice.15
  33.3 0.6 dynamic_slice.14
  34.1 0.7 fusion.23
  34.8 32.7 %all-to-all-done = bf16[64,2,1600]{2,1,0:T(2,128)(2,1)S(1)} async-done(((bf16[64,2,1600]{2,1,0:T(2,128)(2,1)}), bf16[64,2,1600]{2,1,0:T(2,128)(2,1)S(1)}, u32[]{:S(2)}, u32[]{:S(2)}) %all-to-all-start) | async-done | bytes 409632 | tf_op jit(solution)/shard_map/all_to_all | solution.py:82
  67.5 0.5 reshape.112
  67.9 0.8 fusion.21
  68.8 1.2 fusion.6
  70.1 1.1 convert_element_type.94
  71.2 4.6 %all-to-all-start.1 = ((bf16[64,2,1600]{2,1,0:T(2,128)(2,1)}), bf16[64,2,1600]{2,1,0:T(2,128)(2,1)S(1)}, u32[]{:S(2)}, u32[]{:S(2)}) async-start(bf16[64,2,1600]{2,1,0:T(2,128)(2,1)} %convert_element_type.94), calls=%async_computation.1 | async-start | bytes 851968 | tf_op jit(solution)/shard_map/all_to_all | solution.py:102
  76.5 0.1 reshape.118
  76.7 0.2 select_reduce_fusion.1
  76.9 0.2 select_reduce_fusion
  77.1 34.2 %all-to-all-done.1 = bf16[64,2,1600]{2,1,0:T(2,128)(2,1)S(1)} async-done(((bf16[64,2,1600]{2,1,0:T(2,128)(2,1)}), bf16[64,2,1600]{2,1,0:T(2,128)(2,1)S(1)}, u32[]{:S(2)}, u32[]{:S(2)}) %all-to-all-start.1) | async-done | bytes 409632 | tf_op jit(solution)/shard_map/all_to_all | solution.py:102
  111.4 0.3 reshape.113
  111.7 0.1 convert_bitcast_fusion
  111.9 2.5 %fusion.13 = f32[2,8,25,512]{3,1,0,2:T(8,128)S(1)} fusion(bf16[16,128,1]{1,0,2:T(8,128)(2,1)S(1)} %reshape.118, bf16[16,8,25,512]{3,1,2,0:T(8,128)(2,1)} %all-gather.3.cloned.1.call-done), kind=kOutput, calls=%fused_computation.8 | convolution fusion | flops 53043200 | bytes 4100096 | tf_op jit(solution)/shard_map/ok,kjc->ojc/dot_general | solution.py:67
  114.4 1.4 %fusion.19 = bf16[2,8,25,512]{3,1,2,0:T(8,128)(2,1)} fusion(f32[2,8,25,512]{3,1,0,2:T(8,128)S(1)} %fusion.13, f32[2,8,25,4,128]{4,2,0,3,1:T(8,128)S(1)} %convert_bitcast_fusion, f32[2,8,25,512]{3,1,2,0:T(8,128)S(1)} %convert_element_type.98, f32[25]{0:T(128)S(1)} %add_multiply_fusion, f32[2,512]{1,0:T(2,128)S(1)} %broadcast_multiply_fusion, f32[2]{0:T(128)S(1)} %copy-done.6), kind=kLoop, calls=%fused_computation.14 | loop fusion | flops 1433600 | bytes 2871404 | tf_op jit(solution)/shard_map/convert_element_type | solution.py:121
  (51 shorter events, 1.4 us)
Async XLA Ops:
  6.5 27.4 %copy-start.2 = (bf16[40,40]{1,0:T(8,128)(2,1)S(1)}, bf16[40,40]{1,0:T(8,128)(2,1)}, u32[]{:S(2)}) copy-start(bf16[40,40]{1,0:T(8,128)(2,1)} %param.19) | copy-start | bytes 9604
  6.5 25.8 %copy-start.3 = (bf16[40,40]{1,0:T(8,128)(2,1)S(1)}, bf16[40,40]{1,0:T(8,128)(2,1)}, u32[]{:S(2)}) copy-start(bf16[40,40]{1,0:T(8,128)(2,1)} %param.17) | copy-start | bytes 9604
  6.5 26.0 %copy-start.4 = (bf16[40,40]{1,0:T(8,128)(2,1)S(1)}, bf16[40,40]{1,0:T(8,128)(2,1)}, u32[]{:S(2)}) copy-start(bf16[40,40]{1,0:T(8,128)(2,1)} %param.16) | copy-start | bytes 9604
  6.5 26.2 %copy-start.7 = (f32[64]{0:T(128)S(1)}, f32[64]{0:T(128)}, u32[]{:S(2)}) copy-start(f32[64]{0:T(128)} %param.21) | copy-start | bytes 772
  6.5 26.8 %copy-start.8 = (f32[64]{0:T(128)S(1)}, f32[64]{0:T(128)}, u32[]{:S(2)}) copy-start(f32[64]{0:T(128)} %param.20) | copy-start | bytes 772
  6.5 105.3 %all-gather.3.cloned.1.call-start = ((), (), s32[]{:S(2)}) async-start(), calls=%async_computation.2 | async-start | bytes 3686400 | tf_op jit(solution)/shard_map/all_gather | solution.py:58
  9.6 57.9 %all-to-all-start = ((bf16[64,2,1600]{2,1,0:T(2,128)(2,1)}), bf16[64,2,1600]{2,1,0:T(2,128)(2,1)S(1)}, u32[]{:S(2)}, u32[]{:S(2)}) async-start(bf16[64,2,1600]{2,1,0:T(2,128)(2,1)} %reshape_reshape.3), calls=%async_computation | async-start | bytes 851968 | tf_op jit(solution)/shard_map/all_to_all | solution.py:82
  34.0 41.8 %copy-start.1 = (bf16[64,64]{1,0:T(8,128)(2,1)S(1)}, bf16[64,64]{1,0:T(8,128)(2,1)}, u32[]{:S(2)}) copy-start(bf16[64,64]{1,0:T(8,128)(2,1)} %param.15) | copy-start | bytes 24580
  34.0 41.9 %copy-start = (bf16[2,8,25,512]{3,1,2,0:T(8,128)(2,1)S(1)}, bf16[2,8,25,512]{3,1,2,0:T(8,128)(2,1)}, u32[]{:S(2)}) copy-start(bf16[2,8,25,512]{3,1,2,0:T(8,128)(2,1)} %param.13) | copy-start | bytes 1228804
  68.7 7.9 %copy-start.9 = (f32[40]{0:T(128)S(1)}, f32[40]{0:T(128)}, u32[]{:S(2)}) copy-start(f32[40]{0:T(128)} %param.22) | copy-start | bytes 484
  68.7 8.1 %copy-start.10 = (f32[40]{0:T(128)S(1)}, f32[40]{0:T(128)}, u32[]{:S(2)}) copy-start(f32[40]{0:T(128)} %param.23) | copy-start | bytes 484
  68.8 8.3 %copy-start.5 = (f32[512]{0:T(512)S(1)}, f32[512]{0:T(512)}, u32[]{:S(2)}) copy-start(f32[512]{0:T(512)} %param.24) | copy-start | bytes 6148
  68.8 8.3 %copy-start.6 = (f32[2]{0:T(128)S(1)}, f32[2]{0:T(128)}, u32[]{:S(2)}) copy-start(f32[2]{0:T(128)} %constant.60.clone) | copy-start | bytes 28
  71.2 40.2 %all-to-all-start.1 = ((bf16[64,2,1600]{2,1,0:T(2,128)(2,1)}), bf16[64,2,1600]{2,1,0:T(2,128)(2,1)S(1)}, u32[]{:S(2)}, u32[]{:S(2)}) async-start(bf16[64,2,1600]{2,1,0:T(2,128)(2,1)} %convert_element_type.94), calls=%async_computation.1 | async-start | bytes 851968 | tf_op jit(solution)/shard_map/all_to_all | solution.py:102
Sparse Core Ops, SparseCore 0:
  9.5 84.3 all-gather.2

commit v13 on v11

--- a/solution.py
+++ b/solution.py
@@ -82,7 +82,6 @@
     incoming = lax.all_to_all(
         outgoing.reshape(rc_count, 2, -1), "rc", split_axis=0, concat_axis=0, tiled=True
     )
-    rows = incoming.reshape(rc_count * pair_count, group_width).astype(jnp.float32)
     my_state = first_state + lax.axis_index("rc") // (2 * col_groups)
     left_g = lax.dynamic_slice_in_dim(left_strength, my_state, 1)
     right_g = lax.dynamic_slice_in_dim(right_strength, my_state, 1)
@@ -90,14 +89,17 @@
     right_ops32 = right_ops.astype(jnp.float32)
     left_mat = left_ops32[:levels] + left_g * left_ops32[levels:]
     right_mat = right_ops32[:levels] + right_g * right_ops32[levels:]
-    cube = rows.reshape(levels, levels, -1)
-    left_out = jnp.einsum(
-        "xa,abn->xbn", left_mat, cube, precision=lax.Precision.HIGHEST
-    ).reshape(rows.shape)
+    cube = incoming.reshape(levels, levels, -1)
+
+    def split_dot(spec, operator, operand):
+        high = operator.astype(jnp.bfloat16)
+        low = (operator - high.astype(jnp.float32)).astype(jnp.bfloat16)
+        first = jnp.einsum(spec, high, operand, preferred_element_type=jnp.float32)
+        return first + jnp.einsum(spec, low, operand, preferred_element_type=jnp.float32)
+
+    left_out = split_dot("xa,abn->xbn", left_mat, cube)
     right_mats = jnp.broadcast_to(right_mat, (levels,) + right_mat.shape)
-    right_out = jnp.einsum(
-        "ayb,abn->ayn", right_mats, cube, precision=lax.Precision.HIGHEST
-    ).reshape(rows.shape)
+    right_out = split_dot("ayb,abn->ayn", right_mats, cube)
     summed = (left_out + right_out).astype(jnp.bfloat16).reshape(rc_count, 2, -1)
     returned = lax.all_to_all(summed, "rc", split_axis=0, concat_axis=0, tiled=True)
     returned = returned.reshape(state_count, col_groups, 2, pair_count, group_width)

time: 123 us -> 123 us (level)
    convert_element_type x0 -> x2, other arithmetic: none -> 1.28 us  [the longest x1 0.65 us: split_dot(): high = operator.astype(jnp.bfloat16)]
  transfers between devices with their start and end apart: 3 -> 3, of which waited for: 2 -> 2; matrix products, arithmetic and copies ran while one was open for 9% -> 10% of each run, Pallas kernels for 0% -> 0%
where the time goes in v13:
time: 123 us
  waiting for transfers between devices  67.9 us (55%)
  starting transfers between devices  25 us (20%)
  between operations  13.7 us (11%)
  local copies, waits for them, and re-layouts  8.34 us (7%)
  matrix products  4.5 us (4%)
  other arithmetic  3.19 us (3%)
    all_to_all x1, waiting for transfers between devices, shards(): lax.all_to_all(summed, 'rc', split_axis=0, concat_axis=0, tiled=True)  34.3 us
    all_to_all x1, waiting for transfers between devices, shards(): lax.all_to_all(outgoing.reshape(rc_count, 2, -1), 'rc', split_axis=0, con...  32.9 us
    all_to_all x1, starting transfers between devices, shards(): lax.all_to_all(outgoing.reshape(rc_count, 2, -1), 'rc', split_axis=0, con...  20.3 us
    all_to_all x1, starting transfers between devices, shards(): lax.all_to_all(summed, 'rc', split_axis=0, concat_axis=0, tiled=True)  4.63 us
    dot_general x1, matrix products, shards(): jnp.einsum('ok,kjc->ojc', mixer, gathered.reshape(-1, pair_count, column_...  2.46 us
  transfers between devices with their start and end apart: 3, of which 2 were waited for; matrix products, arithmetic and copies ran while one was open for 10% of the time, Pallas kernels for 0%

profile of v13, /device:TPU:32, one launch (start us, length us, event | category | flops | bytes accessed | tf_op | source)
XLA Modules:
  0.0 122.6 jit_solution(1890872564074086391)
XLA Ops:
  6.6 0.7 all-gather.3.cloned.1.call-update
  7.3 1.2 copy.110
  8.5 1.1 reshape_reshape.3
  9.6 20.3 %all-to-all-start = ((bf16[64,2,1600]{2,1,0:T(2,128)(2,1)}), bf16[64,2,1600]{2,1,0:T(2,128)(2,1)S(1)}, u32[]{:S(2)}, u32[]{:S(2)}) async-start(bf16[64,2,1600]{2,1,0:T(2,128)(2,1)} %reshape_reshape.3), calls=%async_computation | async-start | bytes 851968 | tf_op jit(solution)/shard_map/all_to_all | solution.py:82
  29.9 0.8 copy.75
  30.8 0.8 copy.73
  31.9 0.6 dynamic_slice.14
  32.5 0.6 dynamic_slice.15
  33.2 0.7 fusion.44
  33.9 0.6 subtract_convert_fusion
  34.5 32.9 %all-to-all-done = bf16[64,2,1600]{2,1,0:T(2,128)(2,1)S(1)} async-done(((bf16[64,2,1600]{2,1,0:T(2,128)(2,1)}), bf16[64,2,1600]{2,1,0:T(2,128)(2,1)S(1)}, u32[]{:S(2)}, u32[]{:S(2)}) %all-to-all-start) | async-done | bytes 409632 | tf_op jit(solution)/shard_map/all_to_all | solution.py:82
  67.5 0.5 reshape.87
  68.0 0.3 fusion.24
  68.2 0.4 fusion.26
  68.6 0.4 fusion.28
  69.0 1.1 fusion.7
  70.1 1.1 reshape.88
  71.2 4.6 %all-to-all-start.1 = ((bf16[64,2,1600]{2,1,0:T(2,128)(2,1)}), bf16[64,2,1600]{2,1,0:T(2,128)(2,1)S(1)}, u32[]{:S(2)}, u32[]{:S(2)}) async-start(bf16[64,2,1600]{2,1,0:T(2,128)(2,1)} %reshape.88), calls=%async_computation.1 | async-start | bytes 851968 | tf_op jit(solution)/shard_map/all_to_all | solution.py:104
  76.7 0.2 select_reduce_fusion.1
  77.1 34.3 %all-to-all-done.1 = bf16[64,2,1600]{2,1,0:T(2,128)(2,1)S(1)} async-done(((bf16[64,2,1600]{2,1,0:T(2,128)(2,1)}), bf16[64,2,1600]{2,1,0:T(2,128)(2,1)S(1)}, u32[]{:S(2)}, u32[]{:S(2)}) %all-to-all-start.1) | async-done | bytes 409632 | tf_op jit(solution)/shard_map/all_to_all | solution.py:104
  111.4 0.3 reshape.89
  111.9 2.5 %fusion.11 = f32[16,25,512]{2,0,1:T(8,128)S(1)} fusion(bf16[16,128,1]{1,0,2:T(8,128)(2,1)S(1)} %reshape.92, bf16[16,8,25,512]{3,1,2,0:T(8,128)(2,1)} %all-gather.3.cloned.1.call-done), kind=kOutput, calls=%fused_computation.8 | convolution fusion | flops 53043200 | bytes 4100096 | tf_op jit(solution)/shard_map/ok,kjc->ojc/dot_general | solution.py:67
  114.4 0.6 fusion.16
  115.0 0.8 pad_maximum_fusion
  (51 shorter events, 1.7 us)
Async XLA Ops:
  6.5 25.1 %copy-start.2 = (bf16[40,40]{1,0:T(8,128)(2,1)S(1)}, bf16[40,40]{1,0:T(8,128)(2,1)}, u32[]{:S(2)}) copy-start(bf16[40,40]{1,0:T(8,128)(2,1)} %param.18) | copy-start | bytes 9604
  6.5 25.2 %copy-start.4 = (bf16[40,40]{1,0:T(8,128)(2,1)S(1)}, bf16[40,40]{1,0:T(8,128)(2,1)}, u32[]{:S(2)}) copy-start(bf16[40,40]{1,0:T(8,128)(2,1)} %param.17) | copy-start | bytes 9604
  6.5 25.4 %copy-start.6 = (f32[64]{0:T(128)S(1)}, f32[64]{0:T(128)}, u32[]{:S(2)}) copy-start(f32[64]{0:T(128)} %param.19) | copy-start | bytes 772
  6.5 26.0 %copy-start.7 = (f32[64]{0:T(128)S(1)}, f32[64]{0:T(128)}, u32[]{:S(2)}) copy-start(f32[64]{0:T(128)} %param.20) | copy-start | bytes 772
  6.5 105.3 %all-gather.3.cloned.1.call-start = ((), (), s32[]{:S(2)}) async-start(), calls=%async_computation.2 | async-start | bytes 3686400 | tf_op jit(solution)/shard_map/all_gather | solution.py:58
  9.6 57.9 %all-to-all-start = ((bf16[64,2,1600]{2,1,0:T(2,128)(2,1)}), bf16[64,2,1600]{2,1,0:T(2,128)(2,1)S(1)}, u32[]{:S(2)}, u32[]{:S(2)}) async-start(bf16[64,2,1600]{2,1,0:T(2,128)(2,1)} %reshape_reshape.3), calls=%async_computation | async-start | bytes 851968 | tf_op jit(solution)/shard_map/all_to_all | solution.py:82
  68.6 7.3 %copy-start.1 = (bf16[64,64]{1,0:T(8,128)(2,1)S(1)}, bf16[64,64]{1,0:T(8,128)(2,1)}, u32[]{:S(2)}) copy-start(bf16[64,64]{1,0:T(8,128)(2,1)} %param.14) | copy-start | bytes 24580
  68.6 7.4 %copy-start.3 = (bf16[64,64]{1,0:T(8,128)(2,1)S(1)}, bf16[64,64]{1,0:T(8,128)(2,1)}, u32[]{:S(2)}) copy-start(bf16[64,64]{1,0:T(8,128)(2,1)} %param.13) | copy-start | bytes 24580
  69.0 7.8 %copy-start.8 = (f32[40]{0:T(128)S(1)}, f32[40]{0:T(128)}, u32[]{:S(2)}) copy-start(f32[40]{0:T(128)} %param.21) | copy-start | bytes 484
  69.0 7.9 %copy-start.9 = (f32[40]{0:T(128)S(1)}, f32[40]{0:T(128)}, u32[]{:S(2)}) copy-start(f32[40]{0:T(128)} %param.22) | copy-start | bytes 484
  71.2 40.2 %all-to-all-start.1 = ((bf16[64,2,1600]{2,1,0:T(2,128)(2,1)}), bf16[64,2,1600]{2,1,0:T(2,128)(2,1)S(1)}, u32[]{:S(2)}, u32[]{:S(2)}) async-start(bf16[64,2,1600]{2,1,0:T(2,128)(2,1)} %reshape.88), calls=%async_computation.1 | async-start | bytes 851968 | tf_op jit(solution)/shard_map/all_to_all | solution.py:104
  111.7 2.6 %copy-start = (bf16[2,8,25,512]{3,1,2,0:T(8,128)(2,1)S(1)}, bf16[2,8,25,512]{3,1,2,0:T(8,128)(2,1)}, u32[]{:S(2)}) copy-start(bf16[2,8,25,512]{3,1,2,0:T(8,128)(2,1)} %param.12) | copy-start | bytes 1228804
  111.7 2.6 %copy-start.5 = (f32[512]{0:T(512)S(1)}, f32[512]{0:T(512)}, u32[]{:S(2)}) copy-start(f32[512]{0:T(512)} %param.23) | copy-start | bytes 6148
Sparse Core Ops, SparseCore 0:
  9.5 84.1 all-gather.2

commit v14 on v11

--- a/solution.py
+++ b/solution.py
@@ -61,17 +61,18 @@
     own_imag = lax.dynamic_slice_in_dim(herm_imag, first_state, state_count, axis=0)
     real3 = own_real.reshape(state_count, sys_count, state_count)
     imag3 = own_imag.reshape(state_count, sys_count, state_count)
-    mixer = jnp.stack(
-        [jnp.stack([real3, -imag3], axis=2), jnp.stack([imag3, real3], axis=2)], axis=0
-    ).reshape(2 * state_count, -1)
-    product = jnp.einsum(
-        "ok,kjc->ojc",
-        mixer,
-        gathered.reshape(-1, pair_count, column_total),
-        preferred_element_type=jnp.float32,
+    flat_gathered = gathered.reshape(-1, pair_count, column_total)
+    mixers = (
+        jnp.stack([real3, -imag3], axis=2).reshape(state_count, -1),
+        jnp.stack([imag3, real3], axis=2).reshape(state_count, -1),
     )
-    product = lax.reduce_precision(product, exponent_bits=8, mantissa_bits=7)
-    system_rows = product.astype(jnp.bfloat16).reshape(density.shape)
+    parts = []
+    for mixer in mixers:
+        part = jnp.einsum(
+            "ok,kjc->ojc", mixer, flat_gathered, preferred_element_type=jnp.float32
+        )
+        part = lax.reduce_precision(part, exponent_bits=8, mantissa_bits=7)
+        parts.append(part.astype(jnp.bfloat16))
     rc_count = lax.axis_size("rc")
     col_groups = rc_count // (2 * state_count)
     group_width = column_total // col_groups
@@ -110,14 +111,13 @@
         jnp.sum(left_pick * left_damping[None, :], axis=1)
         + jnp.sum(right_pick * right_damping[None, :], axis=1)
     )
-    system_term = system_rows.astype(jnp.float32)
     ladder = ladder_rows.astype(jnp.float32)
     real_in = density[0].astype(jnp.float32)
     imag_in = density[1].astype(jnp.float32)
     energy_grid = energies[None, None, :]
     damp_grid = damping[None, :, None]
-    new_real = system_term[1] + ladder[1] - energy_grid * imag_in - damp_grid * real_in
-    new_imag = -system_term[0] - ladder[0] + energy_grid * real_in - damp_grid * imag_in
+    new_real = parts[1].astype(jnp.float32) + ladder[1] - energy_grid * imag_in - damp_grid * real_in
+    new_imag = -parts[0].astype(jnp.float32) - ladder[0] + energy_grid * real_in - damp_grid * imag_in
     return jnp.stack([new_real, new_imag]).astype(jnp.bfloat16)
 
 

time: 123 us -> 125 us (1.016)
  matrix products: 4.47 us -> 7.41 us
    dot_general x1 -> x2, matrix products: 2.46 us -> 5.41 us  [shards(): jnp.einsum('ok,kjc->ojc', mixer, flat_gathered, preferred_element_type=jn...]
where the time goes in v14:
time: 125 us
  waiting for transfers between devices  68.8 us (55%)
  starting transfers between devices  25 us (20%)
  between operations  13.7 us (11%)
  local copies, waits for them, and re-layouts  8.15 us (7%)
  matrix products  7.41 us (6%)
  other arithmetic  1.93 us (2%)
    all_to_all x1, waiting for transfers between devices, shards(): lax.all_to_all(summed, 'rc', split_axis=0, concat_axis=0, tiled=True)  34.6 us
    all_to_all x1, waiting for transfers between devices, shards(): lax.all_to_all(outgoing.reshape(rc_count, 2, -1), 'rc', split_axis=0, con...  33.5 us
    all_to_all x1, starting transfers between devices, shards(): lax.all_to_all(outgoing.reshape(rc_count, 2, -1), 'rc', split_axis=0, con...  20.3 us
    dot_general x2, matrix products, shards(): jnp.einsum('ok,kjc->ojc', mixer, flat_gathered, preferred_element_type=jn...  5.41 us
    all_to_all x1, starting transfers between devices, shards(): lax.all_to_all(summed, 'rc', split_axis=0, concat_axis=0, tiled=True)  4.63 us
  transfers between devices with their start and end apart: 3, of which 2 were waited for; matrix products, arithmetic and copies ran while one was open for 9% of the time, Pallas kernels for 0%

profile of v14, /device:TPU:32, one launch (start us, length us, event | category | flops | bytes accessed | tf_op | source)
XLA Modules:
  0.0 124.9 jit_solution(4656728496281582306)
XLA Ops:
  6.6 0.7 all-gather.3.cloned.1.call-update
  7.3 1.2 copy.124
  8.5 1.1 reshape_reshape.3
  9.6 20.3 %all-to-all-start = ((bf16[64,2,1600]{2,1,0:T(2,128)(2,1)}), bf16[64,2,1600]{2,1,0:T(2,128)(2,1)S(1)}, u32[]{:S(2)}, u32[]{:S(2)}) async-start(bf16[64,2,1600]{2,1,0:T(2,128)(2,1)} %reshape_reshape.3), calls=%async_computation | async-start | bytes 851968 | tf_op jit(solution)/shard_map/all_to_all | solution.py:83
  29.9 0.8 copy.101
  30.8 0.8 copy.103
  31.6 0.6 dynamic_slice.15
  32.2 0.6 dynamic_slice.14
  33.0 0.1 copy.97
  33.3 0.7 fusion.29
  34.0 33.5 %all-to-all-done = bf16[64,2,1600]{2,1,0:T(2,128)(2,1)S(1)} async-done(((bf16[64,2,1600]{2,1,0:T(2,128)(2,1)}), bf16[64,2,1600]{2,1,0:T(2,128)(2,1)S(1)}, u32[]{:S(2)}, u32[]{:S(2)}) %all-to-all-start) | async-done | bytes 409632 | tf_op jit(solution)/shard_map/all_to_all | solution.py:83
  67.5 0.5 reshape.86
  68.0 0.8 fusion.19
  68.8 1.2 fusion
  70.1 1.1 convert_element_type.104
  71.2 4.6 %all-to-all-start.1 = ((bf16[64,2,1600]{2,1,0:T(2,128)(2,1)}), bf16[64,2,1600]{2,1,0:T(2,128)(2,1)S(1)}, u32[]{:S(2)}, u32[]{:S(2)}) async-start(bf16[64,2,1600]{2,1,0:T(2,128)(2,1)} %convert_element_type.104), calls=%async_computation.1 | async-start | bytes 851968 | tf_op jit(solution)/shard_map/all_to_all | solution.py:103
  75.9 0.1 copy.90
  76.4 0.2 select_reduce_fusion
  76.6 0.2 select_reduce_fusion.1
  76.8 34.6 %all-to-all-done.1 = bf16[64,2,1600]{2,1,0:T(2,128)(2,1)S(1)} async-done(((bf16[64,2,1600]{2,1,0:T(2,128)(2,1)}), bf16[64,2,1600]{2,1,0:T(2,128)(2,1)S(1)}, u32[]{:S(2)}, u32[]{:S(2)}) %all-to-all-start.1) | async-done | bytes 409632 | tf_op jit(solution)/shard_map/all_to_all | solution.py:103
  111.4 0.3 reshape.89
  111.9 3.7 %fusion.16 = bf16[1,8,25,512]{3,1,2,0:T(8,128)(2,1)S(1)} fusion(bf16[8,2,8,25,512]{4,2,3,1,0:T(8,128)(2,1)} %bitcast.121, f32[1,8,25,4,128]{4,2,0,3,1:T(8,128)S(1)} %get-tuple-element.5, f32[25]{0:T(128)S(1)} %add_multiply_fusion, f32[512]{0:T(512)S(1)} %copy-done.7, bf16[2,8,25,512]{3,1,2,0:T(8,128)(2,1)S(1)} %copy-done, ...), kind=kOutput, calls=%fused_computation.19 | convolution fusion | flops 27344896 | bytes 4304996 | tf_op jit(solution)/shard_map/ok,kjc->ojc/dot_general | solution.py:71
  115.6 1.7 %fusion.17 = bf16[1,8,25,512]{3,1,2,0:T(8,128)(2,1)S(1)} fusion(bf16[8,2,8,25,512]{4,2,3,1,0:T(8,128)(2,1)S(1)} %bitcast.122, f32[1,8,25,4,128]{4,2,0,3,1:T(8,128)S(1)} %get-tuple-element.6, f32[25]{0:T(128)S(1)} %add_multiply_fusion, f32[512]{0:T(512)S(1)} %copy-done.7, bf16[2,8,25,512]{3,1,2,0:T(8,128)(2,1)S(1)} %copy-done, ...), kind=kOutput, calls=%fused_computation.20 | convolution fusion | flops 27447296 | bytes 4304996 | tf_op jit(solution)/shard_map/ok,kjc->ojc/dot_general | solution.py:71
  117.3 0.8 pad_maximum_fusion
  (49 shorter events, 1.1 us)
Async XLA Ops:
  6.5 26.6 %copy-start.2 = (bf16[40,40]{1,0:T(8,128)(2,1)S(1)}, bf16[40,40]{1,0:T(8,128)(2,1)}, u32[]{:S(2)}) copy-start(bf16[40,40]{1,0:T(8,128)(2,1)} %param.18) | copy-start | bytes 9604
  6.5 25.1 %copy-start.8 = (f32[64]{0:T(128)S(1)}, f32[64]{0:T(128)}, u32[]{:S(2)}) copy-start(f32[64]{0:T(128)} %param.20) | copy-start | bytes 772
  6.5 25.6 %copy-start.9 = (f32[64]{0:T(128)S(1)}, f32[64]{0:T(128)}, u32[]{:S(2)}) copy-start(f32[64]{0:T(128)} %param.19) | copy-start | bytes 772
  6.5 26.3 %copy-start.4 = (bf16[40,40]{1,0:T(8,128)(2,1)S(1)}, bf16[40,40]{1,0:T(8,128)(2,1)}, u32[]{:S(2)}) copy-start(bf16[40,40]{1,0:T(8,128)(2,1)} %param.15) | copy-start | bytes 9604
  6.5 26.5 %copy-start.5 = (bf16[40,40]{1,0:T(8,128)(2,1)S(1)}, bf16[40,40]{1,0:T(8,128)(2,1)}, u32[]{:S(2)}) copy-start(bf16[40,40]{1,0:T(8,128)(2,1)} %param.16) | copy-start | bytes 9604
  6.5 105.3 %all-gather.3.cloned.1.call-start = ((), (), s32[]{:S(2)}) async-start(), calls=%async_computation.2 | async-start | bytes 3686400 | tf_op jit(solution)/shard_map/all_gather | solution.py:58
  9.6 57.9 %all-to-all-start = ((bf16[64,2,1600]{2,1,0:T(2,128)(2,1)}), bf16[64,2,1600]{2,1,0:T(2,128)(2,1)S(1)}, u32[]{:S(2)}, u32[]{:S(2)}) async-start(bf16[64,2,1600]{2,1,0:T(2,128)(2,1)} %reshape_reshape.3), calls=%async_computation | async-start | bytes 851968 | tf_op jit(solution)/shard_map/all_to_all | solution.py:83
  33.2 42.6 %copy-start.1 = (bf16[64,64]{1,0:T(8,128)(2,1)S(1)}, bf16[64,64]{1,0:T(8,128)(2,1)}, u32[]{:S(2)}) copy-start(bf16[64,64]{1,0:T(8,128)(2,1)} %param.14) | copy-start | bytes 24580
  33.2 42.7 %copy-start.3 = (bf16[64,64]{1,0:T(8,128)(2,1)S(1)}, bf16[64,64]{1,0:T(8,128)(2,1)}, u32[]{:S(2)}) copy-start(bf16[64,64]{1,0:T(8,128)(2,1)} %param.13) | copy-start | bytes 24580
  33.9 42.5 %copy-start.10 = (f32[40]{0:T(128)S(1)}, f32[40]{0:T(128)}, u32[]{:S(2)}) copy-start(f32[40]{0:T(128)} %param.22) | copy-start | bytes 484
  34.0 42.6 %copy-start.11 = (f32[40]{0:T(128)S(1)}, f32[40]{0:T(128)}, u32[]{:S(2)}) copy-start(f32[40]{0:T(128)} %param.21) | copy-start | bytes 484
  70.0 41.9 %copy-start = (bf16[2,8,25,512]{3,1,2,0:T(8,128)(2,1)S(1)}, bf16[2,8,25,512]{3,1,2,0:T(8,128)(2,1)}, u32[]{:S(2)}) copy-start(bf16[2,8,25,512]{3,1,2,0:T(8,128)(2,1)} %param.12) | copy-start | bytes 1228804
  70.0 41.9 %copy-start.7 = (f32[512]{0:T(512)S(1)}, f32[512]{0:T(512)}, u32[]{:S(2)}) copy-start(f32[512]{0:T(512)} %param.23) | copy-start | bytes 6148
  71.2 40.2 %all-to-all-start.1 = ((bf16[64,2,1600]{2,1,0:T(2,128)(2,1)}), bf16[64,2,1600]{2,1,0:T(2,128)(2,1)S(1)}, u32[]{:S(2)}, u32[]{:S(2)}) async-start(bf16[64,2,1600]{2,1,0:T(2,128)(2,1)} %convert_element_type.104), calls=%async_computation.1 | async-start | bytes 851968 | tf_op jit(solution)/shard_map/all_to_all | solution.py:103
  111.8 3.8 %copy-start.6 = (bf16[16,8,25,512]{3,1,2,0:T(8,128)(2,1)S(1)}, bf16[16,8,25,512]{3,1,2,0:T(8,128)(2,1)}, u32[]{:S(2)}) copy-start(bf16[16,8,25,512]{3,1,2,0:T(8,128)(2,1)} %all-gather.3.cloned.1.call-done) | copy-start | bytes 9830404
Sparse Core Ops, SparseCore 0:
  9.5 84.3 all-gather.2

commit v15 on v11

--- a/solution.py
+++ b/solution.py
@@ -92,11 +92,11 @@
     right_mat = right_ops32[:levels] + right_g * right_ops32[levels:]
     cube = rows.reshape(levels, levels, -1)
     left_out = jnp.einsum(
-        "xa,abn->xbn", left_mat, cube, precision=lax.Precision.HIGHEST
+        "xa,abn->xbn", left_mat, cube, precision=lax.Precision.HIGH
     ).reshape(rows.shape)
     right_mats = jnp.broadcast_to(right_mat, (levels,) + right_mat.shape)
     right_out = jnp.einsum(
-        "ayb,abn->ayn", right_mats, cube, precision=lax.Precision.HIGHEST
+        "ayb,abn->ayn", right_mats, cube, precision=lax.Precision.HIGH
     ).reshape(rows.shape)
     summed = (left_out + right_out).astype(jnp.bfloat16).reshape(rc_count, 2, -1)
     returned = lax.all_to_all(summed, "rc", split_axis=0, concat_axis=0, tiled=True)

time: 123 us -> 123 us (level)
  no operation moved by 1% of the time
where the time goes in v15:
time: 123 us; the launch traced here: 122 us
  waiting for transfers between devices  68.7 us (56%)
  starting transfers between devices  25 us (20%)
  between operations  13.7 us (11%)
  local copies, waits for them, and re-layouts  8.34 us (7%)
  matrix products  4.15 us (3%)
  other arithmetic  2.56 us (2%)
    all_to_all x1, waiting for transfers between devices, shards(): lax.all_to_all(summed, 'rc', split_axis=0, concat_axis=0, tiled=True)  34.5 us
    all_to_all x1, waiting for transfers between devices, shards(): lax.all_to_all(outgoing.reshape(rc_count, 2, -1), 'rc', split_axis=0, con...  33.6 us
    all_to_all x1, starting transfers between devices, shards(): lax.all_to_all(outgoing.reshape(rc_count, 2, -1), 'rc', split_axis=0, con...  20.3 us
    all_to_all x1, starting transfers between devices, shards(): lax.all_to_all(summed, 'rc', split_axis=0, concat_axis=0, tiled=True)  4.63 us
    dot_general x1, matrix products, shards(): jnp.einsum('ok,kjc->ojc', mixer, gathered.reshape(-1, pair_count, column_...  2.46 us
  transfers between devices with their start and end apart: 3, of which 2 were waited for; matrix products, arithmetic and copies ran while one was open for 9% of the time, Pallas kernels for 0%

profile of v15, /device:TPU:32, one launch (start us, length us, event | category | flops | bytes accessed | tf_op | source)
XLA Modules:
  0.0 122.4 jit_solution(12592175539771912094)
XLA Ops:
  6.6 0.7 all-gather.3.cloned.1.call-update
  7.3 1.2 copy.97
  8.5 1.1 reshape_reshape.3
  9.6 20.3 %all-to-all-start = ((bf16[64,2,1600]{2,1,0:T(2,128)(2,1)}), bf16[64,2,1600]{2,1,0:T(2,128)(2,1)S(1)}, u32[]{:S(2)}, u32[]{:S(2)}) async-start(bf16[64,2,1600]{2,1,0:T(2,128)(2,1)} %reshape_reshape.3), calls=%async_computation | async-start | bytes 851968 | tf_op jit(solution)/shard_map/all_to_all | solution.py:82
  29.9 0.8 copy.75
  30.7 0.8 copy.73
  31.7 0.1 copy.67
  31.9 0.6 dynamic_slice.15
  32.5 0.6 dynamic_slice.14
  33.3 0.7 fusion.25
  33.9 33.6 %all-to-all-done = bf16[64,2,1600]{2,1,0:T(2,128)(2,1)S(1)} async-done(((bf16[64,2,1600]{2,1,0:T(2,128)(2,1)}), bf16[64,2,1600]{2,1,0:T(2,128)(2,1)S(1)}, u32[]{:S(2)}, u32[]{:S(2)}) %all-to-all-start) | async-done | bytes 409632 | tf_op jit(solution)/shard_map/all_to_all | solution.py:82
  67.5 0.5 reshape.93
  68.0 0.6 fusion.23
  68.6 1.1 fusion.6
  69.7 1.1 convert_element_type.97
  70.9 4.6 %all-to-all-start.1 = ((bf16[64,2,1600]{2,1,0:T(2,128)(2,1)}), bf16[64,2,1600]{2,1,0:T(2,128)(2,1)S(1)}, u32[]{:S(2)}, u32[]{:S(2)}) async-start(bf16[64,2,1600]{2,1,0:T(2,128)(2,1)} %convert_element_type.97), calls=%async_computation.1 | async-start | bytes 851968 | tf_op jit(solution)/shard_map/all_to_all | solution.py:102
  76.2 0.1 reshape.97
  76.3 0.2 select_reduce_fusion.1
  76.5 0.2 select_reduce_fusion
  76.7 34.5 %all-to-all-done.1 = bf16[64,2,1600]{2,1,0:T(2,128)(2,1)S(1)} async-done(((bf16[64,2,1600]{2,1,0:T(2,128)(2,1)}), bf16[64,2,1600]{2,1,0:T(2,128)(2,1)S(1)}, u32[]{:S(2)}, u32[]{:S(2)}) %all-to-all-start.1) | async-done | bytes 409632 | tf_op jit(solution)/shard_map/all_to_all | solution.py:102
  111.2 0.3 reshape.94
  111.7 2.5 %fusion.10 = f32[16,25,512]{2,0,1:T(8,128)S(1)} fusion(bf16[16,128,1]{1,0,2:T(8,128)(2,1)S(1)} %reshape.97, bf16[16,8,25,512]{3,1,2,0:T(8,128)(2,1)} %all-gather.3.cloned.1.call-done), kind=kOutput, calls=%fused_computation.7 | convolution fusion | flops 53043200 | bytes 4100096 | tf_op jit(solution)/shard_map/ok,kjc->ojc/dot_general | solution.py:67
  114.2 0.6 fusion.15
  114.8 0.8 pad_maximum_fusion
  (50 shorter events, 1.3 us)
Async XLA Ops:
  6.5 26.6 %copy-start.2 = (bf16[40,40]{1,0:T(8,128)(2,1)S(1)}, bf16[40,40]{1,0:T(8,128)(2,1)}, u32[]{:S(2)}) copy-start(bf16[40,40]{1,0:T(8,128)(2,1)} %param.18) | copy-start | bytes 9604
  6.5 25.0 %copy-start.4 = (bf16[40,40]{1,0:T(8,128)(2,1)S(1)}, bf16[40,40]{1,0:T(8,128)(2,1)}, u32[]{:S(2)}) copy-start(bf16[40,40]{1,0:T(8,128)(2,1)} %param.16) | copy-start | bytes 9604
  6.5 25.2 %copy-start.5 = (bf16[40,40]{1,0:T(8,128)(2,1)S(1)}, bf16[40,40]{1,0:T(8,128)(2,1)}, u32[]{:S(2)}) copy-start(bf16[40,40]{1,0:T(8,128)(2,1)} %param.15) | copy-start | bytes 9604
  6.5 25.4 %copy-start.7 = (f32[64]{0:T(128)S(1)}, f32[64]{0:T(128)}, u32[]{:S(2)}) copy-start(f32[64]{0:T(128)} %param.20) | copy-start | bytes 772
  6.5 26.0 %copy-start.8 = (f32[64]{0:T(128)S(1)}, f32[64]{0:T(128)}, u32[]{:S(2)}) copy-start(f32[64]{0:T(128)} %param.19) | copy-start | bytes 772
  6.5 105.1 %all-gather.3.cloned.1.call-start = ((), (), s32[]{:S(2)}) async-start(), calls=%async_computation.2 | async-start | bytes 3686400 | tf_op jit(solution)/shard_map/all_gather | solution.py:58
  9.6 57.9 %all-to-all-start = ((bf16[64,2,1600]{2,1,0:T(2,128)(2,1)}), bf16[64,2,1600]{2,1,0:T(2,128)(2,1)S(1)}, u32[]{:S(2)}, u32[]{:S(2)}) async-start(bf16[64,2,1600]{2,1,0:T(2,128)(2,1)} %reshape_reshape.3), calls=%async_computation | async-start | bytes 851968 | tf_op jit(solution)/shard_map/all_to_all | solution.py:82
  33.2 42.3 %copy-start.1 = (bf16[64,64]{1,0:T(8,128)(2,1)S(1)}, bf16[64,64]{1,0:T(8,128)(2,1)}, u32[]{:S(2)}) copy-start(bf16[64,64]{1,0:T(8,128)(2,1)} %param.14) | copy-start | bytes 24580
  33.2 42.4 %copy-start.3 = (bf16[64,64]{1,0:T(8,128)(2,1)S(1)}, bf16[64,64]{1,0:T(8,128)(2,1)}, u32[]{:S(2)}) copy-start(bf16[64,64]{1,0:T(8,128)(2,1)} %param.13) | copy-start | bytes 24580
  68.0 8.4 %copy-start.9 = (f32[40]{0:T(128)S(1)}, f32[40]{0:T(128)}, u32[]{:S(2)}) copy-start(f32[40]{0:T(128)} %param.21) | copy-start | bytes 484
  68.0 8.6 %copy-start.10 = (f32[40]{0:T(128)S(1)}, f32[40]{0:T(128)}, u32[]{:S(2)}) copy-start(f32[40]{0:T(128)} %param.22) | copy-start | bytes 484
  70.9 40.3 %all-to-all-start.1 = ((bf16[64,2,1600]{2,1,0:T(2,128)(2,1)}), bf16[64,2,1600]{2,1,0:T(2,128)(2,1)S(1)}, u32[]{:S(2)}, u32[]{:S(2)}) async-start(bf16[64,2,1600]{2,1,0:T(2,128)(2,1)} %convert_element_type.97), calls=%async_computation.1 | async-start | bytes 851968 | tf_op jit(solution)/shard_map/all_to_all | solution.py:102
  111.5 2.6 %copy-start = (bf16[2,8,25,512]{3,1,2,0:T(8,128)(2,1)S(1)}, bf16[2,8,25,512]{3,1,2,0:T(8,128)(2,1)}, u32[]{:S(2)}) copy-start(bf16[2,8,25,512]{3,1,2,0:T(8,128)(2,1)} %param.12) | copy-start | bytes 1228804
  111.5 2.6 %copy-start.6 = (f32[512]{0:T(512)S(1)}, f32[512]{0:T(512)}, u32[]{:S(2)}) copy-start(f32[512]{0:T(512)} %param.23) | copy-start | bytes 6148
Sparse Core Ops, SparseCore 0:
  9.5 84.8 all-gather.2

commit v16 on v11

--- a/solution.py
+++ b/solution.py
@@ -91,14 +91,14 @@
     left_mat = left_ops32[:levels] + left_g * left_ops32[levels:]
     right_mat = right_ops32[:levels] + right_g * right_ops32[levels:]
     cube = rows.reshape(levels, levels, -1)
+    right_mats = jnp.broadcast_to(right_mat, (levels,) + right_mat.shape)
     left_out = jnp.einsum(
         "xa,abn->xbn", left_mat, cube, precision=lax.Precision.HIGHEST
     ).reshape(rows.shape)
-    right_mats = jnp.broadcast_to(right_mat, (levels,) + right_mat.shape)
     right_out = jnp.einsum(
         "ayb,abn->ayn", right_mats, cube, precision=lax.Precision.HIGHEST
     ).reshape(rows.shape)
-    summed = (left_out + right_out).astype(jnp.bfloat16).reshape(rc_count, 2, -1)
+    summed = (right_out + left_out).astype(jnp.bfloat16).reshape(rc_count, 2, -1)
     returned = lax.all_to_all(summed, "rc", split_axis=0, concat_axis=0, tiled=True)
     returned = returned.reshape(state_count, col_groups, 2, pair_count, group_width)
     ladder_rows = jnp.transpose(returned, (2, 0, 3, 1, 4)).reshape(density.shape)

time: 123 us -> 123 us (level)
  no operation moved by 1% of the time
where the time goes in v16:
time: 123 us
  waiting for transfers between devices  68.9 us (56%)
  starting transfers between devices  25.1 us (20%)
  between operations  13.7 us (11%)
  local copies, waits for them, and re-layouts  8.26 us (7%)
  matrix products  4.37 us (4%)
  other arithmetic  2.59 us (2%)
    all_to_all x1, waiting for transfers between devices, shards(): lax.all_to_all(summed, 'rc', split_axis=0, concat_axis=0, tiled=True)  34.6 us
    all_to_all x1, waiting for transfers between devices, shards(): lax.all_to_all(outgoing.reshape(rc_count, 2, -1), 'rc', split_axis=0, con...  33.6 us
    all_to_all x1, starting transfers between devices, shards(): lax.all_to_all(outgoing.reshape(rc_count, 2, -1), 'rc', split_axis=0, con...  20.4 us
    all_to_all x1, starting transfers between devices, shards(): lax.all_to_all(summed, 'rc', split_axis=0, concat_axis=0, tiled=True)  4.63 us
    dot_general x1, matrix products, shards(): jnp.einsum('ok,kjc->ojc', mixer, gathered.reshape(-1, pair_count, column_...  2.46 us
  transfers between devices with their start and end apart: 3, of which 2 were waited for; matrix products, arithmetic and copies ran while one was open for 9% of the time, Pallas kernels for 0%

profile of v16, /device:TPU:32, one launch (start us, length us, event | category | flops | bytes accessed | tf_op | source)
XLA Modules:
  0.0 122.8 jit_solution(10305560704218074972)
XLA Ops:
  6.6 0.7 all-gather.3.cloned.1.call-update
  7.3 1.2 copy.95
  8.5 1.1 reshape_reshape.3
  9.6 20.4 %all-to-all-start = ((bf16[64,2,1600]{2,1,0:T(2,128)(2,1)}), bf16[64,2,1600]{2,1,0:T(2,128)(2,1)S(1)}, u32[]{:S(2)}, u32[]{:S(2)}) async-start(bf16[64,2,1600]{2,1,0:T(2,128)(2,1)} %reshape_reshape.3), calls=%async_computation | async-start | bytes 851968 | tf_op jit(solution)/shard_map/all_to_all | solution.py:82
  30.0 0.8 copy.72
  30.9 0.8 copy.70
  31.9 0.1 copy.66
  32.0 0.6 dynamic_slice.15
  32.7 0.7 dynamic_slice.14
  33.4 0.7 fusion.29
  34.1 33.6 %all-to-all-done = bf16[64,2,1600]{2,1,0:T(2,128)(2,1)S(1)} async-done(((bf16[64,2,1600]{2,1,0:T(2,128)(2,1)}), bf16[64,2,1600]{2,1,0:T(2,128)(2,1)S(1)}, u32[]{:S(2)}, u32[]{:S(2)}) %all-to-all-start) | async-done | bytes 409632 | tf_op jit(solution)/shard_map/all_to_all | solution.py:82
  67.6 0.5 reshape.93
  68.1 1.1 fusion.22
  69.2 0.8 fusion.6
  70.0 1.1 convert_element_type.97
  71.1 4.6 %all-to-all-start.1 = ((bf16[64,2,1600]{2,1,0:T(2,128)(2,1)}), bf16[64,2,1600]{2,1,0:T(2,128)(2,1)S(1)}, u32[]{:S(2)}, u32[]{:S(2)}) async-start(bf16[64,2,1600]{2,1,0:T(2,128)(2,1)} %convert_element_type.97), calls=%async_computation.1 | async-start | bytes 851968 | tf_op jit(solution)/shard_map/all_to_all | solution.py:102
  76.5 0.1 reshape.97
  76.6 0.2 select_reduce_fusion.1
  76.8 0.2 select_reduce_fusion
  77.0 34.6 %all-to-all-done.1 = bf16[64,2,1600]{2,1,0:T(2,128)(2,1)S(1)} async-done(((bf16[64,2,1600]{2,1,0:T(2,128)(2,1)}), bf16[64,2,1600]{2,1,0:T(2,128)(2,1)S(1)}, u32[]{:S(2)}, u32[]{:S(2)}) %all-to-all-start.1) | async-done | bytes 409632 | tf_op jit(solution)/shard_map/all_to_all | solution.py:102
  111.6 0.3 reshape.94
  112.1 2.5 %fusion.10 = f32[16,25,512]{2,0,1:T(8,128)S(1)} fusion(bf16[16,128,1]{1,0,2:T(8,128)(2,1)S(1)} %reshape.97, bf16[16,8,25,512]{3,1,2,0:T(8,128)(2,1)} %all-gather.3.cloned.1.call-done), kind=kOutput, calls=%fused_computation.7 | convolution fusion | flops 53043200 | bytes 4100096 | tf_op jit(solution)/shard_map/ok,kjc->ojc/dot_general | solution.py:67
  114.6 0.6 fusion.15
  115.2 0.8 pad_maximum_fusion
  (47 shorter events, 1.2 us)
Async XLA Ops:
  6.5 25.2 %copy-start.2 = (bf16[40,40]{1,0:T(8,128)(2,1)S(1)}, bf16[40,40]{1,0:T(8,128)(2,1)}, u32[]{:S(2)}) copy-start(bf16[40,40]{1,0:T(8,128)(2,1)} %param.18) | copy-start | bytes 9604
  6.5 25.3 %copy-start.4 = (bf16[40,40]{1,0:T(8,128)(2,1)S(1)}, bf16[40,40]{1,0:T(8,128)(2,1)}, u32[]{:S(2)}) copy-start(bf16[40,40]{1,0:T(8,128)(2,1)} %param.17) | copy-start | bytes 9604
  6.5 25.5 %copy-start.6 = (f32[64]{0:T(128)S(1)}, f32[64]{0:T(128)}, u32[]{:S(2)}) copy-start(f32[64]{0:T(128)} %param.19) | copy-start | bytes 772
  6.5 26.1 %copy-start.7 = (f32[64]{0:T(128)S(1)}, f32[64]{0:T(128)}, u32[]{:S(2)}) copy-start(f32[64]{0:T(128)} %param.20) | copy-start | bytes 772
  6.5 105.6 %all-gather.3.cloned.1.call-start = ((), (), s32[]{:S(2)}) async-start(), calls=%async_computation.2 | async-start | bytes 3686400 | tf_op jit(solution)/shard_map/all_gather | solution.py:58
  9.6 66.2 %copy-start.1 = (bf16[64,64]{1,0:T(8,128)(2,1)S(1)}, bf16[64,64]{1,0:T(8,128)(2,1)}, u32[]{:S(2)}) copy-start(bf16[64,64]{1,0:T(8,128)(2,1)} %param.14) | copy-start | bytes 24580
  9.6 58.1 %all-to-all-start = ((bf16[64,2,1600]{2,1,0:T(2,128)(2,1)}), bf16[64,2,1600]{2,1,0:T(2,128)(2,1)S(1)}, u32[]{:S(2)}, u32[]{:S(2)}) async-start(bf16[64,2,1600]{2,1,0:T(2,128)(2,1)} %reshape_reshape.3), calls=%async_computation | async-start | bytes 851968 | tf_op jit(solution)/shard_map/all_to_all | solution.py:82
  30.0 45.9 %copy-start.3 = (bf16[64,64]{1,0:T(8,128)(2,1)S(1)}, bf16[64,64]{1,0:T(8,128)(2,1)}, u32[]{:S(2)}) copy-start(bf16[64,64]{1,0:T(8,128)(2,1)} %param.13) | copy-start | bytes 24580
  33.3 43.3 %copy-start.8 = (f32[40]{0:T(128)S(1)}, f32[40]{0:T(128)}, u32[]{:S(2)}) copy-start(f32[40]{0:T(128)} %param.21) | copy-start | bytes 484
  33.3 43.5 %copy-start.9 = (f32[40]{0:T(128)S(1)}, f32[40]{0:T(128)}, u32[]{:S(2)}) copy-start(f32[40]{0:T(128)} %param.22) | copy-start | bytes 484
  71.1 40.5 %all-to-all-start.1 = ((bf16[64,2,1600]{2,1,0:T(2,128)(2,1)}), bf16[64,2,1600]{2,1,0:T(2,128)(2,1)S(1)}, u32[]{:S(2)}, u32[]{:S(2)}) async-start(bf16[64,2,1600]{2,1,0:T(2,128)(2,1)} %convert_element_type.97), calls=%async_computation.1 | async-start | bytes 851968 | tf_op jit(solution)/shard_map/all_to_all | solution.py:102
  112.0 2.6 %copy-start = (bf16[2,8,25,512]{3,1,2,0:T(8,128)(2,1)S(1)}, bf16[2,8,25,512]{3,1,2,0:T(8,128)(2,1)}, u32[]{:S(2)}) copy-start(bf16[2,8,25,512]{3,1,2,0:T(8,128)(2,1)} %param.12) | copy-start | bytes 1228804
  112.0 2.6 %copy-start.5 = (f32[512]{0:T(512)S(1)}, f32[512]{0:T(512)}, u32[]{:S(2)}) copy-start(f32[512]{0:T(512)} %param.23) | copy-start | bytes 6148
Sparse Core Ops, SparseCore 0:
  9.5 84.9 all-gather.2

commit v17 on v12

--- a/solution.py
+++ b/solution.py
@@ -91,14 +91,14 @@
     left_mat = left_ops32[:levels] + left_g * left_ops32[levels:]
     right_mat = right_ops32[:levels] + right_g * right_ops32[levels:]
     cube = rows.reshape(levels, levels, -1)
+    right_mats = jnp.broadcast_to(right_mat, (levels,) + right_mat.shape)
     left_out = jnp.einsum(
         "xa,abn->xbn", left_mat, cube, precision=lax.Precision.HIGHEST
     ).reshape(rows.shape)
-    right_mats = jnp.broadcast_to(right_mat, (levels,) + right_mat.shape)
     right_out = jnp.einsum(
         "ayb,abn->ayn", right_mats, cube, precision=lax.Precision.HIGHEST
     ).reshape(rows.shape)
-    summed = (left_out + right_out).astype(jnp.bfloat16).reshape(rc_count, 2, -1)
+    summed = (right_out + left_out).astype(jnp.bfloat16).reshape(rc_count, 2, -1)
     returned = lax.all_to_all(summed, "rc", split_axis=0, concat_axis=0, tiled=True)
     returned = returned.reshape(state_count, col_groups, 2, pair_count, group_width)
     ladder_rows = jnp.transpose(returned[:, :, ::-1], (2, 0, 3, 1, 4)).reshape(density.shape)

time: 123 us -> 123 us (level)
    unnamed x27 -> x25, local copies, waits for them, and re-layouts: 1.9 us -> 2.64 us
where the time goes in v17:
time: 123 us; the launch traced here: 122 us
  waiting for transfers between devices  67.8 us (55%)
  starting transfers between devices  25 us (20%)
  between operations  13.7 us (11%)
  local copies, waits for them, and re-layouts  8.92 us (7%)
  matrix products  4.38 us (4%)
  other arithmetic  2.72 us (2%)
    all_to_all x1, waiting for transfers between devices, shards(): lax.all_to_all(summed, 'rc', split_axis=0, concat_axis=0, tiled=True)  34.3 us
    all_to_all x1, waiting for transfers between devices, shards(): lax.all_to_all(outgoing.reshape(rc_count, 2, -1), 'rc', split_axis=0, con...  32.8 us
    all_to_all x1, starting transfers between devices, shards(): lax.all_to_all(outgoing.reshape(rc_count, 2, -1), 'rc', split_axis=0, con...  20.3 us
    all_to_all x1, starting transfers between devices, shards(): lax.all_to_all(summed, 'rc', split_axis=0, concat_axis=0, tiled=True)  4.63 us
    unnamed x25, local copies, waits for them, and re-layouts  2.64 us
    dot_general x1, matrix products, shards(): jnp.einsum('ok,kjc->ojc', mixer, gathered.reshape(-1, pair_count, column_...  2.46 us
  transfers between devices with their start and end apart: 3, of which 2 were waited for; matrix products, arithmetic and copies ran while one was open for 10% of the time, Pallas kernels for 0%

profile of v17, /device:TPU:32, one launch (start us, length us, event | category | flops | bytes accessed | tf_op | source)
XLA Modules:
  0.0 122.5 jit_solution(16340950800756069422)
XLA Ops:
  6.6 0.7 all-gather.3.cloned.1.call-update
  7.3 1.2 copy.116
  8.5 1.1 reshape_reshape.3
  9.6 20.3 %all-to-all-start = ((bf16[64,2,1600]{2,1,0:T(2,128)(2,1)}), bf16[64,2,1600]{2,1,0:T(2,128)(2,1)S(1)}, u32[]{:S(2)}, u32[]{:S(2)}) async-start(bf16[64,2,1600]{2,1,0:T(2,128)(2,1)} %reshape_reshape.3), calls=%async_computation | async-start | bytes 851968 | tf_op jit(solution)/shard_map/all_to_all | solution.py:82
  29.9 0.9 copy.81
  30.8 0.8 copy.91
  31.7 0.8 copy.89
  32.8 0.6 dynamic_slice.15
  33.4 0.6 dynamic_slice.14
  34.1 0.6 fusion.27
  34.6 32.8 %all-to-all-done = bf16[64,2,1600]{2,1,0:T(2,128)(2,1)S(1)} async-done(((bf16[64,2,1600]{2,1,0:T(2,128)(2,1)}), bf16[64,2,1600]{2,1,0:T(2,128)(2,1)S(1)}, u32[]{:S(2)}, u32[]{:S(2)}) %all-to-all-start) | async-done | bytes 409632 | tf_op jit(solution)/shard_map/all_to_all | solution.py:82
  67.5 0.5 reshape.112
  68.0 1.1 fusion.20
  69.1 0.8 fusion.6
  69.9 1.1 convert_element_type.94
  71.0 4.6 %all-to-all-start.1 = ((bf16[64,2,1600]{2,1,0:T(2,128)(2,1)}), bf16[64,2,1600]{2,1,0:T(2,128)(2,1)S(1)}, u32[]{:S(2)}, u32[]{:S(2)}) async-start(bf16[64,2,1600]{2,1,0:T(2,128)(2,1)} %convert_element_type.94), calls=%async_computation.1 | async-start | bytes 851968 | tf_op jit(solution)/shard_map/all_to_all | solution.py:102
  76.4 0.1 reshape.118
  76.5 0.2 select_reduce_fusion.1
  76.7 0.2 select_reduce_fusion
  77.0 34.3 %all-to-all-done.1 = bf16[64,2,1600]{2,1,0:T(2,128)(2,1)S(1)} async-done(((bf16[64,2,1600]{2,1,0:T(2,128)(2,1)}), bf16[64,2,1600]{2,1,0:T(2,128)(2,1)S(1)}, u32[]{:S(2)}, u32[]{:S(2)}) %all-to-all-start.1) | async-done | bytes 409632 | tf_op jit(solution)/shard_map/all_to_all | solution.py:102
  111.3 0.3 reshape.113
  111.6 0.1 convert_bitcast_fusion
  111.8 2.5 %fusion.13 = f32[2,8,25,512]{3,1,0,2:T(8,128)S(1)} fusion(bf16[16,128,1]{1,0,2:T(8,128)(2,1)S(1)} %reshape.118, bf16[16,8,25,512]{3,1,2,0:T(8,128)(2,1)} %all-gather.3.cloned.1.call-done), kind=kOutput, calls=%fused_computation.8 | convolution fusion | flops 53043200 | bytes 4100096 | tf_op jit(solution)/shard_map/ok,kjc->ojc/dot_general | solution.py:67
  114.3 1.4 %fusion.19 = bf16[2,8,25,512]{3,1,2,0:T(8,128)(2,1)} fusion(f32[2,8,25,512]{3,1,0,2:T(8,128)S(1)} %fusion.13, f32[2,8,25,4,128]{4,2,0,3,1:T(8,128)S(1)} %convert_bitcast_fusion, f32[2,8,25,512]{3,1,2,0:T(8,128)S(1)} %convert_element_type.98, f32[25]{0:T(128)S(1)} %add_multiply_fusion, f32[2,512]{1,0:T(2,128)S(1)} %broadcast_multiply_fusion, f32[2]{0:T(128)S(1)} %copy-done.5), kind=kLoop, calls=%fused_computation.14 | loop fusion | flops 1433600 | bytes 2871404 | tf_op jit(solution)/shard_map/convert_element_type | solution.py:121
  (48 shorter events, 1.3 us)
Async XLA Ops:
  6.5 26.0 %copy-start.2 = (bf16[40,40]{1,0:T(8,128)(2,1)S(1)}, bf16[40,40]{1,0:T(8,128)(2,1)}, u32[]{:S(2)}) copy-start(bf16[40,40]{1,0:T(8,128)(2,1)} %param.19) | copy-start | bytes 9604
  6.5 26.1 %copy-start.3 = (bf16[40,40]{1,0:T(8,128)(2,1)S(1)}, bf16[40,40]{1,0:T(8,128)(2,1)}, u32[]{:S(2)}) copy-start(bf16[40,40]{1,0:T(8,128)(2,1)} %param.18) | copy-start | bytes 9604
  6.5 26.3 %copy-start.6 = (f32[64]{0:T(128)S(1)}, f32[64]{0:T(128)}, u32[]{:S(2)}) copy-start(f32[64]{0:T(128)} %param.20) | copy-start | bytes 772
  6.5 26.9 %copy-start.7 = (f32[64]{0:T(128)S(1)}, f32[64]{0:T(128)}, u32[]{:S(2)}) copy-start(f32[64]{0:T(128)} %param.21) | copy-start | bytes 772
  6.5 105.2 %all-gather.3.cloned.1.call-start = ((), (), s32[]{:S(2)}) async-start(), calls=%async_computation.2 | async-start | bytes 3686400 | tf_op jit(solution)/shard_map/all_gather | solution.py:58
  9.6 57.9 %all-to-all-start = ((bf16[64,2,1600]{2,1,0:T(2,128)(2,1)}), bf16[64,2,1600]{2,1,0:T(2,128)(2,1)S(1)}, u32[]{:S(2)}, u32[]{:S(2)}) async-start(bf16[64,2,1600]{2,1,0:T(2,128)(2,1)} %reshape_reshape.3), calls=%async_computation | async-start | bytes 851968 | tf_op jit(solution)/shard_map/all_to_all | solution.py:82
  29.9 45.8 %copy-start.1 = (bf16[64,64]{1,0:T(8,128)(2,1)S(1)}, bf16[64,64]{1,0:T(8,128)(2,1)}, u32[]{:S(2)}) copy-start(bf16[64,64]{1,0:T(8,128)(2,1)} %param.15) | copy-start | bytes 24580
  29.9 45.9 %copy-start = (bf16[2,8,25,512]{3,1,2,0:T(8,128)(2,1)S(1)}, bf16[2,8,25,512]{3,1,2,0:T(8,128)(2,1)}, u32[]{:S(2)}) copy-start(bf16[2,8,25,512]{3,1,2,0:T(8,128)(2,1)} %param.13) | copy-start | bytes 1228804
  68.0 8.6 %copy-start.8 = (f32[40]{0:T(128)S(1)}, f32[40]{0:T(128)}, u32[]{:S(2)}) copy-start(f32[40]{0:T(128)} %param.22) | copy-start | bytes 484
  68.0 8.7 %copy-start.9 = (f32[40]{0:T(128)S(1)}, f32[40]{0:T(128)}, u32[]{:S(2)}) copy-start(f32[40]{0:T(128)} %param.23) | copy-start | bytes 484
  68.0 8.9 %copy-start.4 = (f32[512]{0:T(512)S(1)}, f32[512]{0:T(512)}, u32[]{:S(2)}) copy-start(f32[512]{0:T(512)} %param.24) | copy-start | bytes 6148
  68.0 8.9 %copy-start.5 = (f32[2]{0:T(128)S(1)}, f32[2]{0:T(128)}, u32[]{:S(2)}) copy-start(f32[2]{0:T(128)} %constant.60.clone) | copy-start | bytes 28
  71.0 40.2 %all-to-all-start.1 = ((bf16[64,2,1600]{2,1,0:T(2,128)(2,1)}), bf16[64,2,1600]{2,1,0:T(2,128)(2,1)S(1)}, u32[]{:S(2)}, u32[]{:S(2)}) async-start(bf16[64,2,1600]{2,1,0:T(2,128)(2,1)} %convert_element_type.94), calls=%async_computation.1 | async-start | bytes 851968 | tf_op jit(solution)/shard_map/all_to_all | solution.py:102
Sparse Core Ops, SparseCore 0:
  9.5 84.5 all-gather.2
